TPU v7x, 32 devices: a whole 2x2x4 slice. The times are simulated.
32 devices in a mesh: seq: 8 (over z, x), ch: 4 (over y, core).
Axes of the slice: x: 2, y: 2, z: 4, core: 2. Of those that a mesh axis runs over, the one named last changes fastest.
Arguments:
- xin: bfloat16 [8192, 16384], P('seq', 'ch'), may hold values from -6 to 6
- gate_in: bfloat16 [8192, 16384], P('seq', 'ch'), may hold values from -6 to 6
- bc_proj: bfloat16 [8192, 256], P('seq', 'ch'), may hold values from -6 to 6
- dt_raw: float32 [8192, 128], P('seq', 'ch'), may hold values from -6 to 6
- dt_bias: float32 [128], P('ch'), may hold values from -1 to 1
- rate: float32 [128], P('ch'), may hold values from 6.1035156e-05 to 0.1
- skip_gain: float32 [128], P('ch'), may hold values from 0.5 to 2
- conv_x: bfloat16 [4, 16384], P(None, 'ch'), may hold values from -3 to 3
- conv_bc: bfloat16 [4, 256], P(None, 'ch'), may hold values from -3 to 3
- norm_gain: float32 [16384], P('ch'), may hold values from 0.5 to 1.5
- valid_blocks: int32 [8], P('seq'), may hold values from 1 to 8, 48 in all
Outputs:
- mixed: bfloat16 [8192, 16384], P('seq', 'ch')
Inputs may be any that keep to these rules, and one draw needn't show every extreme that they name: valid_blocks sums to 48; some entry equals 8.
All inputs are finite; a program needn't handle non-finite values.
Results may differ from a plain program's by a relative error of at most 0.0034.
Values may be sent and summed in bfloat16 or wider, within the bound.
No kernel may reach another device: no remote copies, remote signals or barrier semaphores. Data moves between devices by JAX's collectives and lax.ppermute only.
A program may use at most 256 MiB of HBM per device.

v0:
```python
import jax
import jax.numpy as jnp
from jax import lax
from jax.sharding import PartitionSpec as P

SEGMENT_LENGTH = 256
BLOCK = 128
INNER = 16384


def passed_along(block, axis, distance):
    devices = range(lax.axis_size(axis))
    route = [(i - distance, i) for i in devices if i - distance in devices]
    return lax.ppermute(block, axis, route)


def prefix(part, axis, combine, identity):
    place = lax.axis_index(axis)
    gathered = jax.tree.map(lambda a: lax.all_gather(a, axis), part)
    state = jax.tree.map(lambda a, e: jnp.zeros_like(a) + jnp.asarray(e, a.dtype), part, identity)

    def one(turn, state):
        return combine(
            state, jax.tree.map(lambda a: lax.dynamic_index_in_dim(a, turn, 0, False), gathered)
        )

    return lax.fori_loop(0, place, one, state)


def conv_silu(signal, tail_rows, weights):
    stacked = jnp.concatenate([tail_rows, signal], axis=0)
    kernel_taps = weights.shape[0]
    length = signal.shape[0]
    accum = jnp.zeros(signal.shape, jnp.float32)
    for offset in range(kernel_taps):
        accum = accum + weights[offset].astype(jnp.float32) * stacked[
            offset : offset + length
        ].astype(jnp.float32)
    return jax.nn.silu(accum).astype(jnp.bfloat16)


def combine_states(earlier, latter):
    return (earlier[0] * latter[0], latter[0][:, None, None] * earlier[1] + latter[1])


def local(
    xin,
    gate_in,
    bc_proj,
    dt_raw,
    dt_bias,
    rate,
    skip_gain,
    conv_x,
    conv_bc,
    norm_gain,
    valid_blocks,
):
    row_count, channels = xin.shape
    head_count = dt_raw.shape[1]
    head_size = channels // head_count
    span_count = row_count // SEGMENT_LENGTH
    kernel_taps = conv_x.shape[0]
    live_rows = valid_blocks[0] * BLOCK
    tail_x = lax.dynamic_slice_in_dim(xin, live_rows - (kernel_taps - 1), kernel_taps - 1, 0)
    tail_bc = lax.dynamic_slice_in_dim(bc_proj, live_rows - (kernel_taps - 1), kernel_taps - 1, 0)
    prev_x, prev_bc = passed_along((tail_x, tail_bc), "seq", 1)
    xconv = conv_silu(xin, prev_x, conv_x)
    bc_local = conv_silu(bc_proj, prev_bc, conv_bc)
    bc_full = lax.all_gather(bc_local, "ch", axis=1, tiled=True)
    state_size = bc_full.shape[1] // 2
    row_valid = (jnp.arange(row_count) < live_rows).astype(jnp.float32)
    step_size = jax.nn.softplus(dt_raw + dt_bias[None, :]) * row_valid[:, None]
    xfour = xconv.reshape(span_count, SEGMENT_LENGTH, head_count, head_size)
    b_three = bc_full[:, :state_size].reshape(span_count, SEGMENT_LENGTH, state_size)
    c_three = bc_full[:, state_size:].reshape(span_count, SEGMENT_LENGTH, state_size)
    step_three = step_size.reshape(span_count, SEGMENT_LENGTH, head_count)
    cumul = jnp.cumsum(-rate[None, None, :] * step_three, axis=1)
    scores = jnp.einsum("cqn,csn->cqs", c_three, b_three, preferred_element_type=jnp.float32)
    cum_heads = jnp.transpose(cumul, (0, 2, 1))
    diff = cum_heads[:, :, :, None] - cum_heads[:, :, None, :]
    causal = jnp.arange(SEGMENT_LENGTH)[:, None] >= jnp.arange(SEGMENT_LENGTH)[None, :]
    decay = jnp.where(causal, jnp.exp(jnp.where(causal, diff, 0.0)), 0.0)
    weights = (
        scores[:, None] * decay * jnp.transpose(step_three, (0, 2, 1))[:, :, None, :]
    ).astype(jnp.bfloat16)
    intra = jnp.einsum("chqs,cshp->cqhp", weights, xfour, preferred_element_type=jnp.float32)
    last_cum = cum_heads[:, :, -1]
    to_end = jnp.exp(last_cum[:, None, :] - cumul) * step_three
    x_weighted = (xfour.astype(jnp.float32) * to_end[..., None]).astype(jnp.bfloat16)
    block_state = jnp.einsum(
        "csn,cshp->chnp", b_three, x_weighted, preferred_element_type=jnp.float32
    )
    block_decay = jnp.exp(last_cum)
    current = jnp.zeros((head_count, state_size, head_size), jnp.float32)
    factor = jnp.ones((head_count,), jnp.float32)
    local_enter = []
    factor_list = []
    for index in range(span_count):
        local_enter.append(current)
        factor_list.append(factor)
        current = block_decay[index][:, None, None] * current + block_state[index]
        factor = factor * block_decay[index]
    own_pair = (factor, current)
    identity = (
        jnp.ones((head_count,), jnp.float32),
        jnp.zeros((head_count, state_size, head_size), jnp.float32),
    )
    incoming = prefix(own_pair, "seq", combine_states, identity)
    group_state = incoming[1]
    state_enter = jnp.stack(
        [
            local_enter[index] + factor_list[index][:, None, None] * group_state
            for index in range(span_count)
        ],
        axis=0,
    )
    inter = jnp.einsum(
        "cqn,chnp->cqhp", c_three.astype(jnp.float32), state_enter, precision=lax.Precision.HIGHEST
    )
    inter = inter * jnp.exp(cumul)[..., None]
    y_full = intra + inter + skip_gain[None, None, :, None] * xfour.astype(jnp.float32)
    y_full = y_full.reshape(row_count, channels)
    gated = y_full * jax.nn.silu(gate_in.astype(jnp.float32))
    square_sum = lax.psum(jnp.sum(gated * gated, axis=1), "ch")
    mean_sq = square_sum / INNER
    normed = gated * lax.rsqrt(mean_sq + 1e-05)[:, None] * norm_gain[None, :] * row_valid[:, None]
    return normed.astype(jnp.bfloat16)


def solution(mesh):
    placed = (
        P("seq", "ch"),
        P("seq", "ch"),
        P("seq", "ch"),
        P("seq", "ch"),
        P("ch"),
        P("ch"),
        P("ch"),
        P(None, "ch"),
        P(None, "ch"),
        P("ch"),
        P("seq"),
    )
    return jax.shard_map(
        local, mesh=mesh, in_specs=placed, out_specs=P("seq", "ch"), check_vma=False
    )
```

profile of v0, /device:TPU:26, one launch (start us, length us, event | category | flops | bytes accessed | tf_op | source)
XLA Modules:
  0.0 431.1 jit_solution(12432923098309442453)
XLA Ops:
  13.5 2.3 reduce-window.6
  20.0 7.2 %all_gather.11 = bf16[1024,256]{0,1:T(8,128)(2,1)S(1)} all-gather(bf16[1024,64]{0,1:T(8,128)(2,1)S(1)} %multiply_convert_fusion.6), channel_id=1, replica_groups=mesh['seq'=8,'ch'=4] {'ch'}, dimensions={1}, use_global_device_ids=true | all-gather | bytes 655360 | tf_op jit(solution)/shard_map/all_gather | solution.py:70
  27.4 18.8 %fusion.26 = bf16[128,8,32,128]{3,1,2,0:T(8,128)(2,1)} fusion(bf16[1024,4096]{1,0:T(8,128)(2,1)} %param.13, f32[4096]{0:T(1024)S(1)} %bitcast.143, bf16[3,4096]{1,0:T(4,128)(2,1)S(1)} %collective-permute-done, f32[4096]{0:T(1024)S(1)} %bitcast.144, f32[4096]{0:T(1024)S(1)} %bitcast.142, f32[4096]{0:T(1024)S(1)} %bitcast.141), kind=kLoop, calls=%fused_computation.39 | loop fusion | flops 104857600 | bytes 16867328
  46.3 9.4 %copy.92 = bf16[128,8,32,128]{3,2,1,0:T(8,128)(2,1)} copy(bf16[128,8,32,128]{3,1,2,0:T(8,128)(2,1)} %fusion.26) | data formatting | bytes 16777216
  55.7 13.7 %copy.72 = bf16[4,256,32,128]{1,3,2,0:T(8,128)(2,1)} copy(bf16[4,256,32,128]{3,2,1,0:T(8,128)(2,1)} %bitcast.134) | data formatting | bytes 16777216 | tf_op jit(solution)/shard_map/reshape | solution.py:74
  69.4 5.7 %fusion.27 = f32[4,32,128,128]{2,3,1,0:T(8,128)S(1)} fusion(bf16[4,256,128,1]{2,1,3,0:T(8,128)(2,1)S(1)} %bitcast.138, bf16[4,256,32,128]{1,3,2,0:T(8,128)(2,1)} %copy.72, f32[4,256,32]{1,2,0:T(8,128)S(1)} %copy.76), kind=kOutput, calls=%fused_computation.40 | convolution fusion | flops 1086324736 | bytes 17170432 | tf_op jit(solution)/shard_map/csn,cshp->chnp/dot_general | solution.py:91
  75.1 3.2 copy-done
  81.0 18.2 %all-gather = f32[8,1,32]{2,1,0:T(1,128)S(1)} all-gather(f32[1,1,32]{2,1,0:T(1,128)S(1)} %get-tuple-element.88), channel_id=1, replica_groups=mesh['seq'=8,'ch'=4] {'seq'}, dimensions={0}, use_global_device_ids=true | all-gather | bytes 1152 | tf_op jit(solution)/shard_map/all_gather | solution.py:19
  100.8 208.3 %all-gather.3.cloned.1.call-done = f32[8,32,128,128]{3,2,1,0:T(8,128)} async-done(((f32[1,32,128,128]{3,2,1,0:T(8,128)}), f32[8,32,128,128]{3,2,1,0:T(8,128)}) %all-gather.3.cloned.1.call-update) | async-done | bytes 16777232 | tf_op jit(solution)/shard_map/all_gather | solution.py:19
  309.3 14.3 %while.12 = (s32[]{:T(128)}, f32[32,128,128]{2,1,0:T(8,128)S(1)}, s32[]{:T(128)}, f32[8,32]{1,0:T(8,128)S(1)}, f32[8,32,128,128]{3,2,1,0:T(8,128)}, /*index=5*/s32[]{:T(128)}, s32[]{:T(128)}, s32[]{:T(128)}) while((s32[]{:T(128)}, f32[32,128,128]{2,1,0:T(8,128)S(1)}, s32[]{:T(128)}, f32[8,32]{1,0:T(8,128)S(1)}, f32[8,32,128,128]{3,2,1,0:T(8,128)}, ...), condition=%wide.region_3.4_spmd, body=%wide.region_2.3_spmd.sunk | while | flops 1048581 | bytes 6291975 | solution.py:27
  309.4 2.0 bitcast_add_fusion.6
  311.4 2.0 bitcast_add_fusion.6
  313.4 2.0 bitcast_add_fusion.6
  315.4 2.0 bitcast_add_fusion.6
  317.4 2.0 bitcast_add_fusion.6
  319.4 2.0 bitcast_add_fusion.6
  321.5 2.0 bitcast_add_fusion.6
  325.5 4.1 add_bitcast_fusion
  329.7 10.9 %fusion.17 = f32[4,256,32,128]{1,3,2,0:T(8,128)} fusion(bf16[4,256,128,1]{2,1,3,0:T(8,128)(2,1)S(1)} %bitcast.137, f32[1,32,128,128]{2,3,1,0:T(8,128)S(1)} %get-tuple-element.78, f32[1,32,128,128]{2,3,1,0:T(8,128)S(1)} %get-tuple-element.77, f32[1,32,128,128]{2,3,1,0:T(8,128)S(1)} %get-tuple-element.79, f32[1,32,128,128]{2,3,1,0:T(8,128)S(1)} %bitcast.135), kind=kOutput, calls=%fused_computation.30 | convolution fusion | flops 6448742400 | bytes 25427968 | tf_op jit(solution)/shard_map/cqn,chnp->cqhp/dot_general | solution.py:118
  340.6 17.0 %fusion.2 = f32[4,256,32,128]{1,3,2,0:T(8,128)} fusion(bf16[4,256,32,128]{1,3,2,0:T(8,128)(2,1)S(1)} %bitcast.133, f32[4,256,32,128]{1,3,2,0:T(8,128)} %fusion.17, f32[4,32,256]{2,1,0:T(8,128)S(1)} %copy.71, f32[4,32,256]{2,1,0:T(8,128)S(1)} %copy_bitcast_fusion, f32[4,256,256]{2,1,0:T(8,128)S(1)} %copy-done.2, pred[256,256]{1,0:T(8,128)(4,1)S(1)} %iota_compare_fusion, ...), kind=kOutput, calls=%fused_computation.9 | convolution fusion | flops 2218786816 | bytes 43450496 | tf_op jit(solution)/shard_map/chqs,cshp->cqhp/dot_general | solution.py:87
  357.6 19.8 %copy.84 = f32[4,256,32,128]{3,2,1,0:T(8,128)} copy(f32[4,256,32,128]{1,3,2,0:T(8,128)} %fusion.2) | data formatting | bytes 33554432 | tf_op jit(solution)/shard_map/add | solution.py:122
  377.4 16.2 %multiply_reduce_fusion = f32[1024]{0:T(1024)S(1)} fusion(bf16[1024,4096]{1,0:T(8,128)(2,1)} %param.14, f32[128,8,32,128]{3,2,1,0:T(8,128)} %bitcast.130), kind=kLoop, calls=%fused_computation.16 | loop fusion | flops 33553408 | bytes 25169920 | tf_op jit(solution)/shard_map/reduce_sum | solution.py:125
  393.6 6.9 %psum.7 = f32[1024]{0:T(1024)S(1)} all-reduce(f32[1024]{0:T(1024)S(1)} %multiply_reduce_fusion), channel_id=1, replica_groups=mesh['seq'=8,'ch'=4] {'ch'}, use_global_device_ids=true, to_apply=%region_5.6 | all-reduce | flops 1024 | bytes 8192 | tf_op jit(solution)/shard_map/psum | solution.py:125
  400.5 23.8 %multiply_convert_fusion.2 = bf16[1024,4096]{1,0:T(8,128)(2,1)} fusion(f32[1024]{0:T(1024)S(1)} %fusion.38, f32[4096]{0:T(1024)S(1)} %copy-done.3, f32[1024]{0:T(1024)S(1)} %add_rsqrt_fusion, bf16[1024,4096]{1,0:T(8,128)(2,1)} %param.14, f32[128,8,32,128]{3,2,1,0:T(8,128)} %bitcast.131), kind=kLoop, calls=%fused_computation.15 | loop fusion | flops 41943040 | bytes 33579008 | tf_op jit(solution)/shard_map/convert_element_type | solution.py:128
  (64 shorter events, 17.0 us)
Async XLA Ops:
  6.5 302.5 %all-gather.3.cloned.1.call-start = ((), (), s32[]{:S(2)}) async-start(), calls=%async_computation | async-start | bytes 18874368 | tf_op jit(solution)/shard_map/all_gather | solution.py:19
  8.1 19.4 %collective-permute-start = (bf16[3,4096]{1,0:T(4,128)(2,1)S(1)}, bf16[3,4096]{1,0:T(4,128)(2,1)S(1)}, u32[]{:S(2)}, u32[]{:S(2)}) collective-permute-start(bf16[3,4096]{1,0:T(4,128)(2,1)S(1)} %constant_dynamic-slice_fusion.1), channel_id=1, source_target_pairs={{0,4},{4,8},{8,12},{12,16},{16,20},{20,24},{24,28},{1,5},{5,9},{9,... | collective-permute-start | bytes 73736 | tf_op jit(solution)/shard_map/ppermute | solution.py:14
  10.2 8.3 %collective-permute-start.1 = (bf16[3,64]{0,1:T(8,128)(2,1)S(1)}, bf16[3,64]{0,1:T(8,128)(2,1)S(1)}, u32[]{:S(2)}, u32[]{:S(2)}) collective-permute-start(bf16[3,64]{0,1:T(8,128)(2,1)S(1)} %constant_dynamic-slice_fusion), channel_id=1, source_target_pairs={{0,4},{4,8},{8,12},{12,16},{16,20},{20,24},{24,28},{1,5},{5,9},{9,... | collective-permute-start | bytes 1160 | tf_op jit(solution)/shard_map/ppermute | solution.py:14
  75.1 3.2 copy-start
  325.5 4.1 copy-start.1
  325.5 15.1 %slice-start = ((s8[8388608]{0:T(1024)(128)(4,1)}), s8[4194304]{0:T(1024)(128)(4,1)S(1)}, s32[]{:S(2)}) async-start(s8[8388608]{0:T(1024)(128)(4,1)} %bitcast.132), calls=%async_computation.1 | async-start | bytes 8388608
  329.7 10.9 %slice-start.1 = ((s8[8388608]{0:T(1024)(128)(4,1)}), s8[4194304]{0:T(1024)(128)(4,1)S(1)}, s32[]{:S(2)}) async-start(s8[8388608]{0:T(1024)(128)(4,1)} %bitcast.132), calls=%async_computation.2 | async-start | bytes 8388608
  329.7 10.9 %copy-start.2 = (f32[4,256,256]{2,1,0:T(8,128)S(1)}, f32[4,256,256]{2,1,0:T(8,128)}, u32[]{:S(2)}) copy-start(f32[4,256,256]{2,1,0:T(8,128)} %fusion.45) | copy-start | bytes 3145732
  329.7 10.9 %copy-start.4 = (f32[32]{0:T(128)S(1)}, f32[32]{0:T(128)}, u32[]{:S(2)}) copy-start(f32[32]{0:T(128)} %param.19) | copy-start | bytes 388
  377.4 23.1 %copy-start.3 = (f32[4096]{0:T(1024)S(1)}, f32[4096]{0:T(1024)}, u32[]{:S(2)}) copy-start(f32[4096]{0:T(1024)} %param.22) | copy-start | bytes 49156
Sparse Core Ops, SparseCore 0:
  81.1 227.9 all-gather.2
where the time goes:
time: 433 us; the launch traced here: 431 us
  waiting for transfers between devices  208 us (48%)
  other arithmetic  85.4 us (20%)
  local copies, waits for them, and re-layouts  53 us (12%)
  matrix products  34.8 us (8%)
  blocking collectives  32.2 us (7%)
  between operations  14.3 us (3%)
    all_gather x1, waiting for transfers between devices, prefix(): gathered = jax.tree.map(lambda a: lax.all_gather(a, axis), part)  208 us
    convert_element_type x1, other arithmetic, local(): return normed.astype(jnp.bfloat16)  23.8 us
    add x1, local copies, waits for them, and re-layouts, local(): intra + inter + skip_gain[None, None, :, None] * xfour.astype(jnp.float32)  19.8 us
    unnamed x2, other arithmetic  18.8 us
    all_gather x1, blocking collectives, prefix(): gathered = jax.tree.map(lambda a: lax.all_gather(a, axis), part)  18.2 us
    dot_general x1, matrix products, local(): jnp.einsum('chqs,cshp->cqhp', weights, xfour, preferred_element_type=jnp....  17 us
    reduce_sum x1, other arithmetic, local(): square_sum = lax.psum(jnp.sum(gated * gated, axis=1), 'ch')  16.2 us
    add x7, other arithmetic, combine_states(): latter[0][:, None, None] * earlier[1] + latter[1]  13.8 us
  transfers between devices with their start and end apart: 3, of which 1 were waited for; matrix products, arithmetic and copies ran while one was open for 3% of the time, Pallas kernels for 0%

commit v1 on v0

--- a/solution.py
+++ b/solution.py
@@ -25,6 +25,22 @@
         )
 
     return lax.fori_loop(0, place, one, state)
+
+
+def scan_states(factor, state, axis):
+    count = lax.axis_size(axis)
+    heads, size, width = state.shape
+    piece = size // count
+    parts = state.reshape(heads, count, piece, width).transpose(1, 0, 2, 3)
+    got = lax.all_to_all(parts, axis, 0, 0, tiled=True)
+    decays = lax.all_gather(factor, axis)
+    running = jnp.zeros((heads, piece, width), jnp.float32)
+    entries = []
+    for index in range(count):
+        entries.append(running)
+        running = decays[index][:, None, None] * running + got[index]
+    back = lax.all_to_all(jnp.stack(entries, axis=0), axis, 0, 0, tiled=True)
+    return back.transpose(1, 0, 2, 3).reshape(heads, size, width)
 
 
 def conv_silu(signal, tail_rows, weights):
@@ -101,13 +117,7 @@
         factor_list.append(factor)
         current = block_decay[index][:, None, None] * current + block_state[index]
         factor = factor * block_decay[index]
-    own_pair = (factor, current)
-    identity = (
-        jnp.ones((head_count,), jnp.float32),
-        jnp.zeros((head_count, state_size, head_size), jnp.float32),
-    )
-    incoming = prefix(own_pair, "seq", combine_states, identity)
-    group_state = incoming[1]
+    group_state = scan_states(factor, current, "seq")
     state_enter = jnp.stack(
         [
             local_enter[index] + factor_list[index][:, None, None] * group_state

time: 433 us -> 296 us (0.68)
  the two profiles are of different devices: /device:TPU:26 before, /device:TPU:0 now
where the time goes in v1:
time: 296 us; the launch traced here: 295 us
  other arithmetic  78.1 us (26%)
  blocking collectives  63.2 us (21%)
  local copies, waits for them, and re-layouts  50 us (17%)
  waiting for transfers between devices  44.1 us (15%)
  matrix products  35.5 us (12%)
  starting transfers between devices  23.3 us (8%)
    all_gather x1, blocking collectives, scan_states(): decays = lax.all_gather(factor, axis)  50.3 us
    all_to_all x1, waiting for transfers between devices, scan_states(): back = lax.all_to_all(jnp.stack(entries, axis=0), axis, 0, 0, tiled=True)  44.1 us
    unnamed x8, other arithmetic  23.8 us
    convert_element_type x1, other arithmetic, local(): return normed.astype(jnp.bfloat16)  23.8 us
    add x1, local copies, waits for them, and re-layouts, local(): intra + inter + skip_gain[None, None, :, None] * xfour.astype(jnp.float32)  19.9 us
    dot_general x1, matrix products, local(): jnp.einsum('chqs,cshp->cqhp', weights, xfour, preferred_element_type=jnp....  16.9 us
    reduce_sum x1, other arithmetic, local(): square_sum = lax.psum(jnp.sum(gated * gated, axis=1), 'ch')  16.2 us
    reshape x1, local copies, waits for them, and re-layouts, local(): xfour = xconv.reshape(span_count, SEGMENT_LENGTH, head_count, head_size)  13.7 us
  transfers between devices with their start and end apart: 4, of which 1 were waited for; matrix products, arithmetic and copies ran while one was open for 4% of the time, Pallas kernels for 0%

profile of v1, /device:TPU:0, one launch (start us, length us, event | category | flops | bytes accessed | tf_op | source)
XLA Modules:
  0.0 295.1 jit_solution(8217255166965492911)
XLA Ops:
  1.5 4.9 %collective-permute-start.1 = (bf16[3,64]{0,1:T(8,128)(2,1)S(1)}, bf16[3,64]{0,1:T(8,128)(2,1)S(1)}, u32[]{:S(2)}, u32[]{:S(2)}) collective-permute-start(bf16[3,64]{0,1:T(8,128)(2,1)S(1)} %constant_dynamic-slice_fusion), channel_id=1, source_target_pairs={{0,4},{4,8},{8,12},{12,16},{16,20},{20,24},{24,28},{1,5},{5,9},{9,... | collective-permute-start | bytes 1160 | tf_op jit(solution)/shard_map/ppermute | solution.py:14
  7.2 3.5 %collective-permute-start = (bf16[3,4096]{1,0:T(4,128)(2,1)S(1)}, bf16[3,4096]{1,0:T(4,128)(2,1)S(1)}, u32[]{:S(2)}, u32[]{:S(2)}) collective-permute-start(bf16[3,4096]{1,0:T(4,128)(2,1)S(1)} %constant_dynamic-slice_fusion.1), channel_id=1, source_target_pairs={{0,4},{4,8},{8,12},{12,16},{16,20},{20,24},{24,28},{1,5},{5,9},{9,... | collective-permute-start | bytes 73736 | tf_op jit(solution)/shard_map/ppermute | solution.py:14
  10.7 1.1 fusion.38
  12.7 2.3 reduce-window.6
  17.7 1.5 multiply_convert_fusion.6
  19.2 7.2 %all_gather.7 = bf16[1024,256]{0,1:T(8,128)(2,1)S(1)} all-gather(bf16[1024,64]{0,1:T(8,128)(2,1)S(1)} %multiply_convert_fusion.6), channel_id=1, replica_groups=mesh['seq'=8,'ch'=4] {'ch'}, dimensions={1}, use_global_device_ids=true | all-gather | bytes 655360 | tf_op jit(solution)/shard_map/all_gather | solution.py:86
  26.6 18.8 %fusion.26 = bf16[128,8,32,128]{3,1,2,0:T(8,128)(2,1)} fusion(bf16[1024,4096]{1,0:T(8,128)(2,1)} %param.11, f32[4096]{0:T(1024)S(1)} %bitcast.133, bf16[3,4096]{1,0:T(4,128)(2,1)S(1)} %collective-permute-done, f32[4096]{0:T(1024)S(1)} %bitcast.134, f32[4096]{0:T(1024)S(1)} %bitcast.132, f32[4096]{0:T(1024)S(1)} %bitcast.131), kind=kLoop, calls=%fused_computation.37 | loop fusion | flops 104857600 | bytes 16867328
  45.5 9.4 %copy.84 = bf16[128,8,32,128]{3,2,1,0:T(8,128)(2,1)} copy(bf16[128,8,32,128]{3,1,2,0:T(8,128)(2,1)} %fusion.26) | data formatting | bytes 16777216
  54.9 13.7 %copy.60 = bf16[4,256,32,128]{1,3,2,0:T(8,128)(2,1)} copy(bf16[4,256,32,128]{3,2,1,0:T(8,128)(2,1)} %bitcast.118) | data formatting | bytes 16777216 | tf_op jit(solution)/shard_map/reshape | solution.py:90
  68.6 6.3 %fusion.27 = f32[4,32,128,128]{3,2,1,0:T(8,128)S(1)} fusion(bf16[4,256,128,1]{2,1,3,0:T(8,128)(2,1)S(1)} %bitcast.126, bf16[4,256,32,128]{1,3,2,0:T(8,128)(2,1)} %copy.60, f32[4,256,32]{1,2,0:T(8,128)S(1)} %copy.64), kind=kOutput, calls=%fused_computation.38 | convolution fusion | flops 1086324736 | bytes 17170432 | tf_op jit(solution)/shard_map/csn,cshp->chnp/dot_general | solution.py:107
  75.5 2.6 copy-done
  78.1 2.0 fusion.30
  80.2 4.8 %all-to-all-start = ((f32[8,32,16,128]{3,2,1,0:T(8,128)}), f32[8,32,16,128]{3,2,1,0:T(8,128)S(1)}, u32[]{:S(2)}, u32[]{:S(2)}) async-start(f32[8,32,16,128]{3,2,1,0:T(8,128)} %fusion.30), calls=%async_computation | async-start | bytes 4194304 | tf_op jit(solution)/shard_map/all_to_all | solution.py:35
  85.0 50.3 %all-gather = f32[8,1,32]{2,1,0:T(1,128)S(1)} all-gather(f32[1,1,32]{2,1,0:T(1,128)S(1)} %get-tuple-element.35), channel_id=1, replica_groups=mesh['seq'=8,'ch'=4] {'seq'}, dimensions={0}, use_global_device_ids=true | all-gather | bytes 1152 | tf_op jit(solution)/shard_map/all_gather | solution.py:36
  141.8 10.2 %all-to-all-start.1 = ((f32[8,32,16,128]{3,2,1,0:T(8,128)}), f32[8,32,16,128]{3,2,1,0:T(8,128)S(1)}, u32[]{:S(2)}, u32[]{:S(2)}) async-start(f32[8,32,16,128]{3,2,1,0:T(8,128)} %fusion.34), calls=%async_computation.1 | async-start | bytes 4194304 | tf_op jit(solution)/shard_map/all_to_all | solution.py:42
  152.4 1.3 fusion.53
  153.7 44.1 %all-to-all-done.1 = f32[8,32,16,128]{3,2,1,0:T(8,128)S(1)} async-done(((f32[8,32,16,128]{3,2,1,0:T(8,128)}), f32[8,32,16,128]{3,2,1,0:T(8,128)S(1)}, u32[]{:S(2)}, u32[]{:S(2)}) %all-to-all-start.1) | async-done | bytes 2097184 | tf_op jit(solution)/shard_map/all_to_all | solution.py:42
  198.1 3.5 %multiply_add_fusion.1 = (f32[1,32,128,128]{3,2,1,0:T(8,128)S(1)}, f32[1,32,128,128]{3,2,1,0:T(8,128)S(1)}, f32[1,32,128,128]{3,2,1,0:T(8,128)S(1)}) fusion(f32[1,32,128,128]{3,2,1,0:T(8,128)S(1)} %bitcast.119, f32[32]{0:T(128)S(1)} %get-tuple-element.6, f32[4,32,128,128]{3,2,1,0:T(8,128)} %copy-done, f32[32]{0:T(128)S(1)} %get-tuple-element.38, ...), kind=kLoop, calls=%fused_computation.48 | loop fusion | flops 5767168 | bytes 14680832 | tf_op jit(solution)/shard_map/add | solution.py:123
  201.7 10.9 %fusion.17 = f32[4,256,32,128]{1,3,2,0:T(8,128)} fusion(bf16[4,256,128,1]{2,1,3,0:T(8,128)(2,1)S(1)} %bitcast.129, f32[1,32,128,128]{3,2,1,0:T(8,128)S(1)} %get-tuple-element.14, f32[1,32,128,128]{3,2,1,0:T(8,128)S(1)} %get-tuple-element.13, f32[1,32,128,128]{3,2,1,0:T(8,128)S(1)} %get-tuple-element.15, f32[1,32,128,128]{3,2,1,0:T(8,128)S(1)} %bitcast.120), kind=kOutput, calls=%fused_computation.28 | convolution fusion | flops 6448742400 | bytes 25427968 | tf_op jit(solution)/shard_map/cqn,chnp->cqhp/dot_general | solution.py:128
  212.6 16.9 %fusion.2 = f32[4,256,32,128]{1,3,2,0:T(8,128)} fusion(bf16[4,256,32,128]{1,3,2,0:T(8,128)(2,1)S(1)} %bitcast.117, f32[4,256,32,128]{1,3,2,0:T(8,128)} %fusion.17, f32[4,32,256]{2,1,0:T(8,128)S(1)} %copy.59, f32[4,32,256]{2,1,0:T(8,128)S(1)} %copy_bitcast_fusion, f32[4,256,256]{2,1,0:T(8,128)S(1)} %copy-done.1, pred[256,256]{1,0:T(8,128)(4,1)S(1)} %iota_compare_fusion, ...), kind=kOutput, calls=%fused_computation.7 | convolution fusion | flops 2218786816 | bytes 43450496 | tf_op jit(solution)/shard_map/chqs,cshp->cqhp/dot_general | solution.py:103
  229.6 19.9 %copy.73 = f32[4,256,32,128]{3,2,1,0:T(8,128)} copy(f32[4,256,32,128]{1,3,2,0:T(8,128)} %fusion.2) | data formatting | bytes 33554432 | tf_op jit(solution)/shard_map/add | solution.py:132
  249.4 16.2 %multiply_reduce_fusion = f32[1024]{0:T(1024)S(1)} fusion(bf16[1024,4096]{1,0:T(8,128)(2,1)} %param.12, f32[128,8,32,128]{3,2,1,0:T(8,128)} %bitcast.114), kind=kLoop, calls=%fused_computation.14 | loop fusion | flops 33553408 | bytes 25169920 | tf_op jit(solution)/shard_map/reduce_sum | solution.py:135
  265.6 5.7 %psum.7 = f32[1024]{0:T(1024)S(1)} all-reduce(f32[1024]{0:T(1024)S(1)} %multiply_reduce_fusion), channel_id=1, replica_groups=mesh['seq'=8,'ch'=4] {'ch'}, use_global_device_ids=true, to_apply=%region_3.4 | all-reduce | flops 1024 | bytes 8192 | tf_op jit(solution)/shard_map/psum | solution.py:135
  271.3 23.8 %multiply_convert_fusion.2 = bf16[1024,4096]{1,0:T(8,128)(2,1)} fusion(f32[1024]{0:T(1024)S(1)} %fusion.44, f32[4096]{0:T(1024)S(1)} %copy-done.2, f32[1024]{0:T(1024)S(1)} %add_rsqrt_fusion, bf16[1024,4096]{1,0:T(8,128)(2,1)} %param.12, f32[128,8,32,128]{3,2,1,0:T(8,128)} %bitcast.115), kind=kLoop, calls=%fused_computation.13 | loop fusion | flops 41943040 | bytes 33579008 | tf_op jit(solution)/shard_map/convert_element_type | solution.py:138
  (56 shorter events, 13.2 us)
Async XLA Ops:
  1.5 16.2 %collective-permute-start.1 = (bf16[3,64]{0,1:T(8,128)(2,1)S(1)}, bf16[3,64]{0,1:T(8,128)(2,1)S(1)}, u32[]{:S(2)}, u32[]{:S(2)}) collective-permute-start(bf16[3,64]{0,1:T(8,128)(2,1)S(1)} %constant_dynamic-slice_fusion), channel_id=1, source_target_pairs={{0,4},{4,8},{8,12},{12,16},{16,20},{20,24},{24,28},{1,5},{5,9},{9,... | collective-permute-start | bytes 1160 | tf_op jit(solution)/shard_map/ppermute | solution.py:14
  7.2 19.4 %collective-permute-start = (bf16[3,4096]{1,0:T(4,128)(2,1)S(1)}, bf16[3,4096]{1,0:T(4,128)(2,1)S(1)}, u32[]{:S(2)}, u32[]{:S(2)}) collective-permute-start(bf16[3,4096]{1,0:T(4,128)(2,1)S(1)} %constant_dynamic-slice_fusion.1), channel_id=1, source_target_pairs={{0,4},{4,8},{8,12},{12,16},{16,20},{20,24},{24,28},{1,5},{5,9},{9,... | collective-permute-start | bytes 73736 | tf_op jit(solution)/shard_map/ppermute | solution.py:14
  74.9 3.2 %copy-start = (f32[4,32,128,128]{3,2,1,0:T(8,128)}, f32[4,32,128,128]{3,2,1,0:T(8,128)S(1)}, u32[]{:S(2)}) copy-start(f32[4,32,128,128]{3,2,1,0:T(8,128)S(1)} %fusion.27) | copy-start | bytes 25165828
  80.2 55.9 %all-to-all-start = ((f32[8,32,16,128]{3,2,1,0:T(8,128)}), f32[8,32,16,128]{3,2,1,0:T(8,128)S(1)}, u32[]{:S(2)}, u32[]{:S(2)}) async-start(f32[8,32,16,128]{3,2,1,0:T(8,128)} %fusion.30), calls=%async_computation | async-start | bytes 4194304 | tf_op jit(solution)/shard_map/all_to_all | solution.py:35
  141.8 56.0 %all-to-all-start.1 = ((f32[8,32,16,128]{3,2,1,0:T(8,128)}), f32[8,32,16,128]{3,2,1,0:T(8,128)S(1)}, u32[]{:S(2)}, u32[]{:S(2)}) async-start(f32[8,32,16,128]{3,2,1,0:T(8,128)} %fusion.34), calls=%async_computation.1 | async-start | bytes 4194304 | tf_op jit(solution)/shard_map/all_to_all | solution.py:42
  198.1 14.5 %slice-start = ((s8[8388608]{0:T(1024)(128)(4,1)}), s8[4194304]{0:T(1024)(128)(4,1)S(1)}, s32[]{:S(2)}) async-start(s8[8388608]{0:T(1024)(128)(4,1)} %bitcast.116), calls=%async_computation.2 | async-start | bytes 8388608
  201.6 11.0 %slice-start.1 = ((s8[8388608]{0:T(1024)(128)(4,1)}), s8[4194304]{0:T(1024)(128)(4,1)S(1)}, s32[]{:S(2)}) async-start(s8[8388608]{0:T(1024)(128)(4,1)} %bitcast.116), calls=%async_computation.3 | async-start | bytes 8388608
  201.7 11.0 %copy-start.1 = (f32[4,256,256]{2,1,0:T(8,128)S(1)}, f32[4,256,256]{2,1,0:T(8,128)}, u32[]{:S(2)}) copy-start(f32[4,256,256]{2,1,0:T(8,128)} %fusion.53) | copy-start | bytes 3145732
  201.7 11.0 %copy-start.3 = (f32[32]{0:T(128)S(1)}, f32[32]{0:T(128)}, u32[]{:S(2)}) copy-start(f32[32]{0:T(128)} %param.17) | copy-start | bytes 388
  249.4 21.9 %copy-start.2 = (f32[4096]{0:T(1024)S(1)}, f32[4096]{0:T(1024)}, u32[]{:S(2)}) copy-start(f32[4096]{0:T(1024)} %param.20) | copy-start | bytes 49156

commit v2 on v1

--- a/solution.py
+++ b/solution.py
@@ -1,6 +1,10 @@
+import functools
+
 import jax
 import jax.numpy as jnp
 from jax import lax
+from jax.experimental import pallas as pl
+from jax.experimental.pallas import tpu as pltpu
 from jax.sharding import PartitionSpec as P
 
 SEGMENT_LENGTH = 256
@@ -12,19 +16,6 @@
     devices = range(lax.axis_size(axis))
     route = [(i - distance, i) for i in devices if i - distance in devices]
     return lax.ppermute(block, axis, route)
-
-
-def prefix(part, axis, combine, identity):
-    place = lax.axis_index(axis)
-    gathered = jax.tree.map(lambda a: lax.all_gather(a, axis), part)
-    state = jax.tree.map(lambda a, e: jnp.zeros_like(a) + jnp.asarray(e, a.dtype), part, identity)
-
-    def one(turn, state):
-        return combine(
-            state, jax.tree.map(lambda a: lax.dynamic_index_in_dim(a, turn, 0, False), gathered)
-        )
-
-    return lax.fori_loop(0, place, one, state)
 
 
 def scan_states(factor, state, axis):
@@ -55,8 +46,134 @@
     return jax.nn.silu(accum).astype(jnp.bfloat16)
 
 
-def combine_states(earlier, latter):
-    return (earlier[0] * latter[0], latter[0][:, None, None] * earlier[1] + latter[1])
+def state_kernel(x_ref, bt_ref, toend_ref, out_ref):
+    xw = (x_ref[...].astype(jnp.float32) * toend_ref[0, 0]).astype(jnp.bfloat16)
+    out_ref[0, 0] = jnp.dot(bt_ref[0], xw, preferred_element_type=jnp.float32)
+
+
+def intra_kernel(skip_ref, c_ref, b_ref, x_ref, cumc_ref, cumr_ref, stepr_ref, out_ref, scores):
+    head = pl.program_id(1)
+
+    @pl.when(head == 0)
+    def _():
+        scores[...] = lax.dot_general(
+            c_ref[...], b_ref[...], (((1,), (1,)), ((), ())), preferred_element_type=jnp.float32
+        )
+
+    length = scores.shape[0]
+    rows = lax.broadcasted_iota(jnp.int32, (length, length), 0)
+    cols = lax.broadcasted_iota(jnp.int32, (length, length), 1)
+    causal = rows >= cols
+    diff = cumc_ref[0, 0] - cumr_ref[0, 0]
+    decay = jnp.where(causal, jnp.exp(jnp.where(causal, diff, 0.0)), 0.0)
+    weights = (scores[...] * decay * stepr_ref[0, 0]).astype(jnp.bfloat16)
+    x = x_ref[...]
+    intra = jnp.dot(weights, x, preferred_element_type=jnp.float32)
+    out_ref[...] = intra + skip_ref[head] * x.astype(jnp.float32)
+
+
+def gate_kernel(part_ref, c_ref, state_ref, ecum_ref, z_ref, out_ref, sq_ref):
+    head = pl.program_id(1)
+    state = state_ref[0, 0]
+    high = state.astype(jnp.bfloat16)
+    rest = state - high.astype(jnp.float32)
+    mid = rest.astype(jnp.bfloat16)
+    low = (rest - mid.astype(jnp.float32)).astype(jnp.bfloat16)
+    c = c_ref[...]
+    inter = (
+        jnp.dot(c, high, preferred_element_type=jnp.float32)
+        + jnp.dot(c, mid, preferred_element_type=jnp.float32)
+        + jnp.dot(c, low, preferred_element_type=jnp.float32)
+    )
+    y = part_ref[...] + inter * ecum_ref[0, 0]
+    z = z_ref[...].astype(jnp.float32)
+    gated = y * (z / (1.0 + jnp.exp(-z)))
+    out_ref[...] = gated
+    total = jnp.sum(gated * gated, axis=1, keepdims=True)
+
+    @pl.when(head == 0)
+    def _():
+        sq_ref[...] = total
+
+    @pl.when(head > 0)
+    def _():
+        sq_ref[...] = sq_ref[...] + total
+
+
+def block_states(xconv, b_t, to_end_col, spans, heads, width):
+    rows = xconv.shape[0]
+    size = b_t.shape[1]
+    return pl.pallas_call(
+        state_kernel,
+        grid=(spans, heads),
+        in_specs=[
+            pl.BlockSpec((SEGMENT_LENGTH, width), lambda c, h: (c, h)),
+            pl.BlockSpec((1, size, SEGMENT_LENGTH), lambda c, h: (c, 0, 0)),
+            pl.BlockSpec((1, 1, SEGMENT_LENGTH, 1), lambda c, h: (c, h, 0, 0)),
+        ],
+        out_specs=pl.BlockSpec((1, 1, size, width), lambda c, h: (c, h, 0, 0)),
+        out_shape=jax.ShapeDtypeStruct((spans, heads, size, width), jnp.float32),
+        cost_estimate=pl.CostEstimate(
+            flops=2 * rows * heads * width * size,
+            bytes_accessed=rows * heads * width * 2 + spans * heads * size * width * 4,
+            transcendentals=0,
+        ),
+    )(xconv, b_t, to_end_col)
+
+
+def intra_terms(skip_gain, c_part, b_part, xconv, cum_col, cum_row, step_row, spans, heads, width):
+    rows = xconv.shape[0]
+    size = c_part.shape[1]
+    return pl.pallas_call(
+        intra_kernel,
+        grid=(spans, heads),
+        in_specs=[
+            pl.BlockSpec(memory_space=pltpu.SMEM),
+            pl.BlockSpec((SEGMENT_LENGTH, size), lambda c, h: (c, 0)),
+            pl.BlockSpec((SEGMENT_LENGTH, size), lambda c, h: (c, 0)),
+            pl.BlockSpec((SEGMENT_LENGTH, width), lambda c, h: (c, h)),
+            pl.BlockSpec((1, 1, SEGMENT_LENGTH, 1), lambda c, h: (c, h, 0, 0)),
+            pl.BlockSpec((1, 1, 1, SEGMENT_LENGTH), lambda c, h: (c, h, 0, 0)),
+            pl.BlockSpec((1, 1, 1, SEGMENT_LENGTH), lambda c, h: (c, h, 0, 0)),
+        ],
+        out_specs=pl.BlockSpec((SEGMENT_LENGTH, width), lambda c, h: (c, h)),
+        out_shape=jax.ShapeDtypeStruct((rows, heads * width), jnp.float32),
+        scratch_shapes=[pltpu.VMEM((SEGMENT_LENGTH, SEGMENT_LENGTH), jnp.float32)],
+        cost_estimate=pl.CostEstimate(
+            flops=2 * rows * SEGMENT_LENGTH * (heads * width + size),
+            bytes_accessed=rows * heads * width * 6,
+            transcendentals=rows * SEGMENT_LENGTH * heads,
+        ),
+    )(skip_gain, c_part, b_part, xconv, cum_col, cum_row, step_row)
+
+
+def gate_terms(partial, c_part, state_enter, ecum_col, gate_in, spans, heads, width):
+    rows = partial.shape[0]
+    size = c_part.shape[1]
+    return pl.pallas_call(
+        gate_kernel,
+        grid=(spans, heads),
+        in_specs=[
+            pl.BlockSpec((SEGMENT_LENGTH, width), lambda c, h: (c, h)),
+            pl.BlockSpec((SEGMENT_LENGTH, size), lambda c, h: (c, 0)),
+            pl.BlockSpec((1, 1, size, width), lambda c, h: (c, h, 0, 0)),
+            pl.BlockSpec((1, 1, SEGMENT_LENGTH, 1), lambda c, h: (c, h, 0, 0)),
+            pl.BlockSpec((SEGMENT_LENGTH, width), lambda c, h: (c, h)),
+        ],
+        out_specs=[
+            pl.BlockSpec((SEGMENT_LENGTH, width), lambda c, h: (c, h)),
+            pl.BlockSpec((SEGMENT_LENGTH, 1), lambda c, h: (c, 0)),
+        ],
+        out_shape=[
+            jax.ShapeDtypeStruct((rows, heads * width), jnp.float32),
+            jax.ShapeDtypeStruct((rows, 1), jnp.float32),
+        ],
+        cost_estimate=pl.CostEstimate(
+            flops=6 * rows * size * heads * width,
+            bytes_accessed=rows * heads * width * 10,
+            transcendentals=rows * heads * width,
+        ),
+    )(partial, c_part, state_enter, ecum_col, gate_in)
 
 
 def local(
@@ -85,27 +202,31 @@
     bc_local = conv_silu(bc_proj, prev_bc, conv_bc)
     bc_full = lax.all_gather(bc_local, "ch", axis=1, tiled=True)
     state_size = bc_full.shape[1] // 2
+    b_part = bc_full[:, :state_size]
+    c_part = bc_full[:, state_size:]
+    b_t = b_part.reshape(span_count, SEGMENT_LENGTH, state_size).transpose(0, 2, 1)
     row_valid = (jnp.arange(row_count) < live_rows).astype(jnp.float32)
     step_size = jax.nn.softplus(dt_raw + dt_bias[None, :]) * row_valid[:, None]
-    xfour = xconv.reshape(span_count, SEGMENT_LENGTH, head_count, head_size)
-    b_three = bc_full[:, :state_size].reshape(span_count, SEGMENT_LENGTH, state_size)
-    c_three = bc_full[:, state_size:].reshape(span_count, SEGMENT_LENGTH, state_size)
     step_three = step_size.reshape(span_count, SEGMENT_LENGTH, head_count)
     cumul = jnp.cumsum(-rate[None, None, :] * step_three, axis=1)
-    scores = jnp.einsum("cqn,csn->cqs", c_three, b_three, preferred_element_type=jnp.float32)
     cum_heads = jnp.transpose(cumul, (0, 2, 1))
-    diff = cum_heads[:, :, :, None] - cum_heads[:, :, None, :]
-    causal = jnp.arange(SEGMENT_LENGTH)[:, None] >= jnp.arange(SEGMENT_LENGTH)[None, :]
-    decay = jnp.where(causal, jnp.exp(jnp.where(causal, diff, 0.0)), 0.0)
-    weights = (
-        scores[:, None] * decay * jnp.transpose(step_three, (0, 2, 1))[:, :, None, :]
-    ).astype(jnp.bfloat16)
-    intra = jnp.einsum("chqs,cshp->cqhp", weights, xfour, preferred_element_type=jnp.float32)
+    step_heads = jnp.transpose(step_three, (0, 2, 1))
     last_cum = cum_heads[:, :, -1]
-    to_end = jnp.exp(last_cum[:, None, :] - cumul) * step_three
-    x_weighted = (xfour.astype(jnp.float32) * to_end[..., None]).astype(jnp.bfloat16)
-    block_state = jnp.einsum(
-        "csn,cshp->chnp", b_three, x_weighted, preferred_element_type=jnp.float32
+    to_end = jnp.exp(last_cum[:, :, None] - cum_heads) * step_heads
+    block_state = block_states(
+        xconv, b_t, to_end[..., None], span_count, head_count, head_size
+    )
+    partial = intra_terms(
+        skip_gain,
+        c_part,
+        b_part,
+        xconv,
+        cum_heads[..., None],
+        cum_heads[:, :, None, :],
+        step_heads[:, :, None, :],
+        span_count,
+        head_count,
+        head_size,
     )
     block_decay = jnp.exp(last_cum)
     current = jnp.zeros((head_count, state_size, head_size), jnp.float32)
@@ -125,14 +246,17 @@
         ],
         axis=0,
     )
-    inter = jnp.einsum(
-        "cqn,chnp->cqhp", c_three.astype(jnp.float32), state_enter, precision=lax.Precision.HIGHEST
-    )
-    inter = inter * jnp.exp(cumul)[..., None]
-    y_full = intra + inter + skip_gain[None, None, :, None] * xfour.astype(jnp.float32)
-    y_full = y_full.reshape(row_count, channels)
-    gated = y_full * jax.nn.silu(gate_in.astype(jnp.float32))
-    square_sum = lax.psum(jnp.sum(gated * gated, axis=1), "ch")
+    gated, square_part = gate_terms(
+        partial,
+        c_part,
+        state_enter,
+        jnp.exp(cum_heads)[..., None],
+        gate_in,
+        span_count,
+        head_count,
+        head_size,
+    )
+    square_sum = lax.psum(square_part[:, 0], "ch")
     mean_sq = square_sum / INNER
     normed = gated * lax.rsqrt(mean_sq + 1e-05)[:, None] * norm_gain[None, :] * row_valid[:, None]
     return normed.astype(jnp.bfloat16)

time: 296 us -> 432 us (1.46); the launches traced: 295 us -> 425 us
  Pallas kernels: 0 us -> 252 us
  waiting for transfers between devices: 44.1 us -> 0.01 us
  matrix products: 35.5 us -> 0 us
  other arithmetic: 78.1 us -> 49.6 us
  local copies, waits for them, and re-layouts: 50 us -> 36 us
    pallas_call x0 -> x3, Pallas kernels: none -> 252 us  [the longest x1 88.7 us: gate_terms(): pl.pallas_call(gate_kernel, grid=(spans, heads), in_specs=[pl.BlockSpec((...]
    all_to_all x1, waiting for transfers between devices: 44.1 us -> 0.01 us  [scan_states(): back = lax.all_to_all(jnp.stack(entries, axis=0), axis, 0, 0, tiled=True)]
    dot_general x4 -> x0, matrix products: 35.5 us -> none  [the longest x1 16.9 us: local(): jnp.einsum('chqs,cshp->cqhp', weights, xfour, preferred_element_type=jnp....]
    add x1 -> x0, local copies, waits for them, and re-layouts: 19.9 us -> none  [local(): intra + inter + skip_gain[None, None, :, None] * xfour.astype(jnp.float32)]
    unnamed x8 -> x6, other arithmetic: 23.8 us -> 4.95 us
    convert_element_type x1 -> x2, other arithmetic: 1.54 us -> 19 us  [conv_silu(): return jax.nn.silu(accum).astype(jnp.bfloat16)]
    reduce_sum x1 -> x0, other arithmetic: 16.2 us -> none  [local(): square_sum = lax.psum(jnp.sum(gated * gated, axis=1), 'ch')]
    convert_element_type x1, other arithmetic: 23.8 us -> 9.96 us  [local(): return normed.astype(jnp.bfloat16)]
  transfers between devices with their start and end apart: 4 -> 4, of which waited for: 1 -> 0; matrix products, arithmetic and copies ran while one was open for 4% -> 8% of each run, Pallas kernels for 0% -> 20%
where the time goes in v2:
time: 432 us; the launch traced here: 425 us
  Pallas kernels  252 us (58%)
  blocking collectives  63.2 us (15%)
  other arithmetic  49.6 us (11%)
  local copies, waits for them, and re-layouts  36 us (8%)
  starting transfers between devices  23.3 us (5%)
    pallas_call x1, Pallas kernels, gate_terms(): pl.pallas_call(gate_kernel, grid=(spans, heads), in_specs=[pl.BlockSpec((...  88.7 us
    pallas_call x1, Pallas kernels, intra_terms(): pl.pallas_call(intra_kernel, grid=(spans, heads), in_specs=[pl.BlockSpec(...  83.1 us
    pallas_call x1, Pallas kernels, block_states(): pl.pallas_call(state_kernel, grid=(spans, heads), in_specs=[pl.BlockSpec(...  80.5 us
    all_gather x1, blocking collectives, scan_states(): decays = lax.all_gather(factor, axis)  50.3 us
    convert_element_type x2, other arithmetic, conv_silu(): return jax.nn.silu(accum).astype(jnp.bfloat16)  19 us
    all_to_all x1, starting transfers between devices, scan_states(): back = lax.all_to_all(jnp.stack(entries, axis=0), axis, 0, 0, tiled=True)  10.2 us
    convert_element_type x1, other arithmetic, local(): return normed.astype(jnp.bfloat16)  9.96 us
    another operation x5, local copies, waits for them, and re-layouts  8.82 us
  transfers between devices with their start and end apart: 4, of which 0 were waited for; matrix products, arithmetic and copies ran while one was open for 8% of the time, Pallas kernels for 20%

profile of v2, /device:TPU:0, one launch (start us, length us, event | category | flops | bytes accessed | tf_op | source)
XLA Modules:
  0.0 425.3 jit_solution(14353913385798059799)
XLA Ops:
  1.5 4.9 %collective-permute-start = (bf16[3,64]{0,1:T(8,128)(2,1)S(1)}, bf16[3,64]{0,1:T(8,128)(2,1)S(1)}, u32[]{:S(2)}, u32[]{:S(2)}) collective-permute-start(bf16[3,64]{0,1:T(8,128)(2,1)S(1)} %constant_dynamic-slice_fusion.1), channel_id=1, source_target_pairs={{0,4},{4,8},{8,12},{12,16},{16,20},{20,24},{24,28},{1,5},{5,9},{9,... | collective-permute-start | bytes 1160 | tf_op jit(solution)/shard_map/ppermute | solution.py:18
  6.3 0.9 constant_dynamic-slice_fusion
  7.2 3.5 collective-permute-start.1
  10.7 1.1 fusion.10
  12.7 2.3 reduce-window.6
  15.9 8.6 %copy.81.toend_ref = f32[4,32,256,1]{3,2,1,0:T(8,128)} copy(f32[4,32,256,1]{2,1,0,3:T(8,128)S(1)} %multiply_bitcast_fusion) | data formatting | bytes 262144 | tf_op jit(solution)/shard_map/broadcast_in_dim | solution.py:217
  24.7 7.2 %all_gather.7 = bf16[1024,256]{0,1:T(8,128)(2,1)S(1)} all-gather(bf16[1024,64]{0,1:T(8,128)(2,1)S(1)} %multiply_convert_fusion.2), channel_id=1, replica_groups=mesh['seq'=8,'ch'=4] {'ch'}, dimensions={1}, use_global_device_ids=true | all-gather | bytes 655360 | tf_op jit(solution)/shard_map/all_gather | solution.py:203
  32.1 0.9 copy.80
  33.0 18.7 %multiply_convert_fusion.1.x_ref = bf16[1024,4096]{1,0:T(8,128)(2,1)} fusion(bf16[1024,4096]{1,0:T(8,128)(2,1)} %param.11, bf16[3,4096]{1,0:T(4,128)(2,1)S(1)} %collective-permute-done.1, f32[4096]{0:T(1024)S(1)} %bitcast.109, f32[4096]{0:T(1024)S(1)} %bitcast.110, f32[4096]{0:T(1024)S(1)} %bitcast.108, f32[4096]{0:T(1024)S(1)} %bitcast.107), kind=kLoop, calls=%fused_computation.1 | loop fusion | flops 104857600 | bytes 16867328 | tf_op jit(solution)/shard_map/convert_element_type | solution.py:46
  51.7 80.5 %shard_map.110 = f32[4,32,128,128]{3,2,1,0:T(8,128)} custom-call(bf16[1024,4096]{1,0:T(8,128)(2,1)} %multiply_convert_fusion.1.x_ref, bf16[4,128,256]{2,1,0:T(8,128)(2,1)} %bitcast.105, f32[4,32,256,1]{3,2,1,0:T(8,128)} %copy.81.toend_ref), custom_call_target="tpu_custom_call" | custom-call | flops 1073741824 | bytes 16777216 | tf_op jit(solution)/shard_map/pallas_call | solution.py:106
  132.2 4.0 fusion.20
  136.2 2.0 fusion.2
  138.3 4.8 %all-to-all-start = ((f32[8,32,16,128]{3,2,1,0:T(8,128)}), f32[8,32,16,128]{3,2,1,0:T(8,128)S(1)}, u32[]{:S(2)}, u32[]{:S(2)}) async-start(f32[8,32,16,128]{3,2,1,0:T(8,128)} %fusion.2), calls=%async_computation | async-start | bytes 4194304 | tf_op jit(solution)/shard_map/all_to_all | solution.py:26
  143.1 50.3 %all-gather = f32[8,1,32]{2,1,0:T(1,128)S(1)} all-gather(f32[1,1,32]{2,1,0:T(1,128)S(1)} %get-tuple-element.39), channel_id=1, replica_groups=mesh['seq'=8,'ch'=4] {'seq'}, dimensions={0}, use_global_device_ids=true | all-gather | bytes 1152 | tf_op jit(solution)/shard_map/all_gather | solution.py:27
  199.8 10.2 %all-to-all-start.1 = ((f32[8,32,16,128]{3,2,1,0:T(8,128)}), f32[8,32,16,128]{3,2,1,0:T(8,128)S(1)}, u32[]{:S(2)}, u32[]{:S(2)}) async-start(f32[8,32,16,128]{3,2,1,0:T(8,128)} %fusion.6), calls=%async_computation.1 | async-start | bytes 4194304 | tf_op jit(solution)/shard_map/all_to_all | solution.py:33
  210.4 8.6 %copy.78.cumc_ref = f32[4,32,256,1]{3,2,1,0:T(8,128)} copy(f32[4,32,256,1]{2,1,0,3:T(8,128)S(1)} %reduce_window_sum.40) | data formatting | bytes 262144 | tf_op jit(solution)/shard_map/reduce_window_sum
  219.8 8.6 %copy.88.ecum_ref = f32[4,32,256,1]{3,2,1,0:T(8,128)} copy(f32[4,32,256,1]{2,1,3,0:T(8,128)S(1)} %bitcast_exponential_fusion) | data formatting | bytes 262144 | tf_op jit(solution)/shard_map/exp | solution.py:253
  229.2 83.1 %shard_map.109.part_ref = f32[1024,4096]{1,0:T(8,128)} custom-call(f32[32]{0:T(128)} %skip_ref.1, bf16[1024,128]{1,0:T(8,128)(2,1)} %copy.89.c_ref, bf16[1024,128]{1,0:T(8,128)(2,1)} %copy-done, bf16[1024,4096]{1,0:T(8,128)(2,1)} %multiply_convert_fusion.1.x_ref, f32[4,32,256,1]{3,2,1,0:T(8,128)} %copy.78.cumc_ref, f32[4,32,1,256]{3,2,1,0:T(1,128)} %bitcast.104, ...), custom_call_target="tpu_custom_call" | custom-call | flops 2214592512 | bytes 25165824 | tf_op jit(solution)/shard_map/pallas_call | solution.py:127
  312.6 3.4 multiply_add_fusion.1
  316.0 3.7 pad_maximum_fusion.1.state_ref
  319.7 88.7 %shard_map.111 = (f32[1024,4096]{1,0:T(8,128)}, f32[1024,1]{1,0:T(8,128)}) custom-call(f32[1024,4096]{1,0:T(8,128)} %shard_map.109.part_ref, bf16[1024,128]{1,0:T(8,128)(2,1)} %copy.89.c_ref, f32[4,32,128,128]{3,2,1,0:T(8,128)} %pad_maximum_fusion.1.state_ref, f32[4,32,256,1]{3,2,1,0:T(8,128)} %copy.88.ecum_ref, bf16[1024,4096]{1,0:T(8,128)(2,1)} %z_ref.1), custom_call_target="tpu_custom_call" | custom-call | flops 3221225472 | bytes 41943040 | tf_op jit(solution)/shard_map/pallas_call | solution.py:153
  408.4 1.2 reduce.1
  409.6 5.7 %psum.7 = f32[1024]{0:T(1024)S(1)} all-reduce(f32[1024]{0:T(1024)S(1)} %reduce.1), channel_id=1, replica_groups=mesh['seq'=8,'ch'=4] {'ch'}, use_global_device_ids=true, to_apply=%region_2.3 | all-reduce | flops 1024 | bytes 8192 | tf_op jit(solution)/shard_map/psum | solution.py:259
  415.3 10.0 %multiply_convert_fusion = bf16[1024,4096]{1,0:T(8,128)(2,1)} fusion(f32[1024,4096]{1,0:T(8,128)} %get-tuple-element.7, f32[1024]{0:T(1024)S(1)} %fusion.15, f32[4096]{0:T(1024)S(1)} %copy-done.4, f32[1024]{0:T(1024)S(1)} %add_rsqrt_fusion), kind=kLoop, calls=%fused_computation | loop fusion | flops 16777216 | bytes 25190400 | tf_op jit(solution)/shard_map/convert_element_type | solution.py:262
  (57 shorter events, 11.7 us)
Async XLA Ops:
  0.0 15.8 %copy-start.3 = (bf16[4,4096]{1,0:T(4,128)(2,1)S(1)}, bf16[4,4096]{1,0:T(4,128)(2,1)}, u32[]{:S(2)}) copy-start(bf16[4,4096]{1,0:T(4,128)(2,1)} %param.18) | copy-start | bytes 98308
  0.0 15.8 %copy-start.5 = (bf16[4,64]{1,0:T(4,128)(2,1)S(1)}, bf16[4,64]{1,0:T(4,128)(2,1)}, u32[]{:S(2)}) copy-start(bf16[4,64]{1,0:T(4,128)(2,1)} %param.19) | copy-start | bytes 1540
  1.5 23.0 %collective-permute-start = (bf16[3,64]{0,1:T(8,128)(2,1)S(1)}, bf16[3,64]{0,1:T(8,128)(2,1)S(1)}, u32[]{:S(2)}, u32[]{:S(2)}) collective-permute-start(bf16[3,64]{0,1:T(8,128)(2,1)S(1)} %constant_dynamic-slice_fusion.1), channel_id=1, source_target_pairs={{0,4},{4,8},{8,12},{12,16},{16,20},{20,24},{24,28},{1,5},{5,9},{9,... | collective-permute-start | bytes 1160 | tf_op jit(solution)/shard_map/ppermute | solution.py:18
  7.2 25.8 %collective-permute-start.1 = (bf16[3,4096]{1,0:T(4,128)(2,1)S(1)}, bf16[3,4096]{1,0:T(4,128)(2,1)S(1)}, u32[]{:S(2)}, u32[]{:S(2)}) collective-permute-start(bf16[3,4096]{1,0:T(4,128)(2,1)S(1)} %constant_dynamic-slice_fusion), channel_id=1, source_target_pairs={{0,4},{4,8},{8,12},{12,16},{16,20},{20,24},{24,28},{1,5},{5,9},{9,... | collective-permute-start | bytes 73736 | tf_op jit(solution)/shard_map/ppermute | solution.py:18
  15.8 8.6 %copy-start.2 = (bf16[1024,64]{0,1:T(8,128)(2,1)S(1)}, bf16[1024,64]{0,1:T(8,128)(2,1)}, u32[]{:S(2)}) copy-start(bf16[1024,64]{0,1:T(8,128)(2,1)} %param.13) | copy-start | bytes 393220
  32.1 19.6 %copy-start = (bf16[1024,128]{1,0:T(8,128)(2,1)}, bf16[1024,128]{1,0:T(8,128)(2,1)S(1)}, u32[]{:S(2)}) copy-start(bf16[1024,128]{1,0:T(8,128)(2,1)S(1)} %copy.90.b_ref) | copy-start | bytes 786436
  138.3 55.8 %all-to-all-start = ((f32[8,32,16,128]{3,2,1,0:T(8,128)}), f32[8,32,16,128]{3,2,1,0:T(8,128)S(1)}, u32[]{:S(2)}, u32[]{:S(2)}) async-start(f32[8,32,16,128]{3,2,1,0:T(8,128)} %fusion.2), calls=%async_computation | async-start | bytes 4194304 | tf_op jit(solution)/shard_map/all_to_all | solution.py:26
  199.8 112.5 %all-to-all-start.1 = ((f32[8,32,16,128]{3,2,1,0:T(8,128)}), f32[8,32,16,128]{3,2,1,0:T(8,128)S(1)}, u32[]{:S(2)}, u32[]{:S(2)}) async-start(f32[8,32,16,128]{3,2,1,0:T(8,128)} %fusion.6), calls=%async_computation.1 | async-start | bytes 4194304 | tf_op jit(solution)/shard_map/all_to_all | solution.py:33
  210.3 8.7 %copy-start.1 = (f32[4,32,2,128]{3,2,1,0:T(2,128)}, f32[4,32,2,128]{3,2,1,0:T(2,128)S(1)}, u32[]{:S(2)}) copy-start(f32[4,32,2,128]{3,2,1,0:T(2,128)S(1)} %copy.75) | copy-start | bytes 393220
  319.7 95.6 %copy-start.4 = (f32[4096]{0:T(1024)S(1)}, f32[4096]{0:T(1024)}, u32[]{:S(2)}) copy-start(f32[4096]{0:T(1024)} %param.20) | copy-start | bytes 49156

commit v3 on v2

--- a/solution.py
+++ b/solution.py
@@ -46,123 +46,154 @@
     return jax.nn.silu(accum).astype(jnp.bfloat16)
 
 
+HEAD_GROUP = 8
+
+
 def state_kernel(x_ref, bt_ref, toend_ref, out_ref):
-    xw = (x_ref[...].astype(jnp.float32) * toend_ref[0, 0]).astype(jnp.bfloat16)
-    out_ref[0, 0] = jnp.dot(bt_ref[0], xw, preferred_element_type=jnp.float32)
-
-
-def intra_kernel(skip_ref, c_ref, b_ref, x_ref, cumc_ref, cumr_ref, stepr_ref, out_ref, scores):
-    head = pl.program_id(1)
-
-    @pl.when(head == 0)
-    def _():
-        scores[...] = lax.dot_general(
-            c_ref[...], b_ref[...], (((1,), (1,)), ((), ())), preferred_element_type=jnp.float32
-        )
-
+    width = out_ref.shape[-1]
+    bt = bt_ref[0]
+    for j in range(out_ref.shape[1]):
+        x = x_ref[:, j * width : (j + 1) * width].astype(jnp.float32)
+        xw = (x * toend_ref[0, 0, :, j : j + 1]).astype(jnp.bfloat16)
+        out_ref[0, j] = jnp.dot(bt, xw, preferred_element_type=jnp.float32)
+
+
+def intra_kernel(skip_ref, c_ref, b_ref, x_ref, cumc_ref, cumr_ref, stepr_ref, out_ref):
+    group = pl.program_id(1)
+    heads = cumc_ref.shape[-1]
+    width = out_ref.shape[-1] // heads
+    scores = lax.dot_general(
+        c_ref[...], b_ref[...], (((1,), (1,)), ((), ())), preferred_element_type=jnp.float32
+    )
     length = scores.shape[0]
     rows = lax.broadcasted_iota(jnp.int32, (length, length), 0)
     cols = lax.broadcasted_iota(jnp.int32, (length, length), 1)
     causal = rows >= cols
-    diff = cumc_ref[0, 0] - cumr_ref[0, 0]
-    decay = jnp.where(causal, jnp.exp(jnp.where(causal, diff, 0.0)), 0.0)
-    weights = (scores[...] * decay * stepr_ref[0, 0]).astype(jnp.bfloat16)
-    x = x_ref[...]
-    intra = jnp.dot(weights, x, preferred_element_type=jnp.float32)
-    out_ref[...] = intra + skip_ref[head] * x.astype(jnp.float32)
+    for j in range(heads):
+        diff = cumc_ref[0, 0, :, j : j + 1] - cumr_ref[0, 0, j : j + 1, :]
+        decay = jnp.where(causal, jnp.exp(jnp.where(causal, diff, 0.0)), 0.0)
+        weights = (scores * decay * stepr_ref[0, 0, j : j + 1, :]).astype(jnp.bfloat16)
+        x = x_ref[:, j * width : (j + 1) * width]
+        intra = jnp.dot(weights, x, preferred_element_type=jnp.float32)
+        out_ref[:, j * width : (j + 1) * width] = (
+            intra + skip_ref[group * heads + j] * x.astype(jnp.float32)
+        )
 
 
 def gate_kernel(part_ref, c_ref, state_ref, ecum_ref, z_ref, out_ref, sq_ref):
-    head = pl.program_id(1)
-    state = state_ref[0, 0]
-    high = state.astype(jnp.bfloat16)
-    rest = state - high.astype(jnp.float32)
-    mid = rest.astype(jnp.bfloat16)
-    low = (rest - mid.astype(jnp.float32)).astype(jnp.bfloat16)
+    group = pl.program_id(1)
+    heads = ecum_ref.shape[-1]
+    width = out_ref.shape[-1] // heads
     c = c_ref[...]
-    inter = (
-        jnp.dot(c, high, preferred_element_type=jnp.float32)
-        + jnp.dot(c, mid, preferred_element_type=jnp.float32)
-        + jnp.dot(c, low, preferred_element_type=jnp.float32)
-    )
-    y = part_ref[...] + inter * ecum_ref[0, 0]
-    z = z_ref[...].astype(jnp.float32)
-    gated = y * (z / (1.0 + jnp.exp(-z)))
-    out_ref[...] = gated
-    total = jnp.sum(gated * gated, axis=1, keepdims=True)
-
-    @pl.when(head == 0)
+    total = jnp.zeros((c.shape[0], 1), jnp.float32)
+    for j in range(heads):
+        state = state_ref[0, j]
+        high = state.astype(jnp.bfloat16)
+        rest = state - high.astype(jnp.float32)
+        mid = rest.astype(jnp.bfloat16)
+        low = (rest - mid.astype(jnp.float32)).astype(jnp.bfloat16)
+        inter = (
+            jnp.dot(c, high, preferred_element_type=jnp.float32)
+            + jnp.dot(c, mid, preferred_element_type=jnp.float32)
+            + jnp.dot(c, low, preferred_element_type=jnp.float32)
+        )
+        columns = slice(j * width, (j + 1) * width)
+        y = part_ref[:, columns] + inter * ecum_ref[0, 0, :, j : j + 1]
+        z = z_ref[:, columns].astype(jnp.float32)
+        gated = y * (z / (1.0 + jnp.exp(-z)))
+        out_ref[:, columns] = gated
+        total = total + jnp.sum(gated * gated, axis=1, keepdims=True)
+
+    @pl.when(group == 0)
     def _():
         sq_ref[...] = total
 
-    @pl.when(head > 0)
+    @pl.when(group > 0)
     def _():
         sq_ref[...] = sq_ref[...] + total
 
 
-def block_states(xconv, b_t, to_end_col, spans, heads, width):
+def by_group(values, spans, heads):
+    return values.reshape(spans, heads // HEAD_GROUP, HEAD_GROUP, -1)
+
+
+def columns_by_group(values, spans, heads):
+    return by_group(values, spans, heads).transpose(0, 1, 3, 2)
+
+
+def block_states(xconv, b_t, to_end, spans, heads, width):
     rows = xconv.shape[0]
     size = b_t.shape[1]
+    group = HEAD_GROUP
     return pl.pallas_call(
         state_kernel,
-        grid=(spans, heads),
+        grid=(spans, heads // group),
         in_specs=[
-            pl.BlockSpec((SEGMENT_LENGTH, width), lambda c, h: (c, h)),
-            pl.BlockSpec((1, size, SEGMENT_LENGTH), lambda c, h: (c, 0, 0)),
-            pl.BlockSpec((1, 1, SEGMENT_LENGTH, 1), lambda c, h: (c, h, 0, 0)),
-        ],
-        out_specs=pl.BlockSpec((1, 1, size, width), lambda c, h: (c, h, 0, 0)),
+            pl.BlockSpec((SEGMENT_LENGTH, group * width), lambda c, g: (c, g)),
+            pl.BlockSpec((1, size, SEGMENT_LENGTH), lambda c, g: (c, 0, 0)),
+            pl.BlockSpec((1, 1, SEGMENT_LENGTH, group), lambda c, g: (c, g, 0, 0)),
+        ],
+        out_specs=pl.BlockSpec((1, group, size, width), lambda c, g: (c, g, 0, 0)),
         out_shape=jax.ShapeDtypeStruct((spans, heads, size, width), jnp.float32),
         cost_estimate=pl.CostEstimate(
             flops=2 * rows * heads * width * size,
             bytes_accessed=rows * heads * width * 2 + spans * heads * size * width * 4,
             transcendentals=0,
         ),
-    )(xconv, b_t, to_end_col)
-
-
-def intra_terms(skip_gain, c_part, b_part, xconv, cum_col, cum_row, step_row, spans, heads, width):
+    )(xconv, b_t, columns_by_group(to_end, spans, heads))
+
+
+def intra_terms(skip_gain, c_part, b_part, xconv, cum_heads, step_heads, spans, heads, width):
     rows = xconv.shape[0]
     size = c_part.shape[1]
+    group = HEAD_GROUP
     return pl.pallas_call(
         intra_kernel,
-        grid=(spans, heads),
+        grid=(spans, heads // group),
         in_specs=[
             pl.BlockSpec(memory_space=pltpu.SMEM),
-            pl.BlockSpec((SEGMENT_LENGTH, size), lambda c, h: (c, 0)),
-            pl.BlockSpec((SEGMENT_LENGTH, size), lambda c, h: (c, 0)),
-            pl.BlockSpec((SEGMENT_LENGTH, width), lambda c, h: (c, h)),
-            pl.BlockSpec((1, 1, SEGMENT_LENGTH, 1), lambda c, h: (c, h, 0, 0)),
-            pl.BlockSpec((1, 1, 1, SEGMENT_LENGTH), lambda c, h: (c, h, 0, 0)),
-            pl.BlockSpec((1, 1, 1, SEGMENT_LENGTH), lambda c, h: (c, h, 0, 0)),
-        ],
-        out_specs=pl.BlockSpec((SEGMENT_LENGTH, width), lambda c, h: (c, h)),
+            pl.BlockSpec((SEGMENT_LENGTH, size), lambda c, g: (c, 0)),
+            pl.BlockSpec((SEGMENT_LENGTH, size), lambda c, g: (c, 0)),
+            pl.BlockSpec((SEGMENT_LENGTH, group * width), lambda c, g: (c, g)),
+            pl.BlockSpec((1, 1, SEGMENT_LENGTH, group), lambda c, g: (c, g, 0, 0)),
+            pl.BlockSpec((1, 1, group, SEGMENT_LENGTH), lambda c, g: (c, g, 0, 0)),
+            pl.BlockSpec((1, 1, group, SEGMENT_LENGTH), lambda c, g: (c, g, 0, 0)),
+        ],
+        out_specs=pl.BlockSpec((SEGMENT_LENGTH, group * width), lambda c, g: (c, g)),
         out_shape=jax.ShapeDtypeStruct((rows, heads * width), jnp.float32),
-        scratch_shapes=[pltpu.VMEM((SEGMENT_LENGTH, SEGMENT_LENGTH), jnp.float32)],
         cost_estimate=pl.CostEstimate(
             flops=2 * rows * SEGMENT_LENGTH * (heads * width + size),
             bytes_accessed=rows * heads * width * 6,
             transcendentals=rows * SEGMENT_LENGTH * heads,
         ),
-    )(skip_gain, c_part, b_part, xconv, cum_col, cum_row, step_row)
-
-
-def gate_terms(partial, c_part, state_enter, ecum_col, gate_in, spans, heads, width):
+    )(
+        skip_gain,
+        c_part,
+        b_part,
+        xconv,
+        columns_by_group(cum_heads, spans, heads),
+        by_group(cum_heads, spans, heads),
+        by_group(step_heads, spans, heads),
+    )
+
+
+def gate_terms(partial, c_part, state_enter, ecum, gate_in, spans, heads, width):
     rows = partial.shape[0]
     size = c_part.shape[1]
+    group = HEAD_GROUP
     return pl.pallas_call(
         gate_kernel,
-        grid=(spans, heads),
+        grid=(spans, heads // group),
         in_specs=[
-            pl.BlockSpec((SEGMENT_LENGTH, width), lambda c, h: (c, h)),
-            pl.BlockSpec((SEGMENT_LENGTH, size), lambda c, h: (c, 0)),
-            pl.BlockSpec((1, 1, size, width), lambda c, h: (c, h, 0, 0)),
-            pl.BlockSpec((1, 1, SEGMENT_LENGTH, 1), lambda c, h: (c, h, 0, 0)),
-            pl.BlockSpec((SEGMENT_LENGTH, width), lambda c, h: (c, h)),
+            pl.BlockSpec((SEGMENT_LENGTH, group * width), lambda c, g: (c, g)),
+            pl.BlockSpec((SEGMENT_LENGTH, size), lambda c, g: (c, 0)),
+            pl.BlockSpec((1, group, size, width), lambda c, g: (c, g, 0, 0)),
+            pl.BlockSpec((1, 1, SEGMENT_LENGTH, group), lambda c, g: (c, g, 0, 0)),
+            pl.BlockSpec((SEGMENT_LENGTH, group * width), lambda c, g: (c, g)),
         ],
         out_specs=[
-            pl.BlockSpec((SEGMENT_LENGTH, width), lambda c, h: (c, h)),
-            pl.BlockSpec((SEGMENT_LENGTH, 1), lambda c, h: (c, 0)),
+            pl.BlockSpec((SEGMENT_LENGTH, group * width), lambda c, g: (c, g)),
+            pl.BlockSpec((SEGMENT_LENGTH, 1), lambda c, g: (c, 0)),
         ],
         out_shape=[
             jax.ShapeDtypeStruct((rows, heads * width), jnp.float32),
@@ -173,7 +204,7 @@
             bytes_accessed=rows * heads * width * 10,
             transcendentals=rows * heads * width,
         ),
-    )(partial, c_part, state_enter, ecum_col, gate_in)
+    )(partial, c_part, state_enter, columns_by_group(ecum, spans, heads), gate_in)
 
 
 def local(
@@ -213,17 +244,14 @@
     step_heads = jnp.transpose(step_three, (0, 2, 1))
     last_cum = cum_heads[:, :, -1]
     to_end = jnp.exp(last_cum[:, :, None] - cum_heads) * step_heads
-    block_state = block_states(
-        xconv, b_t, to_end[..., None], span_count, head_count, head_size
-    )
+    block_state = block_states(xconv, b_t, to_end, span_count, head_count, head_size)
     partial = intra_terms(
         skip_gain,
         c_part,
         b_part,
         xconv,
-        cum_heads[..., None],
-        cum_heads[:, :, None, :],
-        step_heads[:, :, None, :],
+        cum_heads,
+        step_heads,
         span_count,
         head_count,
         head_size,
@@ -250,7 +278,7 @@
         partial,
         c_part,
         state_enter,
-        jnp.exp(cum_heads)[..., None],
+        jnp.exp(cum_heads),
         gate_in,
         span_count,
         head_count,

time: 432 us -> 239 us (0.55); the launches traced: 425 us -> 237 us
  Pallas kernels: 252 us -> 64 us
  local copies, waits for them, and re-layouts: 36 us -> 16 us
  waiting for transfers between devices: 0.01 us -> 19.9 us
    pallas_call x3, Pallas kernels: 252 us -> 64 us  [the longest x1 27.5 us: gate_terms(): pl.pallas_call(gate_kernel, grid=(spans, heads // group), in_specs=[pl.Bl...]
    all_to_all x1, waiting for transfers between devices: 0.01 us -> 19.9 us  [scan_states(): back = lax.all_to_all(jnp.stack(entries, axis=0), axis, 0, 0, tiled=True)]
    broadcast_in_dim x2 -> x0, local copies, waits for them, and re-layouts: 9.33 us -> none  [the longest x1 8.58 us: local(): to_end[..., None]]
    another operation x5, local copies, waits for them, and re-layouts: 8.82 us -> 2.19 us
    exp x2, local copies, waits for them, and re-layouts: 8.59 us -> 1.98 us  [local(): jnp.exp(cum_heads)]
  transfers between devices with their start and end apart: 4 -> 4, of which waited for: 0 -> 1; matrix products, arithmetic and copies ran while one was open for 8% -> 7% of each run, Pallas kernels for 20% -> 8%
where the time goes in v3:
time: 239 us; the launch traced here: 237 us
  Pallas kernels  64 us (27%)
  blocking collectives  63.2 us (26%)
  other arithmetic  49.7 us (21%)
  starting transfers between devices  23.3 us (10%)
  waiting for transfers between devices  19.9 us (8%)
  local copies, waits for them, and re-layouts  16 us (7%)
    all_gather x1, blocking collectives, scan_states(): decays = lax.all_gather(factor, axis)  50.3 us
    pallas_call x1, Pallas kernels, gate_terms(): pl.pallas_call(gate_kernel, grid=(spans, heads // group), in_specs=[pl.Bl...  27.5 us
    pallas_call x1, Pallas kernels, intra_terms(): pl.pallas_call(intra_kernel, grid=(spans, heads // group), in_specs=[pl.B...  20.1 us
    all_to_all x1, waiting for transfers between devices, scan_states(): back = lax.all_to_all(jnp.stack(entries, axis=0), axis, 0, 0, tiled=True)  19.9 us
    convert_element_type x2, other arithmetic, conv_silu(): return jax.nn.silu(accum).astype(jnp.bfloat16)  19 us
    pallas_call x1, Pallas kernels, block_states(): pl.pallas_call(state_kernel, grid=(spans, heads // group), in_specs=[pl.B...  16.5 us
    all_to_all x1, starting transfers between devices, scan_states(): back = lax.all_to_all(jnp.stack(entries, axis=0), axis, 0, 0, tiled=True)  10.2 us
    convert_element_type x1, other arithmetic, local(): return normed.astype(jnp.bfloat16)  9.96 us
  transfers between devices with their start and end apart: 4, of which 1 were waited for; matrix products, arithmetic and copies ran while one was open for 7% of the time, Pallas kernels for 8%

profile of v3, /device:TPU:0, one launch (start us, length us, event | category | flops | bytes accessed | tf_op | source)
XLA Modules:
  0.0 237.0 jit_solution(689583430810704432)
XLA Ops:
  1.5 4.9 %collective-permute-start = (bf16[3,64]{0,1:T(8,128)(2,1)S(1)}, bf16[3,64]{0,1:T(8,128)(2,1)S(1)}, u32[]{:S(2)}, u32[]{:S(2)}) collective-permute-start(bf16[3,64]{0,1:T(8,128)(2,1)S(1)} %constant_dynamic-slice_fusion.1), channel_id=1, source_target_pairs={{0,4},{4,8},{8,12},{12,16},{16,20},{20,24},{24,28},{1,5},{5,9},{9,... | collective-permute-start | bytes 1160 | tf_op jit(solution)/shard_map/ppermute | solution.py:18
  7.2 3.5 %collective-permute-start.1 = (bf16[3,4096]{1,0:T(4,128)(2,1)S(1)}, bf16[3,4096]{1,0:T(4,128)(2,1)S(1)}, u32[]{:S(2)}, u32[]{:S(2)}) collective-permute-start(bf16[3,4096]{1,0:T(4,128)(2,1)S(1)} %constant_dynamic-slice_fusion), channel_id=1, source_target_pairs={{0,4},{4,8},{8,12},{12,16},{16,20},{20,24},{24,28},{1,5},{5,9},{9,... | collective-permute-start | bytes 73736 | tf_op jit(solution)/shard_map/ppermute | solution.py:18
  11.3 1.1 fusion.10
  12.7 2.3 reduce-window.6
  15.8 1.9 copy.100
  18.1 7.2 %all_gather.7 = bf16[1024,256]{0,1:T(8,128)(2,1)S(1)} all-gather(bf16[1024,64]{0,1:T(8,128)(2,1)S(1)} %multiply_convert_fusion.2), channel_id=1, replica_groups=mesh['seq'=8,'ch'=4] {'ch'}, dimensions={1}, use_global_device_ids=true | all-gather | bytes 655360 | tf_op jit(solution)/shard_map/all_gather | solution.py:234
  25.5 0.9 copy.99
  26.4 18.8 %multiply_convert_fusion.1.x_ref = bf16[1024,4096]{1,0:T(8,128)(2,1)} fusion(bf16[1024,4096]{1,0:T(8,128)(2,1)} %param.11, bf16[3,4096]{1,0:T(4,128)(2,1)S(1)} %collective-permute-done.1, f32[4096]{0:T(1024)S(1)} %bitcast.119, f32[4096]{0:T(1024)S(1)} %bitcast.120, f32[4096]{0:T(1024)S(1)} %bitcast.118, f32[4096]{0:T(1024)S(1)} %bitcast.117), kind=kLoop, calls=%fused_computation.1 | loop fusion | flops 104857600 | bytes 16867328 | tf_op jit(solution)/shard_map/convert_element_type | solution.py:46
  45.1 16.5 %shard_map.110 = f32[4,32,128,128]{3,2,1,0:T(8,128)} custom-call(bf16[1024,4096]{1,0:T(8,128)(2,1)} %multiply_convert_fusion.1.x_ref, bf16[4,128,256]{2,1,0:T(8,128)(2,1)} %bitcast.115, f32[4,4,256,8]{3,2,1,0:T(8,128)} %bitcast.105), custom_call_target="tpu_custom_call" | custom-call | flops 1073741824 | bytes 16777216 | tf_op jit(solution)/shard_map/pallas_call | solution.py:128
  61.6 4.0 %fusion.22 = (f32[1,32,128,128]{3,2,1,0:T(8,128)S(1)}, f32[1,32,128,128]{3,2,1,0:T(8,128)S(1)}, f32[1,32,128,128]{3,2,1,0:T(8,128)S(1)}, f32[1,32,128,128]{3,2,1,0:T(8,128)S(1)}) fusion(f32[4,32,128,128]{3,2,1,0:T(8,128)} %shard_map.110), kind=kLoop, calls=%fused_computation.84 | loop fusion | bytes 16777216 | tf_op jit(solution)/shard_map/slice | solution.py:267
  65.7 2.1 fusion.2
  67.7 4.8 %all-to-all-start = ((f32[8,32,16,128]{3,2,1,0:T(8,128)}), f32[8,32,16,128]{3,2,1,0:T(8,128)S(1)}, u32[]{:S(2)}, u32[]{:S(2)}) async-start(f32[8,32,16,128]{3,2,1,0:T(8,128)} %fusion.2), calls=%async_computation | async-start | bytes 4194304 | tf_op jit(solution)/shard_map/all_to_all | solution.py:26
  72.5 50.3 %all-gather = f32[8,1,32]{2,1,0:T(1,128)S(1)} all-gather(f32[1,1,32]{2,1,0:T(1,128)S(1)} %get-tuple-element.39), channel_id=1, replica_groups=mesh['seq'=8,'ch'=4] {'seq'}, dimensions={0}, use_global_device_ids=true | all-gather | bytes 1152 | tf_op jit(solution)/shard_map/all_gather | solution.py:27
  129.3 10.2 %all-to-all-start.1 = ((f32[8,32,16,128]{3,2,1,0:T(8,128)}), f32[8,32,16,128]{3,2,1,0:T(8,128)S(1)}, u32[]{:S(2)}, u32[]{:S(2)}) async-start(f32[8,32,16,128]{3,2,1,0:T(8,128)} %fusion.6), calls=%async_computation.1 | async-start | bytes 4194304 | tf_op jit(solution)/shard_map/all_to_all | solution.py:33
  140.6 2.0 copy.96
  142.5 2.0 copy.106
  145.3 20.1 %shard_map.109.part_ref = f32[1024,4096]{1,0:T(8,128)} custom-call(f32[32]{0:T(128)} %skip_ref.1, bf16[1024,128]{1,0:T(8,128)(2,1)} %copy.109.c_ref, bf16[1024,128]{1,0:T(8,128)(2,1)} %copy-done, bf16[1024,4096]{1,0:T(8,128)(2,1)} %multiply_convert_fusion.1.x_ref, f32[4,4,256,8]{3,2,1,0:T(8,128)} %bitcast.106, f32[4,4,8,256]{3,2,1,0:T(8,128)} %copy-done.1, ...), custom_call_target="tpu_custom_call" | custom-call | flops 2214592512 | bytes 25165824 | tf_op jit(solution)/shard_map/pallas_call | solution.py:150
  165.4 19.9 %all-to-all-done.1 = f32[8,32,16,128]{3,2,1,0:T(8,128)S(1)} async-done(((f32[8,32,16,128]{3,2,1,0:T(8,128)}), f32[8,32,16,128]{3,2,1,0:T(8,128)S(1)}, u32[]{:S(2)}, u32[]{:S(2)}) %all-to-all-start.1) | async-done | bytes 2097184 | tf_op jit(solution)/shard_map/all_to_all | solution.py:33
  185.5 3.4 %multiply_add_fusion.1 = (f32[1,32,128,128]{3,2,1,0:T(8,128)S(1)}, f32[1,32,128,128]{3,2,1,0:T(8,128)S(1)}, f32[1,32,128,128]{3,2,1,0:T(8,128)S(1)}) fusion(f32[1,32,128,128]{3,2,1,0:T(8,128)S(1)} %bitcast.102, f32[32]{0:T(128)S(1)} %get-tuple-element.10, f32[4,32,128,128]{3,2,1,0:T(8,128)} %shard_map.110, f32[32]{0:T(128)S(1)} %get-tuple-element.42, ...), kind=kLoop, calls=%fused_computation.17 | loop fusion | flops 5767168 | bytes 14680832 | tf_op jit(solution)/shard_map/add | solution.py:272
  188.9 3.7 %pad_maximum_fusion.1.state_ref = f32[4,32,128,128]{3,2,1,0:T(8,128)} fusion(f32[1,32,128,128]{3,2,1,0:T(8,128)S(1)} %get-tuple-element.18, f32[1,32,128,128]{3,2,1,0:T(8,128)S(1)} %get-tuple-element.17, f32[1,32,128,128]{3,2,1,0:T(8,128)S(1)} %get-tuple-element.19, f32[1,32,128,128]{3,2,1,0:T(8,128)S(1)} %bitcast.103), kind=kLoop, calls=%fused_computation.7 | loop fusion | flops 6291456 | bytes 16777216 | tf_op jit(solution)/shard_map/stack | solution.py:270
  192.6 27.5 %shard_map.111 = (f32[1024,4096]{1,0:T(8,128)}, f32[1024,1]{1,0:T(8,128)}) custom-call(f32[1024,4096]{1,0:T(8,128)} %shard_map.109.part_ref, bf16[1024,128]{1,0:T(8,128)(2,1)} %copy.109.c_ref, f32[4,32,128,128]{3,2,1,0:T(8,128)} %pad_maximum_fusion.1.state_ref, f32[4,4,256,8]{3,2,1,0:T(8,128)} %bitcast.104, bf16[1024,4096]{1,0:T(8,128)(2,1)} %z_ref.1), custom_call_target="tpu_custom_call" | custom-call | flops 3221225472 | bytes 41943040 | tf_op jit(solution)/shard_map/pallas_call | solution.py:184
  220.1 1.2 reduce.1
  221.3 5.7 %psum.7 = f32[1024]{0:T(1024)S(1)} all-reduce(f32[1024]{0:T(1024)S(1)} %reduce.1), channel_id=1, replica_groups=mesh['seq'=8,'ch'=4] {'ch'}, use_global_device_ids=true, to_apply=%region_2.3 | all-reduce | flops 1024 | bytes 8192 | tf_op jit(solution)/shard_map/psum | solution.py:287
  227.0 10.0 %multiply_convert_fusion = bf16[1024,4096]{1,0:T(8,128)(2,1)} fusion(f32[1024,4096]{1,0:T(8,128)} %get-tuple-element.7, f32[1024]{0:T(1024)S(1)} %fusion.17, f32[4096]{0:T(1024)S(1)} %copy-done.4, f32[1024]{0:T(1024)S(1)} %add_rsqrt_fusion), kind=kLoop, calls=%fused_computation | loop fusion | flops 16777216 | bytes 25190400 | tf_op jit(solution)/shard_map/convert_element_type | solution.py:290
  (56 shorter events, 12.4 us)
Async XLA Ops:
  0.0 15.6 %copy-start.3 = (bf16[4,4096]{1,0:T(4,128)(2,1)S(1)}, bf16[4,4096]{1,0:T(4,128)(2,1)}, u32[]{:S(2)}) copy-start(bf16[4,4096]{1,0:T(4,128)(2,1)} %param.18) | copy-start | bytes 98308
  0.0 15.8 %copy-start.5 = (bf16[4,64]{1,0:T(4,128)(2,1)S(1)}, bf16[4,64]{1,0:T(4,128)(2,1)}, u32[]{:S(2)}) copy-start(bf16[4,64]{1,0:T(4,128)(2,1)} %param.19) | copy-start | bytes 1540
  1.5 16.3 %collective-permute-start = (bf16[3,64]{0,1:T(8,128)(2,1)S(1)}, bf16[3,64]{0,1:T(8,128)(2,1)S(1)}, u32[]{:S(2)}, u32[]{:S(2)}) collective-permute-start(bf16[3,64]{0,1:T(8,128)(2,1)S(1)} %constant_dynamic-slice_fusion.1), channel_id=1, source_target_pairs={{0,4},{4,8},{8,12},{12,16},{16,20},{20,24},{24,28},{1,5},{5,9},{9,... | collective-permute-start | bytes 1160 | tf_op jit(solution)/shard_map/ppermute | solution.py:18
  7.2 19.2 %collective-permute-start.1 = (bf16[3,4096]{1,0:T(4,128)(2,1)S(1)}, bf16[3,4096]{1,0:T(4,128)(2,1)S(1)}, u32[]{:S(2)}, u32[]{:S(2)}) collective-permute-start(bf16[3,4096]{1,0:T(4,128)(2,1)S(1)} %constant_dynamic-slice_fusion), channel_id=1, source_target_pairs={{0,4},{4,8},{8,12},{12,16},{16,20},{20,24},{24,28},{1,5},{5,9},{9,... | collective-permute-start | bytes 73736 | tf_op jit(solution)/shard_map/ppermute | solution.py:18
  12.7 5.1 %copy-start.2 = (bf16[1024,64]{0,1:T(8,128)(2,1)S(1)}, bf16[1024,64]{0,1:T(8,128)(2,1)}, u32[]{:S(2)}) copy-start(bf16[1024,64]{0,1:T(8,128)(2,1)} %param.13) | copy-start | bytes 393220
  25.5 19.6 %copy-start = (bf16[1024,128]{1,0:T(8,128)(2,1)}, bf16[1024,128]{1,0:T(8,128)(2,1)S(1)}, u32[]{:S(2)}) copy-start(bf16[1024,128]{1,0:T(8,128)(2,1)S(1)} %copy.110.b_ref) | copy-start | bytes 786436
  67.7 55.8 %all-to-all-start = ((f32[8,32,16,128]{3,2,1,0:T(8,128)}), f32[8,32,16,128]{3,2,1,0:T(8,128)S(1)}, u32[]{:S(2)}, u32[]{:S(2)}) async-start(f32[8,32,16,128]{3,2,1,0:T(8,128)} %fusion.2), calls=%async_computation | async-start | bytes 4194304 | tf_op jit(solution)/shard_map/all_to_all | solution.py:26
  129.3 56.0 %all-to-all-start.1 = ((f32[8,32,16,128]{3,2,1,0:T(8,128)}), f32[8,32,16,128]{3,2,1,0:T(8,128)S(1)}, u32[]{:S(2)}, u32[]{:S(2)}) async-start(f32[8,32,16,128]{3,2,1,0:T(8,128)} %fusion.6), calls=%async_computation.1 | async-start | bytes 4194304 | tf_op jit(solution)/shard_map/all_to_all | solution.py:33
  140.5 4.0 %copy-start.1 = (f32[4,4,8,256]{3,2,1,0:T(8,128)}, f32[4,4,8,256]{3,2,1,0:T(8,128)S(1)}, u32[]{:S(2)}) copy-start(f32[4,4,8,256]{3,2,1,0:T(8,128)S(1)} %reduce_window_sum.21.cumr_ref) | copy-start | bytes 393220
  192.6 34.4 %copy-start.4 = (f32[4096]{0:T(1024)S(1)}, f32[4096]{0:T(1024)}, u32[]{:S(2)}) copy-start(f32[4096]{0:T(1024)} %param.20) | copy-start | bytes 49156

commit v4 on v3

--- a/solution.py
+++ b/solution.py
@@ -49,11 +49,26 @@
 HEAD_GROUP = 8
 
 
-def state_kernel(x_ref, bt_ref, toend_ref, out_ref):
+def state_kernel(x_ref, halo_ref, taps_ref, bt_ref, toend_ref, out_ref, conv_ref):
     width = out_ref.shape[-1]
+    taps = taps_ref[...].astype(jnp.float32)
+    kernel_taps = taps.shape[0]
+    signal = x_ref[...].astype(jnp.float32)
+    edge = halo_ref[0].astype(jnp.float32)
+    lead = edge.shape[0]
+    stacked = jnp.concatenate([edge, signal[:lead]], axis=0)
+    accum = jnp.zeros(signal.shape, jnp.float32)
+    head = jnp.zeros((lead, signal.shape[1]), jnp.float32)
+    for offset in range(kernel_taps):
+        shift = kernel_taps - 1 - offset
+        moved = signal if shift == 0 else pltpu.roll(signal, shift, 0)
+        accum = accum + taps[offset : offset + 1] * moved
+        head = head + taps[offset : offset + 1] * stacked[lead - shift : 2 * lead - shift]
+    conv_ref[...] = (accum / (1.0 + jnp.exp(-accum))).astype(jnp.bfloat16)
+    conv_ref[:lead, :] = (head / (1.0 + jnp.exp(-head))).astype(jnp.bfloat16)
     bt = bt_ref[0]
     for j in range(out_ref.shape[1]):
-        x = x_ref[:, j * width : (j + 1) * width].astype(jnp.float32)
+        x = conv_ref[:, j * width : (j + 1) * width].astype(jnp.float32)
         xw = (x * toend_ref[0, 0, :, j : j + 1]).astype(jnp.bfloat16)
         out_ref[0, j] = jnp.dot(bt, xw, preferred_element_type=jnp.float32)
 
@@ -121,26 +136,36 @@
     return by_group(values, spans, heads).transpose(0, 1, 3, 2)
 
 
-def block_states(xconv, b_t, to_end, spans, heads, width):
-    rows = xconv.shape[0]
+def block_states(xin, halo, conv_x, b_t, to_end, spans, heads, width):
+    rows = xin.shape[0]
     size = b_t.shape[1]
     group = HEAD_GROUP
+    lead = halo.shape[1]
+    kernel_taps = conv_x.shape[0]
     return pl.pallas_call(
         state_kernel,
         grid=(spans, heads // group),
         in_specs=[
             pl.BlockSpec((SEGMENT_LENGTH, group * width), lambda c, g: (c, g)),
+            pl.BlockSpec((1, lead, group * width), lambda c, g: (c, 0, g)),
+            pl.BlockSpec((kernel_taps, group * width), lambda c, g: (0, g)),
             pl.BlockSpec((1, size, SEGMENT_LENGTH), lambda c, g: (c, 0, 0)),
             pl.BlockSpec((1, 1, SEGMENT_LENGTH, group), lambda c, g: (c, g, 0, 0)),
         ],
-        out_specs=pl.BlockSpec((1, group, size, width), lambda c, g: (c, g, 0, 0)),
-        out_shape=jax.ShapeDtypeStruct((spans, heads, size, width), jnp.float32),
+        out_specs=[
+            pl.BlockSpec((1, group, size, width), lambda c, g: (c, g, 0, 0)),
+            pl.BlockSpec((SEGMENT_LENGTH, group * width), lambda c, g: (c, g)),
+        ],
+        out_shape=[
+            jax.ShapeDtypeStruct((spans, heads, size, width), jnp.float32),
+            jax.ShapeDtypeStruct((rows, heads * width), jnp.bfloat16),
+        ],
         cost_estimate=pl.CostEstimate(
             flops=2 * rows * heads * width * size,
-            bytes_accessed=rows * heads * width * 2 + spans * heads * size * width * 4,
-            transcendentals=0,
+            bytes_accessed=rows * heads * width * 4 + spans * heads * size * width * 4,
+            transcendentals=rows * heads * width,
         ),
-    )(xconv, b_t, columns_by_group(to_end, spans, heads))
+    )(xin, halo, conv_x, b_t, columns_by_group(to_end, spans, heads))
 
 
 def intra_terms(skip_gain, c_part, b_part, xconv, cum_heads, step_heads, spans, heads, width):
@@ -229,7 +254,12 @@
     tail_x = lax.dynamic_slice_in_dim(xin, live_rows - (kernel_taps - 1), kernel_taps - 1, 0)
     tail_bc = lax.dynamic_slice_in_dim(bc_proj, live_rows - (kernel_taps - 1), kernel_taps - 1, 0)
     prev_x, prev_bc = passed_along((tail_x, tail_bc), "seq", 1)
-    xconv = conv_silu(xin, prev_x, conv_x)
+    lead = 8
+    edges = jnp.concatenate(
+        [prev_x[None], xin.reshape(span_count, SEGMENT_LENGTH, channels)[:-1, -(kernel_taps - 1) :]],
+        axis=0,
+    )
+    halo = jnp.pad(edges, ((0, 0), (lead - (kernel_taps - 1), 0), (0, 0)))
     bc_local = conv_silu(bc_proj, prev_bc, conv_bc)
     bc_full = lax.all_gather(bc_local, "ch", axis=1, tiled=True)
     state_size = bc_full.shape[1] // 2
@@ -244,7 +274,9 @@
     step_heads = jnp.transpose(step_three, (0, 2, 1))
     last_cum = cum_heads[:, :, -1]
     to_end = jnp.exp(last_cum[:, :, None] - cum_heads) * step_heads
-    block_state = block_states(xconv, b_t, to_end, span_count, head_count, head_size)
+    block_state, xconv = block_states(
+        xin, halo, conv_x, b_t, to_end, span_count, head_count, head_size
+    )
     partial = intra_terms(
         skip_gain,
         c_part,

time: 239 us -> 228 us (0.954)
  other arithmetic: 49.7 us -> 31.7 us
  Pallas kernels: 64 us -> 69.6 us
    convert_element_type x2 -> x1, other arithmetic: 19 us -> 0.28 us  [conv_silu(): return jax.nn.silu(accum).astype(jnp.bfloat16)]
    pallas_call x1, Pallas kernels: 16.5 us -> 22 us  [block_states(): pl.pallas_call(state_kernel, grid=(spans, heads // group), in_specs=[pl.B...]
  transfers between devices with their start and end apart: 4 -> 4, of which waited for: 1 -> 1; matrix products, arithmetic and copies ran while one was open for 7% -> 7% of each run, Pallas kernels for 8% -> 9%
where the time goes in v4:
time: 228 us; the launch traced here: 226 us
  Pallas kernels  69.6 us (31%)
  blocking collectives  63.2 us (28%)
  other arithmetic  31.7 us (14%)
  starting transfers between devices  23.3 us (10%)
  waiting for transfers between devices  19.9 us (9%)
  local copies, waits for them, and re-layouts  17 us (7%)
    all_gather x1, blocking collectives, scan_states(): decays = lax.all_gather(factor, axis)  50.3 us
    pallas_call x1, Pallas kernels, gate_terms(): pl.pallas_call(gate_kernel, grid=(spans, heads // group), in_specs=[pl.Bl...  27.6 us
    pallas_call x1, Pallas kernels, block_states(): pl.pallas_call(state_kernel, grid=(spans, heads // group), in_specs=[pl.B...  22 us
    pallas_call x1, Pallas kernels, intra_terms(): pl.pallas_call(intra_kernel, grid=(spans, heads // group), in_specs=[pl.B...  20.1 us
    all_to_all x1, waiting for transfers between devices, scan_states(): back = lax.all_to_all(jnp.stack(entries, axis=0), axis, 0, 0, tiled=True)  19.9 us
    all_to_all x1, starting transfers between devices, scan_states(): back = lax.all_to_all(jnp.stack(entries, axis=0), axis, 0, 0, tiled=True)  10.2 us
    convert_element_type x1, other arithmetic, local(): return normed.astype(jnp.bfloat16)  9.96 us
    ppermute x2, starting transfers between devices, passed_along(): return lax.ppermute(block, axis, route)  8.32 us
  transfers between devices with their start and end apart: 4, of which 1 were waited for; matrix products, arithmetic and copies ran while one was open for 7% of the time, Pallas kernels for 9%

profile of v4, /device:TPU:0, one launch (start us, length us, event | category | flops | bytes accessed | tf_op | source)
XLA Modules:
  0.0 225.6 jit_solution(10131823030580669737)
XLA Ops:
  1.5 4.9 %collective-permute-start = (bf16[3,64]{0,1:T(8,128)(2,1)S(1)}, bf16[3,64]{0,1:T(8,128)(2,1)S(1)}, u32[]{:S(2)}, u32[]{:S(2)}) collective-permute-start(bf16[3,64]{0,1:T(8,128)(2,1)S(1)} %constant_dynamic-slice_fusion.1), channel_id=1, source_target_pairs={{0,4},{4,8},{8,12},{12,16},{16,20},{20,24},{24,28},{1,5},{5,9},{9,... | collective-permute-start | bytes 1160 | tf_op jit(solution)/shard_map/ppermute | solution.py:18
  6.3 0.9 constant_dynamic-slice_fusion
  7.2 3.5 %collective-permute-start.1 = (bf16[3,4096]{1,0:T(4,128)(2,1)S(1)}, bf16[3,4096]{1,0:T(4,128)(2,1)S(1)}, u32[]{:S(2)}, u32[]{:S(2)}) collective-permute-start(bf16[3,4096]{1,0:T(4,128)(2,1)S(1)} %constant_dynamic-slice_fusion), channel_id=1, source_target_pairs={{0,4},{4,8},{8,12},{12,16},{16,20},{20,24},{24,28},{1,5},{5,9},{9,... | collective-permute-start | bytes 73736 | tf_op jit(solution)/shard_map/ppermute | solution.py:18
  11.3 1.1 fusion.11
  12.7 2.3 %reduce-window.6 = f32[4,32,2,128]{3,1,2,0:T(8,128)S(1)} reduce-window(f32[4,32,2,128]{3,1,2,0:T(8,128)S(1)} %copy.73, f32[]{:T(128)} %constant.27.clone.1), window={size=1x1x1x128 pad=0_0x0_0x0_0x127_0}, to_apply=%region_0.1 | reduce-window | flops 4161536 | bytes 262148 | tf_op jit(solution)/shard_map/reduce-window
  15.8 1.0 slice.157
  16.8 2.0 copy.78
  19.0 7.2 %all_gather.7 = bf16[1024,256]{0,1:T(8,128)(2,1)S(1)} all-gather(bf16[1024,64]{0,1:T(8,128)(2,1)S(1)} %multiply_convert_fusion.1), channel_id=1, replica_groups=mesh['seq'=8,'ch'=4] {'ch'}, dimensions={1}, use_global_device_ids=true | all-gather | bytes 655360 | tf_op jit(solution)/shard_map/all_gather | solution.py:264
  28.1 22.0 %shard_map.109 = (f32[4,32,128,128]{3,2,1,0:T(8,128)}, bf16[1024,4096]{1,0:T(8,128)(2,1)}) custom-call(bf16[1024,4096]{1,0:T(8,128)(2,1)} %x_ref.1, bf16[4,8,4096]{2,1,0:T(8,128)(2,1)} %fusion.6.halo_ref, bf16[4,4096]{1,0:T(4,128)(2,1)} %taps_ref.1, bf16[4,128,256]{2,1,0:T(8,128)(2,1)} %bitcast.114, f32[4,4,256,8]{3,2,1,0:T(8,128)} %bitcast.106), custom_call_target="tpu_custom_call" | custom-call | flops 1073741824 | bytes 25165824 | tf_op jit(solution)/shard_map/pallas_call | solution.py:145
  50.1 4.1 %fusion.23 = (f32[1,32,128,128]{3,2,1,0:T(8,128)S(1)}, f32[1,32,128,128]{3,2,1,0:T(8,128)S(1)}, f32[1,32,128,128]{3,2,1,0:T(8,128)S(1)}, f32[1,32,128,128]{3,2,1,0:T(8,128)S(1)}) fusion(f32[4,32,128,128]{3,2,1,0:T(8,128)} %get-tuple-element.10), kind=kLoop, calls=%fused_computation.78 | loop fusion | bytes 16777216 | tf_op jit(solution)/shard_map/slice | solution.py:299
  54.2 2.1 fusion
  56.3 4.8 %all-to-all-start = ((f32[8,32,16,128]{3,2,1,0:T(8,128)}), f32[8,32,16,128]{3,2,1,0:T(8,128)S(1)}, u32[]{:S(2)}, u32[]{:S(2)}) async-start(f32[8,32,16,128]{3,2,1,0:T(8,128)} %fusion), calls=%async_computation | async-start | bytes 4194304 | tf_op jit(solution)/shard_map/all_to_all | solution.py:26
  61.1 50.3 %all-gather = f32[8,1,32]{2,1,0:T(1,128)S(1)} all-gather(f32[1,1,32]{2,1,0:T(1,128)S(1)} %get-tuple-element.39), channel_id=1, replica_groups=mesh['seq'=8,'ch'=4] {'seq'}, dimensions={0}, use_global_device_ids=true | all-gather | bytes 1152 | tf_op jit(solution)/shard_map/all_gather | solution.py:27
  117.8 10.2 %all-to-all-start.1 = ((f32[8,32,16,128]{3,2,1,0:T(8,128)}), f32[8,32,16,128]{3,2,1,0:T(8,128)S(1)}, u32[]{:S(2)}, u32[]{:S(2)}) async-start(f32[8,32,16,128]{3,2,1,0:T(8,128)} %fusion.7), calls=%async_computation.1 | async-start | bytes 4194304 | tf_op jit(solution)/shard_map/all_to_all | solution.py:33
  129.1 2.0 copy.80
  131.1 2.0 copy.86
  133.9 20.1 %shard_map.110.part_ref = f32[1024,4096]{1,0:T(8,128)} custom-call(f32[32]{0:T(128)} %skip_ref.1, bf16[1024,128]{1,0:T(8,128)(2,1)} %copy.89.c_ref, bf16[1024,128]{1,0:T(8,128)(2,1)} %copy-done, bf16[1024,4096]{1,0:T(8,128)(2,1)} %get-tuple-element.9.x_ref, f32[4,4,256,8]{3,2,1,0:T(8,128)} %bitcast.104, f32[4,4,8,256]{3,2,1,0:T(8,128)} %copy-done.1, ...), custom_call_target="tpu_custom_call" | custom-call | flops 2214592512 | bytes 25165824 | tf_op jit(solution)/shard_map/pallas_call | solution.py:175
  153.9 19.9 %all-to-all-done.1 = f32[8,32,16,128]{3,2,1,0:T(8,128)S(1)} async-done(((f32[8,32,16,128]{3,2,1,0:T(8,128)}), f32[8,32,16,128]{3,2,1,0:T(8,128)S(1)}, u32[]{:S(2)}, u32[]{:S(2)}) %all-to-all-start.1) | async-done | bytes 2097184 | tf_op jit(solution)/shard_map/all_to_all | solution.py:33
  174.1 3.4 %multiply_add_fusion.1 = (f32[1,32,128,128]{3,2,1,0:T(8,128)S(1)}, f32[1,32,128,128]{3,2,1,0:T(8,128)S(1)}, f32[1,32,128,128]{3,2,1,0:T(8,128)S(1)}) fusion(f32[1,32,128,128]{3,2,1,0:T(8,128)S(1)} %bitcast.100, f32[32]{0:T(128)S(1)} %get-tuple-element.14, f32[4,32,128,128]{3,2,1,0:T(8,128)} %get-tuple-element.10, f32[32]{0:T(128)S(1)} %get-tuple-element.42, ...), kind=kLoop, calls=%fused_computation.11 | loop fusion | flops 5767168 | bytes 14680832 | tf_op jit(solution)/shard_map/add | solution.py:304
  177.5 3.7 %pad_maximum_fusion.state_ref = f32[4,32,128,128]{3,2,1,0:T(8,128)} fusion(f32[1,32,128,128]{3,2,1,0:T(8,128)S(1)} %get-tuple-element.22, f32[1,32,128,128]{3,2,1,0:T(8,128)S(1)} %get-tuple-element.21, f32[1,32,128,128]{3,2,1,0:T(8,128)S(1)} %get-tuple-element.23, f32[1,32,128,128]{3,2,1,0:T(8,128)S(1)} %bitcast.101), kind=kLoop, calls=%fused_computation.1 | loop fusion | flops 6291456 | bytes 16777216 | tf_op jit(solution)/shard_map/stack | solution.py:302
  181.2 27.6 %shard_map.111 = (f32[1024,4096]{1,0:T(8,128)}, f32[1024,1]{1,0:T(8,128)}) custom-call(f32[1024,4096]{1,0:T(8,128)} %shard_map.110.part_ref, bf16[1024,128]{1,0:T(8,128)(2,1)} %copy.89.c_ref, f32[4,32,128,128]{3,2,1,0:T(8,128)} %pad_maximum_fusion.state_ref, f32[4,4,256,8]{3,2,1,0:T(8,128)} %bitcast.103, bf16[1024,4096]{1,0:T(8,128)(2,1)} %z_ref.1), custom_call_target="tpu_custom_call" | custom-call | flops 3221225472 | bytes 41943040 | tf_op jit(solution)/shard_map/pallas_call | solution.py:209
  208.8 1.2 reduce.1
  210.0 5.7 %psum.7 = f32[1024]{0:T(1024)S(1)} all-reduce(f32[1024]{0:T(1024)S(1)} %reduce.1), channel_id=1, replica_groups=mesh['seq'=8,'ch'=4] {'ch'}, use_global_device_ids=true, to_apply=%region_2.3 | all-reduce | flops 1024 | bytes 8192 | tf_op jit(solution)/shard_map/psum | solution.py:319
  215.7 10.0 %multiply_convert_fusion = bf16[1024,4096]{1,0:T(8,128)(2,1)} fusion(f32[1024,4096]{1,0:T(8,128)} %get-tuple-element.11, f32[1024]{0:T(1024)S(1)} %fusion.18, f32[4096]{0:T(1024)S(1)} %copy-done.3, f32[1024]{0:T(1024)S(1)} %add_rsqrt_fusion), kind=kLoop, calls=%fused_computation | loop fusion | flops 16777216 | bytes 25190400 | tf_op jit(solution)/shard_map/convert_element_type | solution.py:322
  (54 shorter events, 13.2 us)
Async XLA Ops:
  0.0 15.8 %copy-start.4 = (bf16[4,64]{1,0:T(4,128)(2,1)S(1)}, bf16[4,64]{1,0:T(4,128)(2,1)}, u32[]{:S(2)}) copy-start(bf16[4,64]{1,0:T(4,128)(2,1)} %param.19) | copy-start | bytes 1540
  1.5 17.3 %collective-permute-start = (bf16[3,64]{0,1:T(8,128)(2,1)S(1)}, bf16[3,64]{0,1:T(8,128)(2,1)S(1)}, u32[]{:S(2)}, u32[]{:S(2)}) collective-permute-start(bf16[3,64]{0,1:T(8,128)(2,1)S(1)} %constant_dynamic-slice_fusion.1), channel_id=1, source_target_pairs={{0,4},{4,8},{8,12},{12,16},{16,20},{20,24},{24,28},{1,5},{5,9},{9,... | collective-permute-start | bytes 1160 | tf_op jit(solution)/shard_map/ppermute | solution.py:18
  7.2 20.1 %collective-permute-start.1 = (bf16[3,4096]{1,0:T(4,128)(2,1)S(1)}, bf16[3,4096]{1,0:T(4,128)(2,1)S(1)}, u32[]{:S(2)}, u32[]{:S(2)}) collective-permute-start(bf16[3,4096]{1,0:T(4,128)(2,1)S(1)} %constant_dynamic-slice_fusion), channel_id=1, source_target_pairs={{0,4},{4,8},{8,12},{12,16},{16,20},{20,24},{24,28},{1,5},{5,9},{9,... | collective-permute-start | bytes 73736 | tf_op jit(solution)/shard_map/ppermute | solution.py:18
  12.7 6.0 %copy-start.2 = (bf16[1024,64]{0,1:T(8,128)(2,1)S(1)}, bf16[1024,64]{0,1:T(8,128)(2,1)}, u32[]{:S(2)}) copy-start(bf16[1024,64]{0,1:T(8,128)(2,1)} %param.13) | copy-start | bytes 393220
  26.4 23.7 %copy-start = (bf16[1024,128]{1,0:T(8,128)(2,1)}, bf16[1024,128]{1,0:T(8,128)(2,1)S(1)}, u32[]{:S(2)}) copy-start(bf16[1024,128]{1,0:T(8,128)(2,1)S(1)} %copy.90.b_ref) | copy-start | bytes 786436
  56.3 55.8 %all-to-all-start = ((f32[8,32,16,128]{3,2,1,0:T(8,128)}), f32[8,32,16,128]{3,2,1,0:T(8,128)S(1)}, u32[]{:S(2)}, u32[]{:S(2)}) async-start(f32[8,32,16,128]{3,2,1,0:T(8,128)} %fusion), calls=%async_computation | async-start | bytes 4194304 | tf_op jit(solution)/shard_map/all_to_all | solution.py:26
  117.8 56.0 %all-to-all-start.1 = ((f32[8,32,16,128]{3,2,1,0:T(8,128)}), f32[8,32,16,128]{3,2,1,0:T(8,128)S(1)}, u32[]{:S(2)}, u32[]{:S(2)}) async-start(f32[8,32,16,128]{3,2,1,0:T(8,128)} %fusion.7), calls=%async_computation.1 | async-start | bytes 4194304 | tf_op jit(solution)/shard_map/all_to_all | solution.py:33
  129.1 4.0 %copy-start.1 = (f32[4,4,8,256]{3,2,1,0:T(8,128)}, f32[4,4,8,256]{3,2,1,0:T(8,128)S(1)}, u32[]{:S(2)}) copy-start(f32[4,4,8,256]{3,2,1,0:T(8,128)S(1)} %reduce_window_sum.22.cumr_ref) | copy-start | bytes 393220
  181.2 34.5 %copy-start.3 = (f32[4096]{0:T(1024)S(1)}, f32[4096]{0:T(1024)}, u32[]{:S(2)}) copy-start(f32[4096]{0:T(1024)} %param.20) | copy-start | bytes 49156

commit v5 on v4

--- a/solution.py
+++ b/solution.py
@@ -23,13 +23,17 @@
     heads, size, width = state.shape
     piece = size // count
     parts = state.reshape(heads, count, piece, width).transpose(1, 0, 2, 3)
-    got = lax.all_to_all(parts, axis, 0, 0, tiled=True)
-    decays = lax.all_gather(factor, axis)
+    slot = jnp.zeros((piece, width), jnp.float32).at[0, :heads].set(factor)
+    payload = jnp.concatenate(
+        [parts, jnp.broadcast_to(slot, (count, 1, piece, width))], axis=1
+    )
+    got = lax.all_to_all(payload, axis, 0, 0, tiled=True)
+    decays = got[:, heads, 0, :heads]
     running = jnp.zeros((heads, piece, width), jnp.float32)
     entries = []
     for index in range(count):
         entries.append(running)
-        running = decays[index][:, None, None] * running + got[index]
+        running = decays[index][:, None, None] * running + got[index, :heads]
     back = lax.all_to_all(jnp.stack(entries, axis=0), axis, 0, 0, tiled=True)
     return back.transpose(1, 0, 2, 3).reshape(heads, size, width)
 
@@ -136,7 +140,7 @@
     return by_group(values, spans, heads).transpose(0, 1, 3, 2)
 
 
-def block_states(xin, halo, conv_x, b_t, to_end, spans, heads, width):
+def block_states(xin, halo, conv_x, b_t, to_end, spans, heads, width, offset):
     rows = xin.shape[0]
     size = b_t.shape[1]
     group = HEAD_GROUP
@@ -146,9 +150,9 @@
         state_kernel,
         grid=(spans, heads // group),
         in_specs=[
-            pl.BlockSpec((SEGMENT_LENGTH, group * width), lambda c, g: (c, g)),
-            pl.BlockSpec((1, lead, group * width), lambda c, g: (c, 0, g)),
-            pl.BlockSpec((kernel_taps, group * width), lambda c, g: (0, g)),
+            pl.BlockSpec((SEGMENT_LENGTH, group * width), lambda c, g: (c, g + offset)),
+            pl.BlockSpec((1, lead, group * width), lambda c, g: (c, 0, g + offset)),
+            pl.BlockSpec((kernel_taps, group * width), lambda c, g: (0, g + offset)),
             pl.BlockSpec((1, size, SEGMENT_LENGTH), lambda c, g: (c, 0, 0)),
             pl.BlockSpec((1, 1, SEGMENT_LENGTH, group), lambda c, g: (c, g, 0, 0)),
         ],
@@ -202,7 +206,7 @@
     )
 
 
-def gate_terms(partial, c_part, state_enter, ecum, gate_in, spans, heads, width):
+def gate_terms(partial, c_part, state_enter, ecum, gate_in, spans, heads, width, offset):
     rows = partial.shape[0]
     size = c_part.shape[1]
     group = HEAD_GROUP
@@ -214,7 +218,7 @@
             pl.BlockSpec((SEGMENT_LENGTH, size), lambda c, g: (c, 0)),
             pl.BlockSpec((1, group, size, width), lambda c, g: (c, g, 0, 0)),
             pl.BlockSpec((1, 1, SEGMENT_LENGTH, group), lambda c, g: (c, g, 0, 0)),
-            pl.BlockSpec((SEGMENT_LENGTH, group * width), lambda c, g: (c, g)),
+            pl.BlockSpec((SEGMENT_LENGTH, group * width), lambda c, g: (c, g + offset)),
         ],
         out_specs=[
             pl.BlockSpec((SEGMENT_LENGTH, group * width), lambda c, g: (c, g)),
@@ -274,48 +278,59 @@
     step_heads = jnp.transpose(step_three, (0, 2, 1))
     last_cum = cum_heads[:, :, -1]
     to_end = jnp.exp(last_cum[:, :, None] - cum_heads) * step_heads
-    block_state, xconv = block_states(
-        xin, halo, conv_x, b_t, to_end, span_count, head_count, head_size
-    )
-    partial = intra_terms(
-        skip_gain,
-        c_part,
-        b_part,
-        xconv,
-        cum_heads,
-        step_heads,
-        span_count,
-        head_count,
-        head_size,
-    )
     block_decay = jnp.exp(last_cum)
-    current = jnp.zeros((head_count, state_size, head_size), jnp.float32)
-    factor = jnp.ones((head_count,), jnp.float32)
-    local_enter = []
-    factor_list = []
-    for index in range(span_count):
-        local_enter.append(current)
-        factor_list.append(factor)
-        current = block_decay[index][:, None, None] * current + block_state[index]
-        factor = factor * block_decay[index]
-    group_state = scan_states(factor, current, "seq")
-    state_enter = jnp.stack(
-        [
-            local_enter[index] + factor_list[index][:, None, None] * group_state
-            for index in range(span_count)
-        ],
-        axis=0,
-    )
-    gated, square_part = gate_terms(
-        partial,
-        c_part,
-        state_enter,
-        jnp.exp(cum_heads),
-        gate_in,
-        span_count,
-        head_count,
-        head_size,
-    )
+    halves = 2 if head_count % (2 * HEAD_GROUP) == 0 else 1
+    part_heads = head_count // halves
+    gated_parts = []
+    square_part = None
+    for part in range(halves):
+        heads = slice(part * part_heads, (part + 1) * part_heads)
+        offset = part * part_heads // HEAD_GROUP
+        block_state, xconv = block_states(
+            xin, halo, conv_x, b_t, to_end[:, heads], span_count, part_heads, head_size, offset
+        )
+        current = jnp.zeros((part_heads, state_size, head_size), jnp.float32)
+        factor = jnp.ones((part_heads,), jnp.float32)
+        local_enter = []
+        factor_list = []
+        for index in range(span_count):
+            local_enter.append(current)
+            factor_list.append(factor)
+            current = block_decay[index, heads][:, None, None] * current + block_state[index]
+            factor = factor * block_decay[index, heads]
+        group_state = scan_states(factor, current, "seq")
+        partial = intra_terms(
+            skip_gain[heads],
+            c_part,
+            b_part,
+            xconv,
+            cum_heads[:, heads],
+            step_heads[:, heads],
+            span_count,
+            part_heads,
+            head_size,
+        )
+        state_enter = jnp.stack(
+            [
+                local_enter[index] + factor_list[index][:, None, None] * group_state
+                for index in range(span_count)
+            ],
+            axis=0,
+        )
+        gated, squares = gate_terms(
+            partial,
+            c_part,
+            state_enter,
+            jnp.exp(cum_heads[:, heads]),
+            gate_in,
+            span_count,
+            part_heads,
+            head_size,
+            offset,
+        )
+        gated_parts.append(gated)
+        square_part = squares if square_part is None else square_part + squares
+    gated = jnp.concatenate(gated_parts, axis=1)
     square_sum = lax.psum(square_part[:, 0], "ch")
     mean_sq = square_sum / INNER
     normed = gated * lax.rsqrt(mean_sq + 1e-05)[:, None] * norm_gain[None, :] * row_valid[:, None]

time: 228 us -> 231 us (1.013)
  blocking collectives: 63.2 us -> 12.9 us
  waiting for transfers between devices: 19.9 us -> 51.8 us
  local copies, waits for them, and re-layouts: 17 us -> 24.8 us
  other arithmetic: 31.7 us -> 38.9 us
  Pallas kernels: 69.6 us -> 75.6 us
    all_gather x1 -> x0, blocking collectives: 50.3 us -> none  [scan_states(): decays = lax.all_gather(factor, axis)]
    all_to_all x1 -> x2, waiting for transfers between devices: 0.01 us -> 31.1 us  [scan_states(): got = lax.all_to_all(payload, axis, 0, 0, tiled=True)]
    reshape x1 -> x6, local copies, waits for them, and re-layouts: 1.95 us -> 6.89 us  [by_group(): return values.reshape(spans, heads // HEAD_GROUP, HEAD_GROUP, -1)]
    unnamed x6 -> x12, other arithmetic: 4.94 us -> 8.97 us
    all_to_all x1 -> x2, starting transfers between devices: 4.79 us -> 8.43 us  [scan_states(): got = lax.all_to_all(payload, axis, 0, 0, tiled=True)]
    all_to_all x1 -> x2, starting transfers between devices: 10.2 us -> 7.37 us  [scan_states(): back = lax.all_to_all(jnp.stack(entries, axis=0), axis, 0, 0, tiled=True)]
    unnamed x13 -> x16, local copies, waits for them, and re-layouts: 1.75 us -> 4.59 us
    transpose x0 -> x2, local copies, waits for them, and re-layouts: none -> 2.62 us  [columns_by_group(): return by_group(values, spans, heads).transpose(0, 1, 3, 2)]
  transfers between devices with their start and end apart: 4 -> 6, of which waited for: 1 -> 3; matrix products, arithmetic and copies ran while one was open for 7% -> 17% of each run, Pallas kernels for 9% -> 15%
where the time goes in v5:
time: 231 us; the launch traced here: 229 us
  Pallas kernels  75.6 us (33%)
  waiting for transfers between devices  51.8 us (22%)
  other arithmetic  38.9 us (17%)
  local copies, waits for them, and re-layouts  24.8 us (11%)
  starting transfers between devices  24.1 us (10%)
  blocking collectives  12.9 us (6%)
    all_to_all x2, waiting for transfers between devices, scan_states(): got = lax.all_to_all(payload, axis, 0, 0, tiled=True)  31.1 us
    pallas_call x2, Pallas kernels, gate_terms(): pl.pallas_call(gate_kernel, grid=(spans, heads // group), in_specs=[pl.Bl...  29.8 us
    pallas_call x2, Pallas kernels, block_states(): pl.pallas_call(state_kernel, grid=(spans, heads // group), in_specs=[pl.B...  24 us
    pallas_call x2, Pallas kernels, intra_terms(): pl.pallas_call(intra_kernel, grid=(spans, heads // group), in_specs=[pl.B...  21.8 us
    all_to_all x2, waiting for transfers between devices, scan_states(): back = lax.all_to_all(jnp.stack(entries, axis=0), axis, 0, 0, tiled=True)  20.7 us
    convert_element_type x1, other arithmetic, local(): return normed.astype(jnp.bfloat16)  10.1 us
    unnamed x12, other arithmetic  8.97 us
    all_to_all x2, starting transfers between devices, scan_states(): got = lax.all_to_all(payload, axis, 0, 0, tiled=True)  8.43 us
  transfers between devices with their start and end apart: 6, of which 3 were waited for; matrix products, arithmetic and copies ran while one was open for 17% of the time, Pallas kernels for 15%

profile of v5, /device:TPU:0, one launch (start us, length us, event | category | flops | bytes accessed | tf_op | source)
XLA Modules:
  0.0 229.0 jit_solution(12420045145820625073)
XLA Ops:
  1.5 4.9 %collective-permute-start = (bf16[3,64]{0,1:T(8,128)(2,1)S(1)}, bf16[3,64]{0,1:T(8,128)(2,1)S(1)}, u32[]{:S(2)}, u32[]{:S(2)}) collective-permute-start(bf16[3,64]{0,1:T(8,128)(2,1)S(1)} %constant_dynamic-slice_fusion.1), channel_id=1, source_target_pairs={{0,4},{4,8},{8,12},{12,16},{16,20},{20,24},{24,28},{1,5},{5,9},{9,... | collective-permute-start | bytes 1160 | tf_op jit(solution)/shard_map/ppermute | solution.py:18
  7.2 3.5 %collective-permute-start.1 = (bf16[3,4096]{1,0:T(4,128)(2,1)S(1)}, bf16[3,4096]{1,0:T(4,128)(2,1)S(1)}, u32[]{:S(2)}, u32[]{:S(2)}) collective-permute-start(bf16[3,4096]{1,0:T(4,128)(2,1)S(1)} %constant_dynamic-slice_fusion), channel_id=1, source_target_pairs={{0,4},{4,8},{8,12},{12,16},{16,20},{20,24},{24,28},{1,5},{5,9},{9,... | collective-permute-start | bytes 73736 | tf_op jit(solution)/shard_map/ppermute | solution.py:18
  12.8 2.3 %reduce-window.6 = f32[4,32,2,128]{3,1,2,0:T(8,128)S(1)} reduce-window(f32[4,32,2,128]{3,1,2,0:T(8,128)S(1)} %copy.92, f32[]{:T(128)} %constant.71.clone.1), window={size=1x1x1x128 pad=0_0x0_0x0_0x127_0}, to_apply=%region_0.1 | reduce-window | flops 4161536 | bytes 262148 | tf_op jit(solution)/shard_map/reduce-window
  19.5 7.2 %all_gather.3 = bf16[1024,256]{0,1:T(8,128)(2,1)S(1)} all-gather(bf16[1024,64]{0,1:T(8,128)(2,1)S(1)} %multiply_convert_fusion), channel_id=1, replica_groups=mesh['seq'=8,'ch'=4] {'ch'}, dimensions={1}, use_global_device_ids=true | all-gather | bytes 655360 | tf_op jit(solution)/shard_map/all_gather | solution.py:268
  29.3 12.0 %shard_map.109 = (f32[4,16,128,128]{3,2,1,0:T(8,128)}, bf16[1024,2048]{1,0:T(8,128)(2,1)}) custom-call(bf16[1024,4096]{1,0:T(8,128)(2,1)} %x_ref.3, bf16[4,8,4096]{2,1,0:T(8,128)(2,1)} %fusion.13.halo_ref, bf16[4,4096]{1,0:T(4,128)(2,1)} %taps_ref.3, bf16[4,128,256]{2,1,0:T(8,128)(2,1)} %bitcast.157, f32[4,2,256,8]{3,2,1,0:T(8,128)} %bitcast.145), custom_call_target="tpu_custom_call" | custom-call | flops 536870912 | bytes 12582912 | tf_op jit(solution)/shard_map/pallas_call | solution.py:149
  41.3 2.4 %fusion.34 = (f32[1,16,128,128]{3,2,1,0:T(8,128)S(1)}, f32[1,16,128,128]{3,2,1,0:T(8,128)S(1)}, f32[1,16,128,128]{3,2,1,0:T(8,128)S(1)}, f32[1,16,128,128]{3,2,1,0:T(8,128)S(1)}) fusion(f32[4,16,128,128]{3,2,1,0:T(8,128)} %get-tuple-element.38), kind=kLoop, calls=%fused_computation.135 | loop fusion | bytes 8388608 | tf_op jit(solution)/shard_map/slice | solution.py:299
  45.3 4.8 %all-to-all-start = ((f32[8,17,16,128]{3,2,1,0:T(8,128)}), f32[8,17,16,128]{3,2,1,0:T(8,128)S(1)}, u32[]{:S(2)}, u32[]{:S(2)}) async-start(f32[8,17,16,128]{3,2,1,0:T(8,128)} %pad_maximum_fusion.2), calls=%async_computation | async-start | bytes 2228224 | tf_op jit(solution)/shard_map/all_to_all | solution.py:30
  52.1 12.0 %shard_map.112 = (f32[4,16,128,128]{3,2,1,0:T(8,128)}, bf16[1024,2048]{1,0:T(8,128)(2,1)}) custom-call(bf16[1024,4096]{1,0:T(8,128)(2,1)} %x_ref.3, bf16[4,8,4096]{2,1,0:T(8,128)(2,1)} %fusion.13.halo_ref, bf16[4,4096]{1,0:T(4,128)(2,1)} %taps_ref.3, bf16[4,128,256]{2,1,0:T(8,128)(2,1)} %bitcast.158, f32[4,2,256,8]{3,2,1,0:T(8,128)} %bitcast.146), custom_call_target="tpu_custom_call" | custom-call | flops 536870912 | bytes 12582912 | tf_op jit(solution)/shard_map/pallas_call | solution.py:149
  64.1 2.4 %fusion.35 = (f32[1,16,128,128]{3,2,1,0:T(8,128)S(1)}, f32[1,16,128,128]{3,2,1,0:T(8,128)S(1)}, f32[1,16,128,128]{3,2,1,0:T(8,128)S(1)}, f32[1,16,128,128]{3,2,1,0:T(8,128)S(1)}) fusion(f32[4,16,128,128]{3,2,1,0:T(8,128)} %get-tuple-element.41), kind=kLoop, calls=%fused_computation.136 | loop fusion | bytes 8388608 | tf_op jit(solution)/shard_map/slice | solution.py:299
  68.1 9.6 %all-to-all-done = f32[8,17,16,128]{3,2,1,0:T(8,128)S(1)} async-done(((f32[8,17,16,128]{3,2,1,0:T(8,128)}), f32[8,17,16,128]{3,2,1,0:T(8,128)S(1)}, u32[]{:S(2)}, u32[]{:S(2)}) %all-to-all-start) | async-done | bytes 1114144 | tf_op jit(solution)/shard_map/all_to_all | solution.py:30
  77.8 3.6 %all-to-all-start.2 = ((f32[8,17,16,128]{3,2,1,0:T(8,128)}), f32[8,17,16,128]{3,2,1,0:T(8,128)S(1)}, u32[]{:S(2)}, u32[]{:S(2)}) async-start(f32[8,17,16,128]{3,2,1,0:T(8,128)} %pad_maximum_fusion.3), calls=%async_computation.2 | async-start | bytes 2228224 | tf_op jit(solution)/shard_map/all_to_all | solution.py:30
  87.3 21.5 %all-to-all-done.2 = f32[8,17,16,128]{3,2,1,0:T(8,128)S(1)} async-done(((f32[8,17,16,128]{3,2,1,0:T(8,128)}), f32[8,17,16,128]{3,2,1,0:T(8,128)S(1)}, u32[]{:S(2)}, u32[]{:S(2)}) %all-to-all-start.2) | async-done | bytes 1114144 | tf_op jit(solution)/shard_map/all_to_all | solution.py:30
  108.8 3.6 %all-to-all-start.1 = ((f32[8,16,16,128]{3,2,1,0:T(8,128)}), f32[8,16,16,128]{3,2,1,0:T(8,128)S(1)}, u32[]{:S(2)}, u32[]{:S(2)}) async-start(f32[8,16,16,128]{3,2,1,0:T(8,128)} %fusion.18), calls=%async_computation.1 | async-start | bytes 2097152 | tf_op jit(solution)/shard_map/all_to_all | solution.py:37
  117.6 20.7 %all-to-all-done.1 = f32[8,16,16,128]{3,2,1,0:T(8,128)S(1)} async-done(((f32[8,16,16,128]{3,2,1,0:T(8,128)}), f32[8,16,16,128]{3,2,1,0:T(8,128)S(1)}, u32[]{:S(2)}, u32[]{:S(2)}) %all-to-all-start.1) | async-done | bytes 1048608 | tf_op jit(solution)/shard_map/all_to_all | solution.py:37
  138.3 3.7 %all-to-all-start.3 = ((f32[8,16,16,128]{3,2,1,0:T(8,128)}), f32[8,16,16,128]{3,2,1,0:T(8,128)S(1)}, u32[]{:S(2)}, u32[]{:S(2)}) async-start(f32[8,16,16,128]{3,2,1,0:T(8,128)} %fusion.17), calls=%async_computation.3 | async-start | bytes 2097152 | tf_op jit(solution)/shard_map/all_to_all | solution.py:37
  151.3 11.0 %shard_map.110.part_ref = f32[1024,2048]{1,0:T(8,128)} custom-call(f32[16]{0:T(128)} %get-tuple-element.119.skip_ref, bf16[1024,128]{1,0:T(8,128)(2,1)} %copy.124.c_ref, bf16[1024,128]{1,0:T(8,128)(2,1)} %copy-done.1, bf16[1024,2048]{1,0:T(8,128)(2,1)} %get-tuple-element.37.x_ref, f32[4,2,256,8]{3,2,1,0:T(8,128)} %copy.101.cumc_ref, ...), custom_call_target="tpu_custom_call" | custom-call | flops 1140850688 | bytes 12582912 | tf_op jit(solution)/shard_map/pallas_call | solution.py:179
  162.3 10.8 %shard_map.113.part_ref = f32[1024,2048]{1,0:T(8,128)} custom-call(f32[16]{0:T(128)} %get-tuple-element.120.skip_ref, bf16[1024,128]{1,0:T(8,128)(2,1)} %copy.124.c_ref, bf16[1024,128]{1,0:T(8,128)(2,1)} %copy-done.1, bf16[1024,2048]{1,0:T(8,128)(2,1)} %get-tuple-element.40.x_ref, f32[4,2,256,8]{3,2,1,0:T(8,128)} %copy.111.cumc_ref, ...), custom_call_target="tpu_custom_call" | custom-call | flops 1140850688 | bytes 12582912 | tf_op jit(solution)/shard_map/pallas_call | solution.py:179
  173.4 2.4 %multiply_add_fusion.5 = (f32[1,16,128,128]{3,2,1,0:T(8,128)S(1)}, f32[1,16,128,128]{3,2,1,0:T(8,128)S(1)}, f32[1,16,128,128]{3,2,1,0:T(8,128)S(1)}) fusion(f32[1,16,128,128]{3,2,1,0:T(8,128)S(1)} %bitcast.140, f32[16]{0:T(128)S(1)} %get-tuple-element.46, f32[4,16,128,128]{3,2,1,0:T(8,128)} %get-tuple-element.38, f32[16]{0:T(128)S(1)} %get-tuple-element.111, ...), kind=kLoop, calls=%fused_computation.29 | loop fusion | flops 2883584 | bytes 7340416 | tf_op jit(solution)/shard_map/add | solution.py:315
  175.8 2.4 %pad_maximum_fusion.state_ref = f32[4,16,128,128]{3,2,1,0:T(8,128)} fusion(f32[1,16,128,128]{3,2,1,0:T(8,128)S(1)} %get-tuple-element.62, f32[1,16,128,128]{3,2,1,0:T(8,128)S(1)} %get-tuple-element.61, f32[1,16,128,128]{3,2,1,0:T(8,128)S(1)} %get-tuple-element.65, f32[1,16,128,128]{3,2,1,0:T(8,128)S(1)} %bitcast.141), kind=kLoop, calls=%fused_computation.4 | loop fusion | flops 3145728 | bytes 8388608 | tf_op jit(solution)/shard_map/stack | solution.py:313
  180.0 2.2 pad_maximum_fusion.1.state_ref
  182.2 14.8 %shard_map.111 = (f32[1024,2048]{1,0:T(8,128)}, f32[1024,1]{1,0:T(8,128)}) custom-call(f32[1024,2048]{1,0:T(8,128)} %shard_map.110.part_ref, bf16[1024,128]{1,0:T(8,128)(2,1)} %copy.124.c_ref, f32[4,16,128,128]{3,2,1,0:T(8,128)} %pad_maximum_fusion.state_ref, f32[4,2,256,8]{3,2,1,0:T(8,128)} %bitcast.144, bf16[1024,4096]{1,0:T(8,128)(2,1)} %z_ref.3), custom_call_target="tpu_custom_call" | custom-call | flops 1610612736 | bytes 20971520 | tf_op jit(solution)/shard_map/pallas_call | solution.py:213
  197.0 15.0 %shard_map.114 = (f32[1024,2048]{1,0:T(8,128)}, f32[1024,1]{1,0:T(8,128)}) custom-call(f32[1024,2048]{1,0:T(8,128)} %shard_map.113.part_ref, bf16[1024,128]{1,0:T(8,128)(2,1)} %copy.124.c_ref, f32[4,16,128,128]{3,2,1,0:T(8,128)} %pad_maximum_fusion.1.state_ref, f32[4,2,256,8]{3,2,1,0:T(8,128)} %bitcast.143, bf16[1024,4096]{1,0:T(8,128)(2,1)} %z_ref.3), custom_call_target="tpu_custom_call" | custom-call | flops 1610612736 | bytes 20971520 | tf_op jit(solution)/shard_map/pallas_call | solution.py:213
  213.2 5.7 %psum.7 = f32[1024]{0:T(1024)S(1)} all-reduce(f32[1024]{0:T(1024)S(1)} %add_reduce_fusion), channel_id=1, replica_groups=mesh['seq'=8,'ch'=4] {'ch'}, use_global_device_ids=true, to_apply=%region_2.3 | all-reduce | flops 1024 | bytes 8192 | tf_op jit(solution)/shard_map/psum | solution.py:334
  219.0 10.1 %fusion.2 = bf16[1024,4096]{1,0:T(8,128)(2,1)} fusion(f32[1024,2048]{1,0:T(8,128)} %get-tuple-element.42, f32[1024,2048]{1,0:T(8,128)} %get-tuple-element.39, f32[1024]{0:T(1024)S(1)} %fusion.25, f32[4096]{0:T(1024)S(1)} %copy-done.4, f32[1024]{0:T(1024)S(1)} %add_rsqrt_fusion), kind=kLoop, calls=%fused_computation.3 | loop fusion | flops 20971520 | bytes 25190400 | tf_op jit(solution)/shard_map/convert_element_type | solution.py:337
  (86 shorter events, 39.4 us)
Async XLA Ops:
  0.0 19.2 %copy-start.3 = (bf16[1024,64]{0,1:T(8,128)(2,1)S(1)}, bf16[1024,64]{0,1:T(8,128)(2,1)}, u32[]{:S(2)}) copy-start(bf16[1024,64]{0,1:T(8,128)(2,1)} %param.17) | copy-start | bytes 393220
  1.5 17.7 %collective-permute-start = (bf16[3,64]{0,1:T(8,128)(2,1)S(1)}, bf16[3,64]{0,1:T(8,128)(2,1)S(1)}, u32[]{:S(2)}, u32[]{:S(2)}) collective-permute-start(bf16[3,64]{0,1:T(8,128)(2,1)S(1)} %constant_dynamic-slice_fusion.1), channel_id=1, source_target_pairs={{0,4},{4,8},{8,12},{12,16},{16,20},{20,24},{24,28},{1,5},{5,9},{9,... | collective-permute-start | bytes 1160 | tf_op jit(solution)/shard_map/ppermute | solution.py:18
  7.2 21.3 %collective-permute-start.1 = (bf16[3,4096]{1,0:T(4,128)(2,1)S(1)}, bf16[3,4096]{1,0:T(4,128)(2,1)S(1)}, u32[]{:S(2)}, u32[]{:S(2)}) collective-permute-start(bf16[3,4096]{1,0:T(4,128)(2,1)S(1)} %constant_dynamic-slice_fusion), channel_id=1, source_target_pairs={{0,4},{4,8},{8,12},{12,16},{16,20},{20,24},{24,28},{1,5},{5,9},{9,... | collective-permute-start | bytes 73736 | tf_op jit(solution)/shard_map/ppermute | solution.py:18
  27.6 13.7 %copy-start.1 = (bf16[1024,128]{1,0:T(8,128)(2,1)}, bf16[1024,128]{1,0:T(8,128)(2,1)S(1)}, u32[]{:S(2)}) copy-start(bf16[1024,128]{1,0:T(8,128)(2,1)S(1)} %copy.125.b_ref) | copy-start | bytes 786436
  45.3 32.5 %all-to-all-start = ((f32[8,17,16,128]{3,2,1,0:T(8,128)}), f32[8,17,16,128]{3,2,1,0:T(8,128)S(1)}, u32[]{:S(2)}, u32[]{:S(2)}) async-start(f32[8,17,16,128]{3,2,1,0:T(8,128)} %pad_maximum_fusion.2), calls=%async_computation | async-start | bytes 2228224 | tf_op jit(solution)/shard_map/all_to_all | solution.py:30
  77.8 31.0 %all-to-all-start.2 = ((f32[8,17,16,128]{3,2,1,0:T(8,128)}), f32[8,17,16,128]{3,2,1,0:T(8,128)S(1)}, u32[]{:S(2)}, u32[]{:S(2)}) async-start(f32[8,17,16,128]{3,2,1,0:T(8,128)} %pad_maximum_fusion.3), calls=%async_computation.2 | async-start | bytes 2228224 | tf_op jit(solution)/shard_map/all_to_all | solution.py:30
  108.8 29.6 %all-to-all-start.1 = ((f32[8,16,16,128]{3,2,1,0:T(8,128)}), f32[8,16,16,128]{3,2,1,0:T(8,128)S(1)}, u32[]{:S(2)}, u32[]{:S(2)}) async-start(f32[8,16,16,128]{3,2,1,0:T(8,128)} %fusion.18), calls=%async_computation.1 | async-start | bytes 2097152 | tf_op jit(solution)/shard_map/all_to_all | solution.py:37
  115.4 32.8 %copy-start.5 = (f32[32]{0:T(128)S(1)}, f32[32]{0:T(128)}, u32[]{:S(2)}) copy-start(f32[32]{0:T(128)} %param.21) | copy-start | bytes 388
  138.3 34.9 %all-to-all-start.3 = ((f32[8,16,16,128]{3,2,1,0:T(8,128)}), f32[8,16,16,128]{3,2,1,0:T(8,128)S(1)}, u32[]{:S(2)}, u32[]{:S(2)}) async-start(f32[8,16,16,128]{3,2,1,0:T(8,128)} %fusion.17), calls=%async_computation.3 | async-start | bytes 2097152 | tf_op jit(solution)/shard_map/all_to_all | solution.py:37
  175.8 3.7 %copy-start = (f32[4,16,128,128]{3,2,1,0:T(8,128)S(1)}, f32[4,16,128,128]{3,2,1,0:T(8,128)}, u32[]{:S(2)}) copy-start(f32[4,16,128,128]{3,2,1,0:T(8,128)} %get-tuple-element.41) | copy-start | bytes 12582916
  197.0 15.0 %copy-start.2 = (f32[1024,1]{1,0:T(8,128)S(1)}, f32[1024,1]{1,0:T(8,128)}, u32[]{:S(2)}) copy-start(f32[1024,1]{1,0:T(8,128)} %get-tuple-element.43) | copy-start | bytes 12292
  197.0 22.0 %copy-start.4 = (f32[4096]{0:T(1024)S(1)}, f32[4096]{0:T(1024)}, u32[]{:S(2)}) copy-start(f32[4096]{0:T(1024)} %param.24) | copy-start | bytes 49156

commit v6 on v5

--- a/solution.py
+++ b/solution.py
@@ -18,24 +18,37 @@
     return lax.ppermute(block, axis, route)
 
 
-def scan_states(factor, state, axis):
+def scan_states(factor, state, axis, tied):
     count = lax.axis_size(axis)
+    split = count % 2 == 0 and count >= 4
+    members = count // 2 if split else count
+    groups = [list(range(0, members)), list(range(members, count))] if split else None
     heads, size, width = state.shape
-    piece = size // count
-    parts = state.reshape(heads, count, piece, width).transpose(1, 0, 2, 3)
+    piece = size // members
+    parts = state.reshape(heads, members, piece, width).transpose(1, 0, 2, 3)
     slot = jnp.zeros((piece, width), jnp.float32).at[0, :heads].set(factor)
     payload = jnp.concatenate(
-        [parts, jnp.broadcast_to(slot, (count, 1, piece, width))], axis=1
-    )
-    got = lax.all_to_all(payload, axis, 0, 0, tiled=True)
+        [parts, jnp.broadcast_to(slot, (members, 1, piece, width))], axis=1
+    )
+    got = lax.all_to_all(payload, axis, 0, 0, tiled=True, axis_index_groups=groups)
     decays = got[:, heads, 0, :heads]
+    tied = lax.optimization_barrier((tied, got))[0]
     running = jnp.zeros((heads, piece, width), jnp.float32)
     entries = []
-    for index in range(count):
+    for index in range(members):
         entries.append(running)
         running = decays[index][:, None, None] * running + got[index, :heads]
-    back = lax.all_to_all(jnp.stack(entries, axis=0), axis, 0, 0, tiled=True)
-    return back.transpose(1, 0, 2, 3).reshape(heads, size, width)
+    if split:
+        route = [(i, i + members) for i in range(members)]
+        earlier = lax.ppermute(running, axis, route)
+        carry = jnp.ones((heads,), jnp.float32)
+        for index in range(members):
+            entries[index] = entries[index] + carry[:, None, None] * earlier
+            carry = carry * decays[index]
+    back = lax.all_to_all(
+        jnp.stack(entries, axis=0), axis, 0, 0, tiled=True, axis_index_groups=groups
+    )
+    return back.transpose(1, 0, 2, 3).reshape(heads, size, width), tied
 
 
 def conv_silu(signal, tail_rows, weights):
@@ -279,7 +292,7 @@
     last_cum = cum_heads[:, :, -1]
     to_end = jnp.exp(last_cum[:, :, None] - cum_heads) * step_heads
     block_decay = jnp.exp(last_cum)
-    halves = 2 if head_count % (2 * HEAD_GROUP) == 0 else 1
+    halves = 1
     part_heads = head_count // halves
     gated_parts = []
     square_part = None
@@ -298,7 +311,7 @@
             factor_list.append(factor)
             current = block_decay[index, heads][:, None, None] * current + block_state[index]
             factor = factor * block_decay[index, heads]
-        group_state = scan_states(factor, current, "seq")
+        group_state, xconv = scan_states(factor, current, "seq", xconv)
         partial = intra_terms(
             skip_gain[heads],
             c_part,

time: 231 us -> 195 us (0.84)
  waiting for transfers between devices: 51.8 us -> 10.6 us
  blocking collectives: 12.9 us -> 43.2 us
  other arithmetic: 38.9 us -> 26.9 us
  local copies, waits for them, and re-layouts: 24.8 us -> 16.2 us
  Pallas kernels: 75.6 us -> 69.5 us
    all_to_all x4 -> x1, waiting for transfers between devices: 51.8 us -> 0.01 us  [scan_states(): lax.all_to_all(jnp.stack(entries, axis=0), axis, 0, 0, tiled=True, axis_i...]
    all_to_all x0 -> x1, blocking collectives: none -> 30.3 us  [scan_states(): lax.all_to_all(payload, axis, 0, 0, tiled=True, axis_index_groups=groups)]
    ppermute x0 -> x1, waiting for transfers between devices: none -> 10.6 us  [scan_states(): earlier = lax.ppermute(running, axis, route)]
    unnamed x12 -> x0, other arithmetic: 8.97 us -> none
    reshape x6 -> x1, local copies, waits for them, and re-layouts: 6.89 us -> 1.96 us  [by_group(): return values.reshape(spans, heads // HEAD_GROUP, HEAD_GROUP, -1)]
    ppermute x0 -> x1, starting transfers between devices: none -> 3.69 us  [scan_states(): earlier = lax.ppermute(running, axis, route)]
    unnamed x16 -> x12, local copies, waits for them, and re-layouts: 4.59 us -> 1.02 us
    transpose x4 -> x1, local copies, waits for them, and re-layouts: 2.82 us -> 0.24 us  [scan_states(): return (back.transpose(1, 0, 2, 3).reshape(heads, size, width), tied)]
  transfers between devices with their start and end apart: 6 -> 4, of which waited for: 3 -> 1; matrix products, arithmetic and copies ran while one was open for 17% -> 8% of each run, Pallas kernels for 15% -> 10%
where the time goes in v6:
time: 195 us; the launch traced here: 193 us
  Pallas kernels  69.5 us (36%)
  blocking collectives  43.2 us (22%)
  other arithmetic  26.9 us (14%)
  starting transfers between devices  25.6 us (13%)
  local copies, waits for them, and re-layouts  16.2 us (8%)
  waiting for transfers between devices  10.6 us (5%)
    all_to_all x1, blocking collectives, scan_states(): lax.all_to_all(payload, axis, 0, 0, tiled=True, axis_index_groups=groups)  30.3 us
    pallas_call x1, Pallas kernels, gate_terms(): pl.pallas_call(gate_kernel, grid=(spans, heads // group), in_specs=[pl.Bl...  27.5 us
    pallas_call x1, Pallas kernels, block_states(): pl.pallas_call(state_kernel, grid=(spans, heads // group), in_specs=[pl.B...  22 us
    pallas_call x1, Pallas kernels, intra_terms(): pl.pallas_call(intra_kernel, grid=(spans, heads // group), in_specs=[pl.B...  20.1 us
    all_to_all x1, starting transfers between devices, scan_states(): lax.all_to_all(jnp.stack(entries, axis=0), axis, 0, 0, tiled=True, axis_i...  13.6 us
    ppermute x1, waiting for transfers between devices, scan_states(): earlier = lax.ppermute(running, axis, route)  10.6 us
    convert_element_type x1, other arithmetic, local(): return normed.astype(jnp.bfloat16)  9.96 us
    ppermute x2, starting transfers between devices, passed_along(): return lax.ppermute(block, axis, route)  8.32 us
  transfers between devices with their start and end apart: 4, of which 1 were waited for; matrix products, arithmetic and copies ran while one was open for 8% of the time, Pallas kernels for 10%

profile of v6, /device:TPU:0, one launch (start us, length us, event | category | flops | bytes accessed | tf_op | source)
XLA Modules:
  0.0 193.0 jit_solution(15438717478827846521)
XLA Ops:
  1.5 4.9 %collective-permute-start = (bf16[3,64]{0,1:T(8,128)(2,1)S(1)}, bf16[3,64]{0,1:T(8,128)(2,1)S(1)}, u32[]{:S(2)}, u32[]{:S(2)}) collective-permute-start(bf16[3,64]{0,1:T(8,128)(2,1)S(1)} %constant_dynamic-slice_fusion.1), channel_id=1, source_target_pairs={{0,4},{4,8},{8,12},{12,16},{16,20},{20,24},{24,28},{1,5},{5,9},{9,... | collective-permute-start | bytes 1160 | tf_op jit(solution)/shard_map/ppermute | solution.py:18
  6.3 0.9 constant_dynamic-slice_fusion
  7.2 3.5 %collective-permute-start.1 = (bf16[3,4096]{1,0:T(4,128)(2,1)S(1)}, bf16[3,4096]{1,0:T(4,128)(2,1)S(1)}, u32[]{:S(2)}, u32[]{:S(2)}) collective-permute-start(bf16[3,4096]{1,0:T(4,128)(2,1)S(1)} %constant_dynamic-slice_fusion), channel_id=1, source_target_pairs={{0,4},{4,8},{8,12},{12,16},{16,20},{20,24},{24,28},{1,5},{5,9},{9,... | collective-permute-start | bytes 73736 | tf_op jit(solution)/shard_map/ppermute | solution.py:18
  11.3 1.1 fusion.13
  12.7 2.3 %reduce-window.6 = f32[4,32,2,128]{3,1,2,0:T(8,128)S(1)} reduce-window(f32[4,32,2,128]{3,1,2,0:T(8,128)S(1)} %copy.88, f32[]{:T(128)} %constant.52.clone.1), window={size=1x1x1x128 pad=0_0x0_0x0_0x127_0}, to_apply=%region_0.1 | reduce-window | flops 4161536 | bytes 262148 | tf_op jit(solution)/shard_map/reduce-window
  15.8 1.0 slice.154
  16.8 2.0 %copy.93 = f32[4,4,8,256]{2,3,1,0:T(8,128)} copy(f32[4,4,8,256]{3,2,1,0:T(8,128)S(1)} %fusion.15) | data formatting | bytes 262144 | tf_op jit(solution)/shard_map/reshape | solution.py:149
  19.0 7.2 %all_gather.3 = bf16[1024,256]{0,1:T(8,128)(2,1)S(1)} all-gather(bf16[1024,64]{0,1:T(8,128)(2,1)S(1)} %multiply_convert_fusion.1), channel_id=1, replica_groups=mesh['seq'=8,'ch'=4] {'ch'}, dimensions={1}, use_global_device_ids=true | all-gather | bytes 655360 | tf_op jit(solution)/shard_map/all_gather | solution.py:281
  28.2 22.0 %shard_map.109 = (f32[4,32,128,128]{3,2,1,0:T(8,128)}, bf16[1024,4096]{1,0:T(8,128)(2,1)}) custom-call(bf16[1024,4096]{1,0:T(8,128)(2,1)} %x_ref.1, bf16[4,8,4096]{2,1,0:T(8,128)(2,1)} %fusion.10.halo_ref, bf16[4,4096]{1,0:T(4,128)(2,1)} %taps_ref.1, bf16[4,128,256]{2,1,0:T(8,128)(2,1)} %bitcast.150, f32[4,4,256,8]{3,2,1,0:T(8,128)} %bitcast.141), custom_call_target="tpu_custom_call" | custom-call | flops 1073741824 | bytes 25165824 | tf_op jit(solution)/shard_map/pallas_call | solution.py:162
  50.1 4.1 %fusion.26 = (f32[1,32,128,128]{3,2,1,0:T(8,128)S(1)}, f32[1,32,128,128]{3,2,1,0:T(8,128)S(1)}, f32[1,32,128,128]{3,2,1,0:T(8,128)S(1)}, f32[1,32,128,128]{3,2,1,0:T(8,128)S(1)}) fusion(f32[4,32,128,128]{3,2,1,0:T(8,128)} %get-tuple-element.23), kind=kLoop, calls=%fused_computation.75 | loop fusion | bytes 16777216 | tf_op jit(solution)/shard_map/slice | solution.py:312
  55.3 30.3 %all_to_all.10 = f32[4,33,32,128]{3,2,1,0:T(8,128)S(1)} all-to-all(f32[4,33,32,128]{3,2,1,0:T(8,128)S(1)} %pad_maximum_fusion.1), channel_id=1, replica_groups={{0,4,8,12},{16,20,24,28},{1,5,9,13},{17,21,25,29},{2,6,10,14},{18,22,26..., dimensions={0} | all-to-all | bytes 4325376 | tf_op jit(solution)/shard_map/all_to_all | solution.py:33
  85.8 3.7 %collective-permute-start.2 = (f32[32,32,128]{2,1,0:T(8,128)S(1)}, f32[32,32,128]{2,1,0:T(8,128)S(1)}, u32[]{:S(2)}, u32[]{:S(2)}) collective-permute-start(f32[32,32,128]{2,1,0:T(8,128)S(1)} %get-tuple-element.31), channel_id=1, source_target_pairs={{0,16},{4,20},{8,24},{12,28},{1,17},{5,21},{9,25},{13,29},{2,18},{... | collective-permute-start | bytes 1572872 | tf_op jit(solution)/shard_map/ppermute | solution.py:43
  89.5 10.6 %collective-permute-done.2 = f32[32,32,128]{2,1,0:T(8,128)S(1)} collective-permute-done((f32[32,32,128]{2,1,0:T(8,128)S(1)}, f32[32,32,128]{2,1,0:T(8,128)S(1)}, u32[]{:S(2)}, u32[]{:S(2)}) %collective-permute-start.2) | collective-permute-done | bytes 524320 | tf_op jit(solution)/shard_map/ppermute | solution.py:43
  100.3 1.5 pad_maximum_fusion.2
  101.9 13.6 %all-to-all-start.1 = ((f32[4,32,32,128]{3,2,1,0:T(8,128)}), f32[4,32,32,128]{3,2,1,0:T(8,128)S(1)}, u32[]{:S(2)}, u32[]{:S(2)}) async-start(f32[4,32,32,128]{3,2,1,0:T(8,128)} %pad_maximum_fusion.2), calls=%async_computation.1 | async-start | bytes 4194304 | tf_op jit(solution)/shard_map/all_to_all | solution.py:48
  116.5 1.9 %copy.99 = f32[4,4,8,256]{2,3,1,0:T(8,128)} copy(f32[4,4,8,256]{3,2,1,0:T(8,128)S(1)} %reduce_window_sum.22.cumr_ref) | data formatting | bytes 262144 | tf_op jit(solution)/shard_map/reduce_window_sum
  118.4 1.9 %copy.101 = f32[4,4,8,256]{2,3,1,0:T(8,128)} copy(f32[4,4,8,256]{3,2,1,0:T(8,128)S(1)} %exp.22) | data formatting | bytes 262144 | tf_op jit(solution)/shard_map/exp | solution.py:337
  121.2 20.1 %shard_map.110.part_ref = f32[1024,4096]{1,0:T(8,128)} custom-call(f32[32]{0:T(128)} %skip_ref.1, bf16[1024,128]{1,0:T(8,128)(2,1)} %copy.104.c_ref, bf16[1024,128]{1,0:T(8,128)(2,1)} %copy-done, bf16[1024,4096]{1,0:T(8,128)(2,1)} %get-tuple-element.24.x_ref, f32[4,4,256,8]{3,2,1,0:T(8,128)} %bitcast.139, f32[4,4,8,256]{3,2,1,0:T(8,128)} %copy-done.1, ...), custom_call_target="tpu_custom_call" | custom-call | flops 2214592512 | bytes 25165824 | tf_op jit(solution)/shard_map/pallas_call | solution.py:192
  141.5 3.4 %multiply_add_fusion.1 = (f32[1,32,128,128]{3,2,1,0:T(8,128)S(1)}, f32[1,32,128,128]{3,2,1,0:T(8,128)S(1)}, f32[1,32,128,128]{3,2,1,0:T(8,128)S(1)}) fusion(f32[1,32,128,128]{3,2,1,0:T(8,128)S(1)} %bitcast.135, f32[32]{0:T(128)S(1)} %get-tuple-element.28, f32[4,32,128,128]{3,2,1,0:T(8,128)} %get-tuple-element.23, f32[32]{0:T(128)S(1)} %get-tuple-element.55, ...), kind=kLoop, calls=%fused_computation.13 | loop fusion | flops 5767168 | bytes 14680832 | tf_op jit(solution)/shard_map/add | solution.py:328
  144.9 3.7 %pad_maximum_fusion.state_ref = f32[4,32,128,128]{3,2,1,0:T(8,128)} fusion(f32[1,32,128,128]{3,2,1,0:T(8,128)S(1)} %get-tuple-element.34, f32[1,32,128,128]{3,2,1,0:T(8,128)S(1)} %get-tuple-element.33, f32[1,32,128,128]{3,2,1,0:T(8,128)S(1)} %get-tuple-element.35, f32[1,32,128,128]{3,2,1,0:T(8,128)S(1)} %bitcast.136), kind=kLoop, calls=%fused_computation.1 | loop fusion | flops 6291456 | bytes 16777216 | tf_op jit(solution)/shard_map/stack | solution.py:326
  148.6 27.5 %shard_map.111 = (f32[1024,4096]{1,0:T(8,128)}, f32[1024,1]{1,0:T(8,128)}) custom-call(f32[1024,4096]{1,0:T(8,128)} %shard_map.110.part_ref, bf16[1024,128]{1,0:T(8,128)(2,1)} %copy.104.c_ref, f32[4,32,128,128]{3,2,1,0:T(8,128)} %pad_maximum_fusion.state_ref, f32[4,4,256,8]{3,2,1,0:T(8,128)} %bitcast.138, bf16[1024,4096]{1,0:T(8,128)(2,1)} %z_ref.1), custom_call_target="tpu_custom_call" | custom-call | flops 3221225472 | bytes 41943040 | tf_op jit(solution)/shard_map/pallas_call | solution.py:226
  176.1 1.2 reduce.3
  177.3 5.7 %psum.7 = f32[1024]{0:T(1024)S(1)} all-reduce(f32[1024]{0:T(1024)S(1)} %reduce.3), channel_id=1, replica_groups=mesh['seq'=8,'ch'=4] {'ch'}, use_global_device_ids=true, to_apply=%region_2.3 | all-reduce | flops 1024 | bytes 8192 | tf_op jit(solution)/shard_map/psum | solution.py:347
  183.0 10.0 %multiply_convert_fusion = bf16[1024,4096]{1,0:T(8,128)(2,1)} fusion(f32[1024,4096]{1,0:T(8,128)} %get-tuple-element.25, f32[1024]{0:T(1024)S(1)} %fusion.18, f32[4096]{0:T(1024)S(1)} %copy-done.3, f32[1024]{0:T(1024)S(1)} %add_rsqrt_fusion), kind=kLoop, calls=%fused_computation | loop fusion | flops 16777216 | bytes 25190400 | tf_op jit(solution)/shard_map/convert_element_type | solution.py:350
  (53 shorter events, 8.2 us)
Async XLA Ops:
  0.0 15.8 %copy-start.4 = (bf16[4,64]{1,0:T(4,128)(2,1)S(1)}, bf16[4,64]{1,0:T(4,128)(2,1)}, u32[]{:S(2)}) copy-start(bf16[4,64]{1,0:T(4,128)(2,1)} %param.21) | copy-start | bytes 1540
  1.5 17.3 %collective-permute-start = (bf16[3,64]{0,1:T(8,128)(2,1)S(1)}, bf16[3,64]{0,1:T(8,128)(2,1)S(1)}, u32[]{:S(2)}, u32[]{:S(2)}) collective-permute-start(bf16[3,64]{0,1:T(8,128)(2,1)S(1)} %constant_dynamic-slice_fusion.1), channel_id=1, source_target_pairs={{0,4},{4,8},{8,12},{12,16},{16,20},{20,24},{24,28},{1,5},{5,9},{9,... | collective-permute-start | bytes 1160 | tf_op jit(solution)/shard_map/ppermute | solution.py:18
  7.2 20.1 %collective-permute-start.1 = (bf16[3,4096]{1,0:T(4,128)(2,1)S(1)}, bf16[3,4096]{1,0:T(4,128)(2,1)S(1)}, u32[]{:S(2)}, u32[]{:S(2)}) collective-permute-start(bf16[3,4096]{1,0:T(4,128)(2,1)S(1)} %constant_dynamic-slice_fusion), channel_id=1, source_target_pairs={{0,4},{4,8},{8,12},{12,16},{16,20},{20,24},{24,28},{1,5},{5,9},{9,... | collective-permute-start | bytes 73736 | tf_op jit(solution)/shard_map/ppermute | solution.py:18
  12.7 6.1 %copy-start.2 = (bf16[1024,64]{0,1:T(8,128)(2,1)S(1)}, bf16[1024,64]{0,1:T(8,128)(2,1)}, u32[]{:S(2)}) copy-start(bf16[1024,64]{0,1:T(8,128)(2,1)} %param.15) | copy-start | bytes 393220
  26.4 23.7 %copy-start = (bf16[1024,128]{1,0:T(8,128)(2,1)}, bf16[1024,128]{1,0:T(8,128)(2,1)S(1)}, u32[]{:S(2)}) copy-start(bf16[1024,128]{1,0:T(8,128)(2,1)S(1)} %copy.105.b_ref) | copy-start | bytes 786436
  85.8 14.2 %collective-permute-start.2 = (f32[32,32,128]{2,1,0:T(8,128)S(1)}, f32[32,32,128]{2,1,0:T(8,128)S(1)}, u32[]{:S(2)}, u32[]{:S(2)}) collective-permute-start(f32[32,32,128]{2,1,0:T(8,128)S(1)} %get-tuple-element.31), channel_id=1, source_target_pairs={{0,16},{4,20},{8,24},{12,28},{1,17},{5,21},{9,25},{13,29},{2,18},{... | collective-permute-start | bytes 1572872 | tf_op jit(solution)/shard_map/ppermute | solution.py:43
  101.9 39.4 %all-to-all-start.1 = ((f32[4,32,32,128]{3,2,1,0:T(8,128)}), f32[4,32,32,128]{3,2,1,0:T(8,128)S(1)}, u32[]{:S(2)}, u32[]{:S(2)}) async-start(f32[4,32,32,128]{3,2,1,0:T(8,128)} %pad_maximum_fusion.2), calls=%async_computation.1 | async-start | bytes 4194304 | tf_op jit(solution)/shard_map/all_to_all | solution.py:48
  116.4 3.9 %copy-start.1 = (f32[4,4,8,256]{3,2,1,0:T(8,128)}, f32[4,4,8,256]{3,2,1,0:T(8,128)S(1)}, u32[]{:S(2)}) copy-start(f32[4,4,8,256]{3,2,1,0:T(8,128)S(1)} %reduce_window_sum.22.cumr_ref) | copy-start | bytes 393220
  148.6 34.4 %copy-start.3 = (f32[4096]{0:T(1024)S(1)}, f32[4096]{0:T(1024)}, u32[]{:S(2)}) copy-start(f32[4096]{0:T(1024)} %param.22) | copy-start | bytes 49156

commit v7 on v6

--- a/solution.py
+++ b/solution.py
@@ -112,14 +112,27 @@
         )
 
 
-def gate_kernel(part_ref, c_ref, state_ref, ecum_ref, z_ref, out_ref, sq_ref):
-    group = pl.program_id(1)
+def gate_kernel(decay_ref, part_ref, c_ref, block_ref, group_ref, ecum_ref, z_ref, out_ref, sq_ref):
+    group = pl.program_id(0)
+    span = pl.program_id(1)
+    spans = block_ref.shape[0]
     heads = ecum_ref.shape[-1]
+    head_count = decay_ref.shape[0] // spans
     width = out_ref.shape[-1] // heads
     c = c_ref[...]
-    total = jnp.zeros((c.shape[0], 1), jnp.float32)
+    total = jnp.zeros((c.shape[0], width), jnp.float32)
     for j in range(heads):
-        state = state_ref[0, j]
+        head = group * heads + j
+        local_state = jnp.zeros(block_ref.shape[2:], jnp.float32)
+        factor = jnp.float32(1.0)
+        for earlier in range(spans - 1):
+            decay = decay_ref[earlier * head_count + head]
+            take = earlier < span
+            local_state = jnp.where(
+                take, decay * local_state + block_ref[earlier, j], local_state
+            )
+            factor = jnp.where(take, factor * decay, factor)
+        state = local_state + factor * group_ref[j]
         high = state.astype(jnp.bfloat16)
         rest = state - high.astype(jnp.float32)
         mid = rest.astype(jnp.bfloat16)
@@ -134,15 +147,8 @@
         z = z_ref[:, columns].astype(jnp.float32)
         gated = y * (z / (1.0 + jnp.exp(-z)))
         out_ref[:, columns] = gated
-        total = total + jnp.sum(gated * gated, axis=1, keepdims=True)
-
-    @pl.when(group == 0)
-    def _():
-        sq_ref[...] = total
-
-    @pl.when(group > 0)
-    def _():
-        sq_ref[...] = sq_ref[...] + total
+        total = total + gated * gated
+    sq_ref[0] = jnp.sum(total, axis=1, keepdims=True)
 
 
 def by_group(values, spans, heads):
@@ -219,34 +225,48 @@
     )
 
 
-def gate_terms(partial, c_part, state_enter, ecum, gate_in, spans, heads, width, offset):
+def gate_terms(
+    block_decay, partial, c_part, block_state, group_state, ecum, gate_in, spans, heads, width, offset
+):
     rows = partial.shape[0]
     size = c_part.shape[1]
     group = HEAD_GROUP
+    groups = heads // group
     return pl.pallas_call(
         gate_kernel,
-        grid=(spans, heads // group),
+        grid=(groups, spans),
         in_specs=[
-            pl.BlockSpec((SEGMENT_LENGTH, group * width), lambda c, g: (c, g)),
-            pl.BlockSpec((SEGMENT_LENGTH, size), lambda c, g: (c, 0)),
-            pl.BlockSpec((1, group, size, width), lambda c, g: (c, g, 0, 0)),
-            pl.BlockSpec((1, 1, SEGMENT_LENGTH, group), lambda c, g: (c, g, 0, 0)),
-            pl.BlockSpec((SEGMENT_LENGTH, group * width), lambda c, g: (c, g + offset)),
+            pl.BlockSpec(memory_space=pltpu.SMEM),
+            pl.BlockSpec((SEGMENT_LENGTH, group * width), lambda g, c: (c, g)),
+            pl.BlockSpec((SEGMENT_LENGTH, size), lambda g, c: (c, 0)),
+            pl.BlockSpec((spans, group, size, width), lambda g, c: (0, g, 0, 0)),
+            pl.BlockSpec((group, size, width), lambda g, c: (g, 0, 0)),
+            pl.BlockSpec((1, 1, SEGMENT_LENGTH, group), lambda g, c: (c, g, 0, 0)),
+            pl.BlockSpec((SEGMENT_LENGTH, group * width), lambda g, c: (c, g + offset)),
         ],
         out_specs=[
-            pl.BlockSpec((SEGMENT_LENGTH, group * width), lambda c, g: (c, g)),
-            pl.BlockSpec((SEGMENT_LENGTH, 1), lambda c, g: (c, 0)),
+            pl.BlockSpec((SEGMENT_LENGTH, group * width), lambda g, c: (c, g)),
+            pl.BlockSpec((1, SEGMENT_LENGTH, 1), lambda g, c: (g, c, 0)),
         ],
         out_shape=[
             jax.ShapeDtypeStruct((rows, heads * width), jnp.float32),
-            jax.ShapeDtypeStruct((rows, 1), jnp.float32),
-        ],
+            jax.ShapeDtypeStruct((groups, rows, 1), jnp.float32),
+        ],
+        compiler_params=pltpu.CompilerParams(vmem_limit_bytes=48 * 1024 * 1024),
         cost_estimate=pl.CostEstimate(
             flops=6 * rows * size * heads * width,
             bytes_accessed=rows * heads * width * 10,
             transcendentals=rows * heads * width,
         ),
-    )(partial, c_part, state_enter, columns_by_group(ecum, spans, heads), gate_in)
+    )(
+        block_decay.reshape(-1),
+        partial,
+        c_part,
+        block_state,
+        group_state,
+        columns_by_group(ecum, spans, heads),
+        gate_in,
+    )
 
 
 def local(
@@ -270,7 +290,8 @@
     live_rows = valid_blocks[0] * BLOCK
     tail_x = lax.dynamic_slice_in_dim(xin, live_rows - (kernel_taps - 1), kernel_taps - 1, 0)
     tail_bc = lax.dynamic_slice_in_dim(bc_proj, live_rows - (kernel_taps - 1), kernel_taps - 1, 0)
-    prev_x, prev_bc = passed_along((tail_x, tail_bc), "seq", 1)
+    prev = passed_along(jnp.concatenate([tail_x, tail_bc], axis=1), "seq", 1)
+    prev_x, prev_bc = prev[:, :channels], prev[:, channels:]
     lead = 8
     edges = jnp.concatenate(
         [prev_x[None], xin.reshape(span_count, SEGMENT_LENGTH, channels)[:-1, -(kernel_taps - 1) :]],
@@ -323,17 +344,12 @@
             part_heads,
             head_size,
         )
-        state_enter = jnp.stack(
-            [
-                local_enter[index] + factor_list[index][:, None, None] * group_state
-                for index in range(span_count)
-            ],
-            axis=0,
-        )
         gated, squares = gate_terms(
+            block_decay[:, heads],
             partial,
             c_part,
-            state_enter,
+            block_state,
+            group_state,
             jnp.exp(cum_heads[:, heads]),
             gate_in,
             span_count,
@@ -341,6 +357,7 @@
             head_size,
             offset,
         )
+        squares = jnp.sum(squares, axis=0)
         gated_parts.append(gated)
         square_part = squares if square_part is None else square_part + squares
     gated = jnp.concatenate(gated_parts, axis=1)

time: 195 us -> 183 us (0.938)
  other arithmetic: 26.9 us -> 18.9 us
  starting transfers between devices: 25.6 us -> 22.2 us
    another operation x6 -> x5, other arithmetic: 6.32 us -> 2.64 us  [the longest x1 3.69 us: local(): jnp.stack([local_enter[index] + factor_list[index][:, None, None] * group...]
    ppermute x2 -> x1, starting transfers between devices: 8.32 us -> 4.87 us  [passed_along(): return lax.ppermute(block, axis, route)]
    add x1 -> x0, other arithmetic: 3.4 us -> none  [local(): local_enter[index] + factor_list[index][:, None, None] * group_state]
  transfers between devices with their start and end apart: 4 -> 3, of which waited for: 1 -> 1; matrix products, arithmetic and copies ran while one was open for 8% -> 8% of each run, Pallas kernels for 10% -> 11%
where the time goes in v7:
time: 183 us; the launch traced here: 181 us
  Pallas kernels  68.4 us (37%)
  blocking collectives  43.3 us (24%)
  starting transfers between devices  22.2 us (12%)
  other arithmetic  18.9 us (10%)
  local copies, waits for them, and re-layouts  17.2 us (9%)
  waiting for transfers between devices  10.5 us (6%)
    all_to_all x1, blocking collectives, scan_states(): lax.all_to_all(payload, axis, 0, 0, tiled=True, axis_index_groups=groups)  30.4 us
    pallas_call x1, Pallas kernels, gate_terms(): pl.pallas_call(gate_kernel, grid=(groups, spans), in_specs=[pl.BlockSpec(...  26.4 us
    pallas_call x1, Pallas kernels, block_states(): pl.pallas_call(state_kernel, grid=(spans, heads // group), in_specs=[pl.B...  22 us
    pallas_call x1, Pallas kernels, intra_terms(): pl.pallas_call(intra_kernel, grid=(spans, heads // group), in_specs=[pl.B...  20 us
    all_to_all x1, starting transfers between devices, scan_states(): lax.all_to_all(jnp.stack(entries, axis=0), axis, 0, 0, tiled=True, axis_i...  13.7 us
    ppermute x1, waiting for transfers between devices, scan_states(): earlier = lax.ppermute(running, axis, route)  10.5 us
    convert_element_type x1, other arithmetic, local(): return normed.astype(jnp.bfloat16)  9.96 us
    all_gather x1, blocking collectives, local(): bc_full = lax.all_gather(bc_local, 'ch', axis=1, tiled=True)  7.2 us
  transfers between devices with their start and end apart: 3, of which 1 were waited for; matrix products, arithmetic and copies ran while one was open for 8% of the time, Pallas kernels for 11%

profile of v7, /device:TPU:0, one launch (start us, length us, event | category | flops | bytes accessed | tf_op | source)
XLA Modules:
  0.0 181.3 jit_solution(5456518585783167237)
XLA Ops:
  0.7 0.8 constant_dynamic-slice_fusion
  1.6 0.9 constant_dynamic-slice_fusion.1
  2.5 4.9 %collective-permute-start = (bf16[3,4160]{1,0:T(4,128)(2,1)S(1)}, bf16[3,4160]{1,0:T(4,128)(2,1)S(1)}, u32[]{:S(2)}, u32[]{:S(2)}) collective-permute-start(bf16[3,4160]{1,0:T(4,128)(2,1)S(1)} %pad_maximum_fusion.3), channel_id=1, source_target_pairs={{0,4},{4,8},{8,12},{12,16},{16,20},{20,24},{24,28},{1,5},{5,9},{9,... | collective-permute-start | bytes 74888 | tf_op jit(solution)/shard_map/ppermute | solution.py:18
  8.0 1.1 fusion.13
  9.4 2.3 %reduce-window.6 = f32[4,32,2,128]{3,1,2,0:T(8,128)S(1)} reduce-window(f32[4,32,2,128]{3,1,2,0:T(8,128)S(1)} %copy.87, f32[]{:T(128)} %constant.47.clone.1), window={size=1x1x1x128 pad=0_0x0_0x0_0x127_0}, to_apply=%region_0.1 | reduce-window | flops 4161536 | bytes 262148 | tf_op jit(solution)/shard_map/reduce-window
  12.5 1.0 slice.167
  13.5 1.9 %copy.97 = f32[4,4,8,256]{2,3,1,0:T(8,128)} copy(f32[4,4,8,256]{3,2,1,0:T(8,128)S(1)} %fusion.15) | data formatting | bytes 262144 | tf_op jit(solution)/shard_map/reshape | solution.py:155
  15.8 7.2 %all_gather.3 = bf16[1024,256]{0,1:T(8,128)(2,1)S(1)} all-gather(bf16[1024,64]{0,1:T(8,128)(2,1)S(1)} %multiply_convert_fusion.1), channel_id=1, replica_groups=mesh['seq'=8,'ch'=4] {'ch'}, dimensions={1}, use_global_device_ids=true | all-gather | bytes 655360 | tf_op jit(solution)/shard_map/all_gather | solution.py:302
  23.2 0.9 copy.95
  24.1 0.8 fusion.10.halo_ref
  24.9 22.0 %shard_map.109 = (f32[4,32,128,128]{3,2,1,0:T(8,128)}, bf16[1024,4096]{1,0:T(8,128)(2,1)}) custom-call(bf16[1024,4096]{1,0:T(8,128)(2,1)} %x_ref.1, bf16[4,8,4096]{2,1,0:T(8,128)(2,1)} %fusion.10.halo_ref, bf16[4,4096]{1,0:T(4,128)(2,1)} %taps_ref.1, bf16[4,128,256]{2,1,0:T(8,128)(2,1)} %bitcast.140, f32[4,4,256,8]{3,2,1,0:T(8,128)} %bitcast.131), custom_call_target="tpu_custom_call" | custom-call | flops 1073741824 | bytes 25165824 | tf_op jit(solution)/shard_map/pallas_call | solution.py:168
  46.9 4.1 %fusion.23 = (f32[1,32,128,128]{3,2,1,0:T(8,128)S(1)}, f32[1,32,128,128]{3,2,1,0:T(8,128)S(1)}, f32[1,32,128,128]{3,2,1,0:T(8,128)S(1)}, f32[1,32,128,128]{3,2,1,0:T(8,128)S(1)}) fusion(f32[4,32,128,128]{3,2,1,0:T(8,128)} %get-tuple-element.23.block_ref), kind=kLoop, calls=%fused_computation.70 | loop fusion | bytes 16777216 | tf_op jit(solution)/shard_map/slice | solution.py:333
  52.1 30.4 %all_to_all.10 = f32[4,33,32,128]{3,2,1,0:T(8,128)S(1)} all-to-all(f32[4,33,32,128]{3,2,1,0:T(8,128)S(1)} %pad_maximum_fusion), channel_id=1, replica_groups={{0,4,8,12},{16,20,24,28},{1,5,9,13},{17,21,25,29},{2,6,10,14},{18,22,26..., dimensions={0} | all-to-all | bytes 4325376 | tf_op jit(solution)/shard_map/all_to_all | solution.py:33
  82.7 3.6 %collective-permute-start.1 = (f32[32,32,128]{2,1,0:T(8,128)S(1)}, f32[32,32,128]{2,1,0:T(8,128)S(1)}, u32[]{:S(2)}, u32[]{:S(2)}) collective-permute-start(f32[32,32,128]{2,1,0:T(8,128)S(1)} %get-tuple-element.31), channel_id=1, source_target_pairs={{0,16},{4,20},{8,24},{12,28},{1,17},{5,21},{9,25},{13,29},{2,18},{... | collective-permute-start | bytes 1572872 | tf_op jit(solution)/shard_map/ppermute | solution.py:43
  86.3 10.5 %collective-permute-done.1 = f32[32,32,128]{2,1,0:T(8,128)S(1)} collective-permute-done((f32[32,32,128]{2,1,0:T(8,128)S(1)}, f32[32,32,128]{2,1,0:T(8,128)S(1)}, u32[]{:S(2)}, u32[]{:S(2)}) %collective-permute-start.1) | collective-permute-done | bytes 524320 | tf_op jit(solution)/shard_map/ppermute | solution.py:43
  97.0 1.5 pad_maximum_fusion.1
  98.6 13.7 %all-to-all-start.1 = ((f32[4,32,32,128]{3,2,1,0:T(8,128)}), f32[4,32,32,128]{3,2,1,0:T(8,128)S(1)}, u32[]{:S(2)}, u32[]{:S(2)}) async-start(f32[4,32,32,128]{3,2,1,0:T(8,128)} %pad_maximum_fusion.1), calls=%async_computation.1 | async-start | bytes 4194304 | tf_op jit(solution)/shard_map/all_to_all | solution.py:48
  113.3 1.9 %copy.103 = f32[4,4,8,256]{2,3,1,0:T(8,128)} copy(f32[4,4,8,256]{3,2,1,0:T(8,128)S(1)} %reduce_window_sum.22.cumr_ref) | data formatting | bytes 262144 | tf_op jit(solution)/shard_map/reduce_window_sum
  115.3 1.9 %copy.105 = f32[4,4,8,256]{2,3,1,0:T(8,128)} copy(f32[4,4,8,256]{3,2,1,0:T(8,128)S(1)} %exp.30) | data formatting | bytes 262144 | tf_op jit(solution)/shard_map/exp | solution.py:353
  117.2 0.9 copy.109.c_ref
  118.1 20.0 %shard_map.110.part_ref = f32[1024,4096]{1,0:T(8,128)} custom-call(f32[32]{0:T(128)} %skip_ref.1, bf16[1024,128]{1,0:T(8,128)(2,1)} %copy.109.c_ref, bf16[1024,128]{1,0:T(8,128)(2,1)} %copy-done.1, bf16[1024,4096]{1,0:T(8,128)(2,1)} %get-tuple-element.24.x_ref, f32[4,4,256,8]{3,2,1,0:T(8,128)} %bitcast.129, f32[4,4,8,256]{3,2,1,0:T(8,128)} %copy-done.2, ...), custom_call_target="tpu_custom_call" | custom-call | flops 2214592512 | bytes 25165824 | tf_op jit(solution)/shard_map/pallas_call | solution.py:198
  139.1 26.4 %shard_map.111 = (f32[1024,4096]{1,0:T(8,128)}, f32[4,1024,1]{2,1,0:T(8,128)S(1)}) custom-call(f32[128]{0:T(128)S(1)} %exp.26.decay_ref, f32[1024,4096]{1,0:T(8,128)} %shard_map.110.part_ref, bf16[1024,128]{1,0:T(8,128)(2,1)S(1)} %copy-done, f32[4,32,128,128]{3,2,1,0:T(8,128)} %get-tuple-element.23.block_ref, f32[32,128,128]{2,1,0:T(8,128)S(1)} %bitcast.126, ...), custom_call_target="tpu_custom_call" | custom-call | flops 3221225472 | bytes 41943040 | tf_op jit(solution)/shard_map/pallas_call | solution.py:235
  165.7 5.7 %psum.7 = f32[1024]{0:T(1024)S(1)} all-reduce(f32[1024]{0:T(1024)S(1)} %reduce_sum.9), channel_id=1, replica_groups=mesh['seq'=8,'ch'=4] {'ch'}, use_global_device_ids=true, to_apply=%region_3.4 | all-reduce | flops 1024 | bytes 8192 | tf_op jit(solution)/shard_map/psum | solution.py:364
  171.3 10.0 %multiply_convert_fusion = bf16[1024,4096]{1,0:T(8,128)(2,1)} fusion(f32[1024,4096]{1,0:T(8,128)} %get-tuple-element.25, f32[1024]{0:T(1024)S(1)} %fusion.18, f32[4096]{0:T(1024)S(1)} %copy-done.4, f32[1024]{0:T(1024)S(1)} %add_rsqrt_fusion), kind=kLoop, calls=%fused_computation | loop fusion | flops 16777216 | bytes 25190400 | tf_op jit(solution)/shard_map/convert_element_type | solution.py:367
  (56 shorter events, 6.1 us)
Async XLA Ops:
  0.0 12.4 %copy-start.5 = (bf16[4,64]{1,0:T(4,128)(2,1)S(1)}, bf16[4,64]{1,0:T(4,128)(2,1)}, u32[]{:S(2)}) copy-start(bf16[4,64]{1,0:T(4,128)(2,1)} %param.21) | copy-start | bytes 1540
  2.5 12.9 %collective-permute-start = (bf16[3,4160]{1,0:T(4,128)(2,1)S(1)}, bf16[3,4160]{1,0:T(4,128)(2,1)S(1)}, u32[]{:S(2)}, u32[]{:S(2)}) collective-permute-start(bf16[3,4160]{1,0:T(4,128)(2,1)S(1)} %pad_maximum_fusion.3), channel_id=1, source_target_pairs={{0,4},{4,8},{8,12},{12,16},{16,20},{20,24},{24,28},{1,5},{5,9},{9,... | collective-permute-start | bytes 74888 | tf_op jit(solution)/shard_map/ppermute | solution.py:18
  9.4 6.2 %copy-start.3 = (bf16[1024,64]{0,1:T(8,128)(2,1)S(1)}, bf16[1024,64]{0,1:T(8,128)(2,1)}, u32[]{:S(2)}) copy-start(bf16[1024,64]{0,1:T(8,128)(2,1)} %param.15) | copy-start | bytes 393220
  23.2 23.7 %copy-start.1 = (bf16[1024,128]{1,0:T(8,128)(2,1)}, bf16[1024,128]{1,0:T(8,128)(2,1)S(1)}, u32[]{:S(2)}) copy-start(bf16[1024,128]{1,0:T(8,128)(2,1)S(1)} %copy.110.b_ref) | copy-start | bytes 786436
  82.7 14.1 %collective-permute-start.1 = (f32[32,32,128]{2,1,0:T(8,128)S(1)}, f32[32,32,128]{2,1,0:T(8,128)S(1)}, u32[]{:S(2)}, u32[]{:S(2)}) collective-permute-start(f32[32,32,128]{2,1,0:T(8,128)S(1)} %get-tuple-element.31), channel_id=1, source_target_pairs={{0,16},{4,20},{8,24},{12,28},{1,17},{5,21},{9,25},{13,29},{2,18},{... | collective-permute-start | bytes 1572872 | tf_op jit(solution)/shard_map/ppermute | solution.py:43
  98.6 39.5 %all-to-all-start.1 = ((f32[4,32,32,128]{3,2,1,0:T(8,128)}), f32[4,32,32,128]{3,2,1,0:T(8,128)S(1)}, u32[]{:S(2)}, u32[]{:S(2)}) async-start(f32[4,32,32,128]{3,2,1,0:T(8,128)} %pad_maximum_fusion.1), calls=%async_computation.1 | async-start | bytes 4194304 | tf_op jit(solution)/shard_map/all_to_all | solution.py:48
  113.2 4.0 %copy-start.2 = (f32[4,4,8,256]{3,2,1,0:T(8,128)}, f32[4,4,8,256]{3,2,1,0:T(8,128)S(1)}, u32[]{:S(2)}) copy-start(f32[4,4,8,256]{3,2,1,0:T(8,128)S(1)} %reduce_window_sum.22.cumr_ref) | copy-start | bytes 393220
  138.1 1.0 copy-start
  165.4 5.9 %copy-start.4 = (f32[4096]{0:T(1024)S(1)}, f32[4096]{0:T(1024)}, u32[]{:S(2)}) copy-start(f32[4096]{0:T(1024)} %param.22) | copy-start | bytes 49156

commit v8 on v7

--- a/solution.py
+++ b/solution.py
@@ -66,6 +66,11 @@
 HEAD_GROUP = 8
 
 
+def silu(value):
+    half = 0.5 * value
+    return half + half * jnp.tanh(half)
+
+
 def state_kernel(x_ref, halo_ref, taps_ref, bt_ref, toend_ref, out_ref, conv_ref):
     width = out_ref.shape[-1]
     taps = taps_ref[...].astype(jnp.float32)
@@ -81,8 +86,8 @@
         moved = signal if shift == 0 else pltpu.roll(signal, shift, 0)
         accum = accum + taps[offset : offset + 1] * moved
         head = head + taps[offset : offset + 1] * stacked[lead - shift : 2 * lead - shift]
-    conv_ref[...] = (accum / (1.0 + jnp.exp(-accum))).astype(jnp.bfloat16)
-    conv_ref[:lead, :] = (head / (1.0 + jnp.exp(-head))).astype(jnp.bfloat16)
+    conv_ref[...] = silu(accum).astype(jnp.bfloat16)
+    conv_ref[:lead, :] = silu(head).astype(jnp.bfloat16)
     bt = bt_ref[0]
     for j in range(out_ref.shape[1]):
         x = conv_ref[:, j * width : (j + 1) * width].astype(jnp.float32)
@@ -145,7 +150,7 @@
         columns = slice(j * width, (j + 1) * width)
         y = part_ref[:, columns] + inter * ecum_ref[0, 0, :, j : j + 1]
         z = z_ref[:, columns].astype(jnp.float32)
-        gated = y * (z / (1.0 + jnp.exp(-z)))
+        gated = y * silu(z)
         out_ref[:, columns] = gated
         total = total + gated * gated
     sq_ref[0] = jnp.sum(total, axis=1, keepdims=True)

time: 183 us -> 183 us (level)
  no operation moved by 1% of the time
where the time goes in v8:
time: 183 us; the launch traced here: 181 us
  Pallas kernels  67.9 us (37%)
  blocking collectives  43.3 us (24%)
  starting transfers between devices  22.2 us (12%)
  other arithmetic  18.9 us (10%)
  local copies, waits for them, and re-layouts  17.2 us (9%)
  waiting for transfers between devices  10.5 us (6%)
    all_to_all x1, blocking collectives, scan_states(): lax.all_to_all(payload, axis, 0, 0, tiled=True, axis_index_groups=groups)  30.4 us
    pallas_call x1, Pallas kernels, gate_terms(): pl.pallas_call(gate_kernel, grid=(groups, spans), in_specs=[pl.BlockSpec(...  25.8 us
    pallas_call x1, Pallas kernels, block_states(): pl.pallas_call(state_kernel, grid=(spans, heads // group), in_specs=[pl.B...  22.1 us
    pallas_call x1, Pallas kernels, intra_terms(): pl.pallas_call(intra_kernel, grid=(spans, heads // group), in_specs=[pl.B...  20 us
    all_to_all x1, starting transfers between devices, scan_states(): lax.all_to_all(jnp.stack(entries, axis=0), axis, 0, 0, tiled=True, axis_i...  13.7 us
    ppermute x1, waiting for transfers between devices, scan_states(): earlier = lax.ppermute(running, axis, route)  10.5 us
    convert_element_type x1, other arithmetic, local(): return normed.astype(jnp.bfloat16)  9.96 us
    all_gather x1, blocking collectives, local(): bc_full = lax.all_gather(bc_local, 'ch', axis=1, tiled=True)  7.2 us
  transfers between devices with their start and end apart: 3, of which 1 were waited for; matrix products, arithmetic and copies ran while one was open for 8% of the time, Pallas kernels for 11%

profile of v8, /device:TPU:0, one launch (start us, length us, event | category | flops | bytes accessed | tf_op | source)
XLA Modules:
  0.0 180.8 jit_solution(3942236935752409132)
XLA Ops:
  0.7 0.8 constant_dynamic-slice_fusion
  1.6 0.9 constant_dynamic-slice_fusion.1
  2.5 4.9 %collective-permute-start = (bf16[3,4160]{1,0:T(4,128)(2,1)S(1)}, bf16[3,4160]{1,0:T(4,128)(2,1)S(1)}, u32[]{:S(2)}, u32[]{:S(2)}) collective-permute-start(bf16[3,4160]{1,0:T(4,128)(2,1)S(1)} %pad_maximum_fusion.3), channel_id=1, source_target_pairs={{0,4},{4,8},{8,12},{12,16},{16,20},{20,24},{24,28},{1,5},{5,9},{9,... | collective-permute-start | bytes 74888 | tf_op jit(solution)/shard_map/ppermute | solution.py:18
  8.0 1.1 fusion.13
  9.4 2.3 %reduce-window.6 = f32[4,32,2,128]{3,1,2,0:T(8,128)S(1)} reduce-window(f32[4,32,2,128]{3,1,2,0:T(8,128)S(1)} %copy.87, f32[]{:T(128)} %constant.47.clone.1), window={size=1x1x1x128 pad=0_0x0_0x0_0x127_0}, to_apply=%region_0.1 | reduce-window | flops 4161536 | bytes 262148 | tf_op jit(solution)/shard_map/reduce-window
  12.5 1.0 slice.167
  13.5 1.9 %copy.97 = f32[4,4,8,256]{2,3,1,0:T(8,128)} copy(f32[4,4,8,256]{3,2,1,0:T(8,128)S(1)} %fusion.15) | data formatting | bytes 262144 | tf_op jit(solution)/shard_map/reshape | solution.py:160
  15.8 7.2 %all_gather.3 = bf16[1024,256]{0,1:T(8,128)(2,1)S(1)} all-gather(bf16[1024,64]{0,1:T(8,128)(2,1)S(1)} %multiply_convert_fusion.1), channel_id=1, replica_groups=mesh['seq'=8,'ch'=4] {'ch'}, dimensions={1}, use_global_device_ids=true | all-gather | bytes 655360 | tf_op jit(solution)/shard_map/all_gather | solution.py:307
  23.2 0.9 copy.95
  24.1 0.8 fusion.10.halo_ref
  24.9 22.1 %shard_map.109 = (f32[4,32,128,128]{3,2,1,0:T(8,128)}, bf16[1024,4096]{1,0:T(8,128)(2,1)}) custom-call(bf16[1024,4096]{1,0:T(8,128)(2,1)} %x_ref.1, bf16[4,8,4096]{2,1,0:T(8,128)(2,1)} %fusion.10.halo_ref, bf16[4,4096]{1,0:T(4,128)(2,1)} %taps_ref.1, bf16[4,128,256]{2,1,0:T(8,128)(2,1)} %bitcast.140, f32[4,4,256,8]{3,2,1,0:T(8,128)} %bitcast.131), custom_call_target="tpu_custom_call" | custom-call | flops 1073741824 | bytes 25165824 | tf_op jit(solution)/shard_map/pallas_call | solution.py:173
  47.0 4.1 %fusion.23 = (f32[1,32,128,128]{3,2,1,0:T(8,128)S(1)}, f32[1,32,128,128]{3,2,1,0:T(8,128)S(1)}, f32[1,32,128,128]{3,2,1,0:T(8,128)S(1)}, f32[1,32,128,128]{3,2,1,0:T(8,128)S(1)}) fusion(f32[4,32,128,128]{3,2,1,0:T(8,128)} %get-tuple-element.23.block_ref), kind=kLoop, calls=%fused_computation.70 | loop fusion | bytes 16777216 | tf_op jit(solution)/shard_map/slice | solution.py:338
  52.2 30.4 %all_to_all.10 = f32[4,33,32,128]{3,2,1,0:T(8,128)S(1)} all-to-all(f32[4,33,32,128]{3,2,1,0:T(8,128)S(1)} %pad_maximum_fusion), channel_id=1, replica_groups={{0,4,8,12},{16,20,24,28},{1,5,9,13},{17,21,25,29},{2,6,10,14},{18,22,26..., dimensions={0} | all-to-all | bytes 4325376 | tf_op jit(solution)/shard_map/all_to_all | solution.py:33
  82.8 3.6 %collective-permute-start.1 = (f32[32,32,128]{2,1,0:T(8,128)S(1)}, f32[32,32,128]{2,1,0:T(8,128)S(1)}, u32[]{:S(2)}, u32[]{:S(2)}) collective-permute-start(f32[32,32,128]{2,1,0:T(8,128)S(1)} %get-tuple-element.31), channel_id=1, source_target_pairs={{0,16},{4,20},{8,24},{12,28},{1,17},{5,21},{9,25},{13,29},{2,18},{... | collective-permute-start | bytes 1572872 | tf_op jit(solution)/shard_map/ppermute | solution.py:43
  86.4 10.5 %collective-permute-done.1 = f32[32,32,128]{2,1,0:T(8,128)S(1)} collective-permute-done((f32[32,32,128]{2,1,0:T(8,128)S(1)}, f32[32,32,128]{2,1,0:T(8,128)S(1)}, u32[]{:S(2)}, u32[]{:S(2)}) %collective-permute-start.1) | collective-permute-done | bytes 524320 | tf_op jit(solution)/shard_map/ppermute | solution.py:43
  97.1 1.5 pad_maximum_fusion.1
  98.7 13.7 %all-to-all-start.1 = ((f32[4,32,32,128]{3,2,1,0:T(8,128)}), f32[4,32,32,128]{3,2,1,0:T(8,128)S(1)}, u32[]{:S(2)}, u32[]{:S(2)}) async-start(f32[4,32,32,128]{3,2,1,0:T(8,128)} %pad_maximum_fusion.1), calls=%async_computation.1 | async-start | bytes 4194304 | tf_op jit(solution)/shard_map/all_to_all | solution.py:48
  113.4 1.9 %copy.103 = f32[4,4,8,256]{2,3,1,0:T(8,128)} copy(f32[4,4,8,256]{3,2,1,0:T(8,128)S(1)} %reduce_window_sum.22.cumr_ref) | data formatting | bytes 262144 | tf_op jit(solution)/shard_map/reduce_window_sum
  115.4 1.9 %copy.105 = f32[4,4,8,256]{2,3,1,0:T(8,128)} copy(f32[4,4,8,256]{3,2,1,0:T(8,128)S(1)} %exp.30) | data formatting | bytes 262144 | tf_op jit(solution)/shard_map/exp | solution.py:358
  117.3 0.9 copy.109.c_ref
  118.2 20.0 %shard_map.110.part_ref = f32[1024,4096]{1,0:T(8,128)} custom-call(f32[32]{0:T(128)} %skip_ref.1, bf16[1024,128]{1,0:T(8,128)(2,1)} %copy.109.c_ref, bf16[1024,128]{1,0:T(8,128)(2,1)} %copy-done.1, bf16[1024,4096]{1,0:T(8,128)(2,1)} %get-tuple-element.24.x_ref, f32[4,4,256,8]{3,2,1,0:T(8,128)} %bitcast.129, f32[4,4,8,256]{3,2,1,0:T(8,128)} %copy-done.2, ...), custom_call_target="tpu_custom_call" | custom-call | flops 2214592512 | bytes 25165824 | tf_op jit(solution)/shard_map/pallas_call | solution.py:203
  139.2 25.8 %shard_map.111 = (f32[1024,4096]{1,0:T(8,128)}, f32[4,1024,1]{2,1,0:T(8,128)S(1)}) custom-call(f32[128]{0:T(128)S(1)} %exp.26.decay_ref, f32[1024,4096]{1,0:T(8,128)} %shard_map.110.part_ref, bf16[1024,128]{1,0:T(8,128)(2,1)S(1)} %copy-done, f32[4,32,128,128]{3,2,1,0:T(8,128)} %get-tuple-element.23.block_ref, f32[32,128,128]{2,1,0:T(8,128)S(1)} %bitcast.126, ...), custom_call_target="tpu_custom_call" | custom-call | flops 3221225472 | bytes 41943040 | tf_op jit(solution)/shard_map/pallas_call | solution.py:240
  165.2 5.7 %psum.7 = f32[1024]{0:T(1024)S(1)} all-reduce(f32[1024]{0:T(1024)S(1)} %reduce_sum.9), channel_id=1, replica_groups=mesh['seq'=8,'ch'=4] {'ch'}, use_global_device_ids=true, to_apply=%region_3.4 | all-reduce | flops 1024 | bytes 8192 | tf_op jit(solution)/shard_map/psum | solution.py:369
  170.8 10.0 %multiply_convert_fusion = bf16[1024,4096]{1,0:T(8,128)(2,1)} fusion(f32[1024,4096]{1,0:T(8,128)} %get-tuple-element.25, f32[1024]{0:T(1024)S(1)} %fusion.18, f32[4096]{0:T(1024)S(1)} %copy-done.4, f32[1024]{0:T(1024)S(1)} %add_rsqrt_fusion), kind=kLoop, calls=%fused_computation | loop fusion | flops 16777216 | bytes 25190400 | tf_op jit(solution)/shard_map/convert_element_type | solution.py:372
  (56 shorter events, 6.1 us)
Async XLA Ops:
  0.0 12.4 %copy-start.5 = (bf16[4,64]{1,0:T(4,128)(2,1)S(1)}, bf16[4,64]{1,0:T(4,128)(2,1)}, u32[]{:S(2)}) copy-start(bf16[4,64]{1,0:T(4,128)(2,1)} %param.21) | copy-start | bytes 1540
  2.5 12.9 %collective-permute-start = (bf16[3,4160]{1,0:T(4,128)(2,1)S(1)}, bf16[3,4160]{1,0:T(4,128)(2,1)S(1)}, u32[]{:S(2)}, u32[]{:S(2)}) collective-permute-start(bf16[3,4160]{1,0:T(4,128)(2,1)S(1)} %pad_maximum_fusion.3), channel_id=1, source_target_pairs={{0,4},{4,8},{8,12},{12,16},{16,20},{20,24},{24,28},{1,5},{5,9},{9,... | collective-permute-start | bytes 74888 | tf_op jit(solution)/shard_map/ppermute | solution.py:18
  9.4 6.2 %copy-start.3 = (bf16[1024,64]{0,1:T(8,128)(2,1)S(1)}, bf16[1024,64]{0,1:T(8,128)(2,1)}, u32[]{:S(2)}) copy-start(bf16[1024,64]{0,1:T(8,128)(2,1)} %param.15) | copy-start | bytes 393220
  23.2 23.8 %copy-start.1 = (bf16[1024,128]{1,0:T(8,128)(2,1)}, bf16[1024,128]{1,0:T(8,128)(2,1)S(1)}, u32[]{:S(2)}) copy-start(bf16[1024,128]{1,0:T(8,128)(2,1)S(1)} %copy.110.b_ref) | copy-start | bytes 786436
  82.8 14.1 %collective-permute-start.1 = (f32[32,32,128]{2,1,0:T(8,128)S(1)}, f32[32,32,128]{2,1,0:T(8,128)S(1)}, u32[]{:S(2)}, u32[]{:S(2)}) collective-permute-start(f32[32,32,128]{2,1,0:T(8,128)S(1)} %get-tuple-element.31), channel_id=1, source_target_pairs={{0,16},{4,20},{8,24},{12,28},{1,17},{5,21},{9,25},{13,29},{2,18},{... | collective-permute-start | bytes 1572872 | tf_op jit(solution)/shard_map/ppermute | solution.py:43
  98.7 39.5 %all-to-all-start.1 = ((f32[4,32,32,128]{3,2,1,0:T(8,128)}), f32[4,32,32,128]{3,2,1,0:T(8,128)S(1)}, u32[]{:S(2)}, u32[]{:S(2)}) async-start(f32[4,32,32,128]{3,2,1,0:T(8,128)} %pad_maximum_fusion.1), calls=%async_computation.1 | async-start | bytes 4194304 | tf_op jit(solution)/shard_map/all_to_all | solution.py:48
  113.3 4.0 %copy-start.2 = (f32[4,4,8,256]{3,2,1,0:T(8,128)}, f32[4,4,8,256]{3,2,1,0:T(8,128)S(1)}, u32[]{:S(2)}) copy-start(f32[4,4,8,256]{3,2,1,0:T(8,128)S(1)} %reduce_window_sum.22.cumr_ref) | copy-start | bytes 393220
  138.2 1.0 copy-start
  164.9 5.9 %copy-start.4 = (f32[4096]{0:T(1024)S(1)}, f32[4096]{0:T(1024)}, u32[]{:S(2)}) copy-start(f32[4096]{0:T(1024)} %param.22) | copy-start | bytes 49156

commit v9 on v8

--- a/solution.py
+++ b/solution.py
@@ -18,7 +18,7 @@
     return lax.ppermute(block, axis, route)
 
 
-def scan_states(factor, state, axis, tied):
+def scan_states(decays, state, axis, tied):
     count = lax.axis_size(axis)
     split = count % 2 == 0 and count >= 4
     members = count // 2 if split else count
@@ -26,18 +26,13 @@
     heads, size, width = state.shape
     piece = size // members
     parts = state.reshape(heads, members, piece, width).transpose(1, 0, 2, 3)
-    slot = jnp.zeros((piece, width), jnp.float32).at[0, :heads].set(factor)
-    payload = jnp.concatenate(
-        [parts, jnp.broadcast_to(slot, (members, 1, piece, width))], axis=1
-    )
-    got = lax.all_to_all(payload, axis, 0, 0, tiled=True, axis_index_groups=groups)
-    decays = got[:, heads, 0, :heads]
-    tied = lax.optimization_barrier((tied, got))[0]
+    got = lax.all_to_all(parts, axis, 0, 0, tiled=True, axis_index_groups=groups)
     running = jnp.zeros((heads, piece, width), jnp.float32)
     entries = []
     for index in range(members):
         entries.append(running)
-        running = decays[index][:, None, None] * running + got[index, :heads]
+        running = decays[index][:, None, None] * running + got[index]
+    running, tied = lax.optimization_barrier((running, tied))
     if split:
         route = [(i, i + members) for i in range(members)]
         earlier = lax.ppermute(running, axis, route)
@@ -95,8 +90,9 @@
         out_ref[0, j] = jnp.dot(bt, xw, preferred_element_type=jnp.float32)
 
 
-def intra_kernel(skip_ref, c_ref, b_ref, x_ref, cumc_ref, cumr_ref, stepr_ref, out_ref):
-    group = pl.program_id(1)
+def intra_kernel(offset, skip_ref, c_ref, b_ref, x_ref, cumc_ref, cumr_ref, stepr_ref, *rest):
+    out_ref = rest[-1]
+    group = pl.program_id(1) + offset
     heads = cumc_ref.shape[-1]
     width = out_ref.shape[-1] // heads
     scores = lax.dot_general(
@@ -196,38 +192,41 @@
     )(xin, halo, conv_x, b_t, columns_by_group(to_end, spans, heads))
 
 
-def intra_terms(skip_gain, c_part, b_part, xconv, cum_heads, step_heads, spans, heads, width):
+def intra_terms(
+    skip_gain, c_part, b_part, xconv, cum_col, cum_row, step_row, spans, groups, width, offset, into
+):
     rows = xconv.shape[0]
     size = c_part.shape[1]
     group = HEAD_GROUP
+    heads = groups * group
+    in_specs = [
+        pl.BlockSpec(memory_space=pltpu.SMEM),
+        pl.BlockSpec((SEGMENT_LENGTH, size), lambda c, g: (c, 0)),
+        pl.BlockSpec((SEGMENT_LENGTH, size), lambda c, g: (c, 0)),
+        pl.BlockSpec((SEGMENT_LENGTH, group * width), lambda c, g: (c, g + offset)),
+        pl.BlockSpec((1, 1, SEGMENT_LENGTH, group), lambda c, g: (c, g + offset, 0, 0)),
+        pl.BlockSpec((1, 1, group, SEGMENT_LENGTH), lambda c, g: (c, g + offset, 0, 0)),
+        pl.BlockSpec((1, 1, group, SEGMENT_LENGTH), lambda c, g: (c, g + offset, 0, 0)),
+    ]
+    operands = [skip_gain, c_part, b_part, xconv, cum_col, cum_row, step_row]
+    aliases = {}
+    if into is not None:
+        in_specs.append(pl.BlockSpec(memory_space=pl.ANY))
+        operands.append(into)
+        aliases = {len(operands) - 1: 0}
     return pl.pallas_call(
-        intra_kernel,
-        grid=(spans, heads // group),
-        in_specs=[
-            pl.BlockSpec(memory_space=pltpu.SMEM),
-            pl.BlockSpec((SEGMENT_LENGTH, size), lambda c, g: (c, 0)),
-            pl.BlockSpec((SEGMENT_LENGTH, size), lambda c, g: (c, 0)),
-            pl.BlockSpec((SEGMENT_LENGTH, group * width), lambda c, g: (c, g)),
-            pl.BlockSpec((1, 1, SEGMENT_LENGTH, group), lambda c, g: (c, g, 0, 0)),
-            pl.BlockSpec((1, 1, group, SEGMENT_LENGTH), lambda c, g: (c, g, 0, 0)),
-            pl.BlockSpec((1, 1, group, SEGMENT_LENGTH), lambda c, g: (c, g, 0, 0)),
-        ],
-        out_specs=pl.BlockSpec((SEGMENT_LENGTH, group * width), lambda c, g: (c, g)),
-        out_shape=jax.ShapeDtypeStruct((rows, heads * width), jnp.float32),
+        functools.partial(intra_kernel, offset),
+        grid=(spans, groups),
+        in_specs=in_specs,
+        out_specs=pl.BlockSpec((SEGMENT_LENGTH, group * width), lambda c, g: (c, g + offset)),
+        out_shape=jax.ShapeDtypeStruct((rows, xconv.shape[1]), jnp.float32),
+        input_output_aliases=aliases,
         cost_estimate=pl.CostEstimate(
             flops=2 * rows * SEGMENT_LENGTH * (heads * width + size),
             bytes_accessed=rows * heads * width * 6,
             transcendentals=rows * SEGMENT_LENGTH * heads,
         ),
-    )(
-        skip_gain,
-        c_part,
-        b_part,
-        xconv,
-        columns_by_group(cum_heads, spans, heads),
-        by_group(cum_heads, spans, heads),
-        by_group(step_heads, spans, heads),
-    )
+    )(*operands)
 
 
 def gate_terms(
@@ -318,6 +317,14 @@
     last_cum = cum_heads[:, :, -1]
     to_end = jnp.exp(last_cum[:, :, None] - cum_heads) * step_heads
     block_decay = jnp.exp(last_cum)
+    count = lax.axis_size("seq")
+    members = count // 2 if count % 2 == 0 and count >= 4 else count
+    groups = [list(range(0, members)), list(range(members, count))] if members < count else None
+    group_decay = jnp.ones((head_count,), jnp.float32)
+    for index in range(span_count):
+        group_decay = group_decay * block_decay[index]
+    decays = lax.all_gather(group_decay, "seq", axis_index_groups=groups)
+    to_end, decays = lax.optimization_barrier((to_end, decays))
     halves = 1
     part_heads = head_count // halves
     gated_parts = []
@@ -337,18 +344,21 @@
             factor_list.append(factor)
             current = block_decay[index, heads][:, None, None] * current + block_state[index]
             factor = factor * block_decay[index, heads]
-        group_state, xconv = scan_states(factor, current, "seq", xconv)
+        cum_col = columns_by_group(cum_heads[:, heads], span_count, part_heads)
+        cum_row = by_group(cum_heads[:, heads], span_count, part_heads)
+        step_row = by_group(step_heads[:, heads], span_count, part_heads)
+        groups = part_heads // HEAD_GROUP
+        first = groups // 2 if groups >= 2 else groups
         partial = intra_terms(
-            skip_gain[heads],
-            c_part,
-            b_part,
-            xconv,
-            cum_heads[:, heads],
-            step_heads[:, heads],
-            span_count,
-            part_heads,
-            head_size,
+            skip_gain[heads], c_part, b_part, xconv, cum_col, cum_row, step_row,
+            span_count, first, head_size, 0, None,
         )
+        group_state, partial = scan_states(decays, current, "seq", partial)
+        if first < groups:
+            partial = intra_terms(
+                skip_gain[heads], c_part, b_part, xconv, cum_col, cum_row, step_row,
+                span_count, groups - first, head_size, first, partial,
+            )
         gated, squares = gate_terms(
             block_decay[:, heads],
             partial,

time: 183 us -> 192 us (1.049)
  waiting for transfers between devices: 10.5 us -> 34.3 us
  blocking collectives: 43.3 us -> 22.1 us
  starting transfers between devices: 22.2 us -> 26.3 us
    all_to_all x1 -> x0, blocking collectives: 30.4 us -> none  [scan_states(): lax.all_to_all(payload, axis, 0, 0, tiled=True, axis_index_groups=groups)]
    all_to_all x1, waiting for transfers between devices: 0.01 us -> 12.7 us  [scan_states(): lax.all_to_all(jnp.stack(entries, axis=0), axis, 0, 0, tiled=True, axis_i...]
    all_to_all x0 -> x1, waiting for transfers between devices: none -> 10.8 us  [scan_states(): lax.all_to_all(parts, axis, 0, 0, tiled=True, axis_index_groups=groups)]
    all_gather x0 -> x1, blocking collectives: none -> 9.22 us  [local(): decays = lax.all_gather(group_decay, 'seq', axis_index_groups=groups)]
    all_to_all x0 -> x1, starting transfers between devices: none -> 3.61 us  [scan_states(): lax.all_to_all(parts, axis, 0, 0, tiled=True, axis_index_groups=groups)]
    pallas_call x1 -> x2, Pallas kernels: 20 us -> 21.8 us  [intra_terms(): pl.pallas_call(functools.partial(intra_kernel, offset), grid=(spans, grou...]
  transfers between devices with their start and end apart: 3 -> 4, of which waited for: 1 -> 3; matrix products, arithmetic and copies ran while one was open for 8% -> 7% of each run, Pallas kernels for 11% -> 11%
where the time goes in v9:
time: 192 us; the launch traced here: 191 us
  Pallas kernels  69.7 us (36%)
  waiting for transfers between devices  34.3 us (18%)
  starting transfers between devices  26.3 us (14%)
  blocking collectives  22.1 us (12%)
  other arithmetic  19.9 us (10%)
  local copies, waits for them, and re-layouts  17.4 us (9%)
    pallas_call x1, Pallas kernels, gate_terms(): pl.pallas_call(gate_kernel, grid=(groups, spans), in_specs=[pl.BlockSpec(...  25.8 us
    pallas_call x1, Pallas kernels, block_states(): pl.pallas_call(state_kernel, grid=(spans, heads // group), in_specs=[pl.B...  22.1 us
    pallas_call x2, Pallas kernels, intra_terms(): pl.pallas_call(functools.partial(intra_kernel, offset), grid=(spans, grou...  21.8 us
    all_to_all x1, starting transfers between devices, scan_states(): lax.all_to_all(jnp.stack(entries, axis=0), axis, 0, 0, tiled=True, axis_i...  14.3 us
    all_to_all x1, waiting for transfers between devices, scan_states(): lax.all_to_all(jnp.stack(entries, axis=0), axis, 0, 0, tiled=True, axis_i...  12.7 us
    ppermute x1, waiting for transfers between devices, scan_states(): earlier = lax.ppermute(running, axis, route)  10.8 us
    all_to_all x1, waiting for transfers between devices, scan_states(): lax.all_to_all(parts, axis, 0, 0, tiled=True, axis_index_groups=groups)  10.8 us
    convert_element_type x1, other arithmetic, local(): return normed.astype(jnp.bfloat16)  9.96 us
  transfers between devices with their start and end apart: 4, of which 3 were waited for; matrix products, arithmetic and copies ran while one was open for 7% of the time, Pallas kernels for 11%

profile of v9, /device:TPU:0, one launch (start us, length us, event | category | flops | bytes accessed | tf_op | source)
XLA Modules:
  0.0 190.7 jit_solution(12826393269731217853)
XLA Ops:
  2.5 4.9 %collective-permute-start = (bf16[3,4160]{1,0:T(4,128)(2,1)S(1)}, bf16[3,4160]{1,0:T(4,128)(2,1)S(1)}, u32[]{:S(2)}, u32[]{:S(2)}) collective-permute-start(bf16[3,4160]{1,0:T(4,128)(2,1)S(1)} %pad_maximum_fusion.2), channel_id=1, source_target_pairs={{0,4},{4,8},{8,12},{12,16},{16,20},{20,24},{24,28},{1,5},{5,9},{9,... | collective-permute-start | bytes 74888 | tf_op jit(solution)/shard_map/ppermute | solution.py:18
  7.4 1.1 fusion.13
  9.4 2.3 %reduce-window.6 = f32[4,32,2,128]{3,1,2,0:T(8,128)S(1)} reduce-window(f32[4,32,2,128]{3,1,2,0:T(8,128)S(1)} %copy.95, f32[]{:T(128)} %constant.9.clone.1), window={size=1x1x1x128 pad=0_0x0_0x0_0x127_0}, to_apply=%region_0.1 | reduce-window | flops 4161536 | bytes 262148 | tf_op jit(solution)/shard_map/reduce-window
  12.6 9.2 %all-gather = f32[4,1,32]{2,1,0:T(1,128)S(1)} all-gather(f32[1,1,32]{2,1,0:T(1,128)S(1)} %get-tuple-element.42), channel_id=1, replica_groups={{0,4,8,12},{16,20,24,28},{1,5,9,13},{17,21,25,29},{2,6,10,14},{18,22,26..., dimensions={0}, use_global_device_ids=true | all-gather | bytes 640 | tf_op jit(solution)/shard_map/all_gather | solution.py:326
  21.8 2.0 %copy.107 = f32[4,4,8,256]{2,3,1,0:T(8,128)} copy(f32[4,4,8,256]{3,0,2,1:T(4,128)S(1)} %bitcast.128) | data formatting | bytes 262144 | tf_op jit(solution)/shard_map/reshape | solution.py:156
  23.8 1.0 slice.142
  25.2 7.2 %all_gather.7 = bf16[1024,256]{0,1:T(8,128)(2,1)S(1)} all-gather(bf16[1024,64]{0,1:T(8,128)(2,1)S(1)} %multiply_convert_fusion.1), channel_id=1, replica_groups=mesh['seq'=8,'ch'=4] {'ch'}, dimensions={1}, use_global_device_ids=true | all-gather | bytes 655360 | tf_op jit(solution)/shard_map/all_gather | solution.py:306
  34.3 22.1 %shard_map.109 = (f32[4,32,128,128]{3,2,1,0:T(8,128)}, bf16[1024,4096]{1,0:T(8,128)(2,1)}) custom-call(bf16[1024,4096]{1,0:T(8,128)(2,1)} %x_ref.1, bf16[4,8,4096]{2,1,0:T(8,128)(2,1)} %fusion.10.halo_ref, bf16[4,4096]{1,0:T(4,128)(2,1)} %taps_ref.1, bf16[4,128,256]{2,1,0:T(8,128)(2,1)} %bitcast.127, f32[4,4,256,8]{3,2,1,0:T(8,128)} %bitcast.117), custom_call_target="tpu_custom_call" | custom-call | flops 1073741824 | bytes 25165824 | tf_op jit(solution)/shard_map/pallas_call | solution.py:169
  56.4 4.1 %fusion.23 = (f32[1,32,128,128]{3,2,1,0:T(8,128)S(1)}, f32[1,32,128,128]{3,2,1,0:T(8,128)S(1)}, f32[1,32,128,128]{3,2,1,0:T(8,128)S(1)}, f32[1,32,128,128]{3,2,1,0:T(8,128)S(1)}) fusion(f32[4,32,128,128]{3,2,1,0:T(8,128)} %get-tuple-element.16.block_ref), kind=kLoop, calls=%fused_computation.69 | loop fusion | bytes 16777216 | tf_op jit(solution)/shard_map/slice | solution.py:345
  60.5 2.0 %fusion = f32[4,32,32,128]{3,2,1,0:T(8,128)} fusion(f32[32,4,32,128]{3,2,1,0:T(8,128)S(1)} %bitcast.119, f32[32,4,32,128]{3,2,1,0:T(8,128)S(1)} %bitcast.120, f32[32,4,32,128]{3,2,1,0:T(8,128)S(1)} %bitcast.121, f32[32,4,32,128]{3,2,1,0:T(8,128)S(1)} %bitcast.118, f32[32]{0:T(128)S(1)} %get-tuple-element.45, f32[32]{0:T(128)S(1)} %get-tuple-element.44, ...), kind=kLoop, calls=%fused_computation.3 | loop fusion | flops 3670016 | bytes 10486272 | tf_op jit(solution)/shard_map/transpose | solution.py:28
  62.5 3.6 %all-to-all-start = ((f32[4,32,32,128]{3,2,1,0:T(8,128)}), f32[4,32,32,128]{3,2,1,0:T(8,128)S(1)}, u32[]{:S(2)}, u32[]{:S(2)}) async-start(f32[4,32,32,128]{3,2,1,0:T(8,128)} %fusion), calls=%async_computation | async-start | bytes 4194304 | tf_op jit(solution)/shard_map/all_to_all | solution.py:29
  66.5 2.0 %copy.109 = f32[4,4,8,256]{2,3,1,0:T(8,128)} copy(f32[4,4,8,256]{3,2,1,0:T(8,128)S(1)} %reduce_window_sum.22.cumr_ref) | data formatting | bytes 262144 | tf_op jit(solution)/shard_map/reduce_window_sum
  70.0 10.9 %shard_map.110.rest_0_ = f32[1024,4096]{1,0:T(8,128)} custom-call(f32[32]{0:T(128)} %skip_ref.3, bf16[1024,128]{1,0:T(8,128)(2,1)} %copy.122.c_ref, bf16[1024,128]{1,0:T(8,128)(2,1)} %copy-done.1, bf16[1024,4096]{1,0:T(8,128)(2,1)} %get-tuple-element.14.x_ref, f32[4,4,256,8]{3,2,1,0:T(8,128)} %bitcast.112, f32[4,4,8,256]{3,2,1,0:T(8,128)} %copy-done.2, ...), custom_call_target="tpu_custom_call" | custom-call | flops 1140850688 | bytes 12582912 | tf_op jit(solution)/shard_map/pallas_call | solution.py:217
  80.9 10.8 %all-to-all-done = f32[4,32,32,128]{3,2,1,0:T(8,128)S(1)} async-done(((f32[4,32,32,128]{3,2,1,0:T(8,128)}), f32[4,32,32,128]{3,2,1,0:T(8,128)S(1)}, u32[]{:S(2)}, u32[]{:S(2)}) %all-to-all-start) | async-done | bytes 2097184 | tf_op jit(solution)/shard_map/all_to_all | solution.py:29
  92.0 3.5 %collective-permute-start.1 = (f32[32,32,128]{2,1,0:T(8,128)S(1)}, f32[32,32,128]{2,1,0:T(8,128)S(1)}, u32[]{:S(2)}, u32[]{:S(2)}) collective-permute-start(f32[32,32,128]{2,1,0:T(8,128)S(1)} %get-tuple-element.18), channel_id=1, source_target_pairs={{0,16},{4,20},{8,24},{12,28},{1,17},{5,21},{9,25},{13,29},{2,18},{... | collective-permute-start | bytes 1572872 | tf_op jit(solution)/shard_map/ppermute | solution.py:38
  95.5 10.8 %collective-permute-done.1 = f32[32,32,128]{2,1,0:T(8,128)S(1)} collective-permute-done((f32[32,32,128]{2,1,0:T(8,128)S(1)}, f32[32,32,128]{2,1,0:T(8,128)S(1)}, u32[]{:S(2)}, u32[]{:S(2)}) %collective-permute-start.1) | collective-permute-done | bytes 524320 | tf_op jit(solution)/shard_map/ppermute | solution.py:38
  106.6 1.5 pad_maximum_fusion
  108.1 14.3 %all-to-all-start.1 = ((f32[4,32,32,128]{3,2,1,0:T(8,128)}), f32[4,32,32,128]{3,2,1,0:T(8,128)S(1)}, u32[]{:S(2)}, u32[]{:S(2)}) async-start(f32[4,32,32,128]{3,2,1,0:T(8,128)} %pad_maximum_fusion), calls=%async_computation.1 | async-start | bytes 4194304 | tf_op jit(solution)/shard_map/all_to_all | solution.py:43
  122.4 2.0 %copy.116 = f32[4,4,8,256]{2,3,1,0:T(8,128)} copy(f32[4,4,8,256]{3,2,1,0:T(8,128)S(1)} %exp.30) | data formatting | bytes 262144 | tf_op jit(solution)/shard_map/exp | solution.py:368
  124.5 10.9 %shard_map.111.part_ref = f32[1024,4096]{1,0:T(8,128)} custom-call(f32[32]{0:T(128)} %skip_ref.3, bf16[1024,128]{1,0:T(8,128)(2,1)} %copy.122.c_ref, bf16[1024,128]{1,0:T(8,128)(2,1)} %copy-done.1, bf16[1024,4096]{1,0:T(8,128)(2,1)} %get-tuple-element.14.x_ref, f32[4,4,256,8]{3,2,1,0:T(8,128)} %bitcast.113, ...), custom_call_target="tpu_custom_call", output_to_operand_aliasing={{}: (7, {})} | custom-call | flops 1140850688 | bytes 12582912 | tf_op jit(solution)/shard_map/pallas_call | solution.py:217
  135.4 12.7 %all-to-all-done.1 = f32[4,32,32,128]{3,2,1,0:T(8,128)S(1)} async-done(((f32[4,32,32,128]{3,2,1,0:T(8,128)}), f32[4,32,32,128]{3,2,1,0:T(8,128)S(1)}, u32[]{:S(2)}, u32[]{:S(2)}) %all-to-all-start.1) | async-done | bytes 2097184 | tf_op jit(solution)/shard_map/all_to_all | solution.py:43
  149.0 25.8 %shard_map.112 = (f32[1024,4096]{1,0:T(8,128)}, f32[4,1024,1]{2,1,0:T(8,128)S(1)}) custom-call(f32[128]{0:T(128)S(1)} %exp.26.decay_ref, f32[1024,4096]{1,0:T(8,128)} %shard_map.111.part_ref, bf16[1024,128]{1,0:T(8,128)(2,1)S(1)} %copy-done, f32[4,32,128,128]{3,2,1,0:T(8,128)} %get-tuple-element.16.block_ref, f32[32,128,128]{2,1,0:T(8,128)S(1)} %bitcast.111, ...), custom_call_target="tpu_custom_call" | custom-call | flops 3221225472 | bytes 41943040 | tf_op jit(solution)/shard_map/pallas_call | solution.py:239
  175.1 5.7 %psum.7 = f32[1024]{0:T(1024)S(1)} all-reduce(f32[1024]{0:T(1024)S(1)} %reduce_sum.9), channel_id=1, replica_groups=mesh['seq'=8,'ch'=4] {'ch'}, use_global_device_ids=true, to_apply=%region_3.4 | all-reduce | flops 1024 | bytes 8192 | tf_op jit(solution)/shard_map/psum | solution.py:379
  180.7 10.0 %multiply_convert_fusion = bf16[1024,4096]{1,0:T(8,128)(2,1)} fusion(f32[1024,4096]{1,0:T(8,128)} %get-tuple-element.19, f32[1024]{0:T(1024)S(1)} %fusion.18, f32[4096]{0:T(1024)S(1)} %copy-done.5, f32[1024]{0:T(1024)S(1)} %add_rsqrt_fusion), kind=kLoop, calls=%fused_computation | loop fusion | flops 16777216 | bytes 25190400 | tf_op jit(solution)/shard_map/convert_element_type | solution.py:382
  (59 shorter events, 9.5 us)
Async XLA Ops:
  0.0 12.5 %copy-start.6 = (bf16[4,64]{1,0:T(4,128)(2,1)S(1)}, bf16[4,64]{1,0:T(4,128)(2,1)}, u32[]{:S(2)}) copy-start(bf16[4,64]{1,0:T(4,128)(2,1)} %param.19) | copy-start | bytes 1540
  2.5 22.3 %collective-permute-start = (bf16[3,4160]{1,0:T(4,128)(2,1)S(1)}, bf16[3,4160]{1,0:T(4,128)(2,1)S(1)}, u32[]{:S(2)}, u32[]{:S(2)}) collective-permute-start(bf16[3,4160]{1,0:T(4,128)(2,1)S(1)} %pad_maximum_fusion.2), channel_id=1, source_target_pairs={{0,4},{4,8},{8,12},{12,16},{16,20},{20,24},{24,28},{1,5},{5,9},{9,... | collective-permute-start | bytes 74888 | tf_op jit(solution)/shard_map/ppermute | solution.py:18
  9.4 15.5 %copy-start.4 = (bf16[1024,64]{0,1:T(8,128)(2,1)S(1)}, bf16[1024,64]{0,1:T(8,128)(2,1)}, u32[]{:S(2)}) copy-start(bf16[1024,64]{0,1:T(8,128)(2,1)} %param.13) | copy-start | bytes 393220
  32.6 23.8 %copy-start.1 = (bf16[1024,128]{1,0:T(8,128)(2,1)}, bf16[1024,128]{1,0:T(8,128)(2,1)S(1)}, u32[]{:S(2)}) copy-start(bf16[1024,128]{1,0:T(8,128)(2,1)S(1)} %copy.123.b_ref) | copy-start | bytes 786436
  62.5 29.2 %all-to-all-start = ((f32[4,32,32,128]{3,2,1,0:T(8,128)}), f32[4,32,32,128]{3,2,1,0:T(8,128)S(1)}, u32[]{:S(2)}, u32[]{:S(2)}) async-start(f32[4,32,32,128]{3,2,1,0:T(8,128)} %fusion), calls=%async_computation | async-start | bytes 4194304 | tf_op jit(solution)/shard_map/all_to_all | solution.py:29
  66.5 3.6 %copy-start.2 = (f32[4,4,8,256]{3,2,1,0:T(8,128)}, f32[4,4,8,256]{3,2,1,0:T(8,128)S(1)}, u32[]{:S(2)}) copy-start(f32[4,4,8,256]{3,2,1,0:T(8,128)S(1)} %reduce_window_sum.22.cumr_ref) | copy-start | bytes 393220
  92.0 14.3 %collective-permute-start.1 = (f32[32,32,128]{2,1,0:T(8,128)S(1)}, f32[32,32,128]{2,1,0:T(8,128)S(1)}, u32[]{:S(2)}, u32[]{:S(2)}) collective-permute-start(f32[32,32,128]{2,1,0:T(8,128)S(1)} %get-tuple-element.18), channel_id=1, source_target_pairs={{0,16},{4,20},{8,24},{12,28},{1,17},{5,21},{9,25},{13,29},{2,18},{... | collective-permute-start | bytes 1572872 | tf_op jit(solution)/shard_map/ppermute | solution.py:38
  108.1 14.3 %copy-start.3 = (f32[4,4,8,256]{3,2,1,0:T(8,128)S(1)}, f32[4,4,8,256]{3,2,1,0:T(8,128)}, u32[]{:S(2)}) copy-start(f32[4,4,8,256]{3,2,1,0:T(8,128)} %copy-done.2) | copy-start | bytes 393220
  108.1 40.0 %all-to-all-start.1 = ((f32[4,32,32,128]{3,2,1,0:T(8,128)}), f32[4,32,32,128]{3,2,1,0:T(8,128)S(1)}, u32[]{:S(2)}, u32[]{:S(2)}) async-start(f32[4,32,32,128]{3,2,1,0:T(8,128)} %pad_maximum_fusion), calls=%async_computation.1 | async-start | bytes 4194304 | tf_op jit(solution)/shard_map/all_to_all | solution.py:43
  148.0 1.0 copy-start
  174.8 5.9 %copy-start.5 = (f32[4096]{0:T(1024)S(1)}, f32[4096]{0:T(1024)}, u32[]{:S(2)}) copy-start(f32[4096]{0:T(1024)} %param.20) | copy-start | bytes 49156

commit v10 on v8

--- a/solution.py
+++ b/solution.py
@@ -63,7 +63,7 @@
     return jax.nn.silu(accum).astype(jnp.bfloat16)
 
 
-HEAD_GROUP = 8
+HEAD_GROUP = 16
 
 
 def silu(value):

time: 183 us -> 177 us (0.967)
  Pallas kernels: 67.9 us -> 59.2 us
  waiting for transfers between devices: 10.5 us -> 14.8 us
    all_to_all x1, waiting for transfers between devices: 0.01 us -> 4.32 us  [scan_states(): lax.all_to_all(jnp.stack(entries, axis=0), axis, 0, 0, tiled=True, axis_i...]
    pallas_call x1, Pallas kernels: 20 us -> 16.1 us  [intra_terms(): pl.pallas_call(intra_kernel, grid=(spans, heads // group), in_specs=[pl.B...]
    pallas_call x1, Pallas kernels: 25.8 us -> 22.5 us  [gate_terms(): pl.pallas_call(gate_kernel, grid=(groups, spans), in_specs=[pl.BlockSpec(...]
  transfers between devices with their start and end apart: 3 -> 3, of which waited for: 1 -> 2; matrix products, arithmetic and copies ran while one was open for 8% -> 7% of each run, Pallas kernels for 11% -> 9%
where the time goes in v10:
time: 177 us; the launch traced here: 176 us
  Pallas kernels  59.2 us (33%)
  blocking collectives  43.3 us (24%)
  starting transfers between devices  22.3 us (13%)
  other arithmetic  18.9 us (11%)
  local copies, waits for them, and re-layouts  16.6 us (9%)
  waiting for transfers between devices  14.8 us (8%)
    all_to_all x1, blocking collectives, scan_states(): lax.all_to_all(payload, axis, 0, 0, tiled=True, axis_index_groups=groups)  30.4 us
    pallas_call x1, Pallas kernels, gate_terms(): pl.pallas_call(gate_kernel, grid=(groups, spans), in_specs=[pl.BlockSpec(...  22.5 us
    pallas_call x1, Pallas kernels, block_states(): pl.pallas_call(state_kernel, grid=(spans, heads // group), in_specs=[pl.B...  20.6 us
    pallas_call x1, Pallas kernels, intra_terms(): pl.pallas_call(intra_kernel, grid=(spans, heads // group), in_specs=[pl.B...  16.1 us
    all_to_all x1, starting transfers between devices, scan_states(): lax.all_to_all(jnp.stack(entries, axis=0), axis, 0, 0, tiled=True, axis_i...  13.7 us
    ppermute x1, waiting for transfers between devices, scan_states(): earlier = lax.ppermute(running, axis, route)  10.5 us
    convert_element_type x1, other arithmetic, local(): return normed.astype(jnp.bfloat16)  9.98 us
    all_gather x1, blocking collectives, local(): bc_full = lax.all_gather(bc_local, 'ch', axis=1, tiled=True)  7.2 us
  transfers between devices with their start and end apart: 3, of which 2 were waited for; matrix products, arithmetic and copies ran while one was open for 7% of the time, Pallas kernels for 9%

profile of v10, /device:TPU:0, one launch (start us, length us, event | category | flops | bytes accessed | tf_op | source)
XLA Modules:
  0.0 176.0 jit_solution(12740828202473283639)
XLA Ops:
  1.6 0.9 constant_dynamic-slice_fusion.1
  2.5 5.0 %collective-permute-start = (bf16[3,4160]{1,0:T(4,128)(2,1)S(1)}, bf16[3,4160]{1,0:T(4,128)(2,1)S(1)}, u32[]{:S(2)}, u32[]{:S(2)}) collective-permute-start(bf16[3,4160]{1,0:T(4,128)(2,1)S(1)} %pad_maximum_fusion.3), channel_id=1, source_target_pairs={{0,4},{4,8},{8,12},{12,16},{16,20},{20,24},{24,28},{1,5},{5,9},{9,... | collective-permute-start | bytes 74888 | tf_op jit(solution)/shard_map/ppermute | solution.py:18
  8.2 1.1 fusion.13
  9.5 2.3 %reduce-window.6 = f32[4,32,2,128]{3,1,2,0:T(8,128)S(1)} reduce-window(f32[4,32,2,128]{3,1,2,0:T(8,128)S(1)} %copy.87, f32[]{:T(128)} %constant.47.clone.1), window={size=1x1x1x128 pad=0_0x0_0x0_0x127_0}, to_apply=%region_0.1 | reduce-window | flops 4161536 | bytes 262148 | tf_op jit(solution)/shard_map/reduce-window
  12.6 1.0 slice.167
  13.6 1.3 copy.97
  15.3 7.2 %all_gather.3 = bf16[1024,256]{0,1:T(8,128)(2,1)S(1)} all-gather(bf16[1024,64]{0,1:T(8,128)(2,1)S(1)} %multiply_convert_fusion.1), channel_id=1, replica_groups=mesh['seq'=8,'ch'=4] {'ch'}, dimensions={1}, use_global_device_ids=true | all-gather | bytes 655360 | tf_op jit(solution)/shard_map/all_gather | solution.py:307
  23.4 0.9 copy.95
  24.3 0.8 fusion.10.halo_ref
  25.2 20.6 %shard_map.109 = (f32[4,32,128,128]{3,2,1,0:T(8,128)}, bf16[1024,4096]{1,0:T(8,128)(2,1)}) custom-call(bf16[1024,4096]{1,0:T(8,128)(2,1)} %x_ref.1, bf16[4,8,4096]{2,1,0:T(8,128)(2,1)} %fusion.10.halo_ref, bf16[4,4096]{1,0:T(4,128)(2,1)} %taps_ref.1, bf16[4,128,256]{2,1,0:T(8,128)(2,1)} %bitcast.130, f32[4,2,256,16]{3,2,1,0:T(8,128)} %bitcast.124), custom_call_target="tpu_custom_call" | custom-call | flops 1073741824 | bytes 25165824 | tf_op jit(solution)/shard_map/pallas_call | solution.py:173
  45.7 4.1 %fusion.21 = (f32[1,32,128,128]{3,2,1,0:T(8,128)S(1)}, f32[1,32,128,128]{3,2,1,0:T(8,128)S(1)}, f32[1,32,128,128]{3,2,1,0:T(8,128)S(1)}, f32[1,32,128,128]{3,2,1,0:T(8,128)S(1)}) fusion(f32[4,32,128,128]{3,2,1,0:T(8,128)} %get-tuple-element.23.block_ref), kind=kLoop, calls=%fused_computation.68 | loop fusion | bytes 16777216 | tf_op jit(solution)/shard_map/slice | solution.py:338
  50.8 30.4 %all_to_all.10 = f32[4,33,32,128]{3,2,1,0:T(8,128)S(1)} all-to-all(f32[4,33,32,128]{3,2,1,0:T(8,128)S(1)} %pad_maximum_fusion), channel_id=1, replica_groups={{0,4,8,12},{16,20,24,28},{1,5,9,13},{17,21,25,29},{2,6,10,14},{18,22,26..., dimensions={0} | all-to-all | bytes 4325376 | tf_op jit(solution)/shard_map/all_to_all | solution.py:33
  81.5 3.6 %collective-permute-start.1 = (f32[32,32,128]{2,1,0:T(8,128)S(1)}, f32[32,32,128]{2,1,0:T(8,128)S(1)}, u32[]{:S(2)}, u32[]{:S(2)}) collective-permute-start(f32[32,32,128]{2,1,0:T(8,128)S(1)} %get-tuple-element.31), channel_id=1, source_target_pairs={{0,16},{4,20},{8,24},{12,28},{1,17},{5,21},{9,25},{13,29},{2,18},{... | collective-permute-start | bytes 1572872 | tf_op jit(solution)/shard_map/ppermute | solution.py:43
  85.1 10.5 %collective-permute-done.1 = f32[32,32,128]{2,1,0:T(8,128)S(1)} collective-permute-done((f32[32,32,128]{2,1,0:T(8,128)S(1)}, f32[32,32,128]{2,1,0:T(8,128)S(1)}, u32[]{:S(2)}, u32[]{:S(2)}) %collective-permute-start.1) | collective-permute-done | bytes 524320 | tf_op jit(solution)/shard_map/ppermute | solution.py:43
  95.8 1.5 pad_maximum_fusion.1
  97.4 13.7 %all-to-all-start.1 = ((f32[4,32,32,128]{3,2,1,0:T(8,128)}), f32[4,32,32,128]{3,2,1,0:T(8,128)S(1)}, u32[]{:S(2)}, u32[]{:S(2)}) async-start(f32[4,32,32,128]{3,2,1,0:T(8,128)} %pad_maximum_fusion.1), calls=%async_computation.1 | async-start | bytes 4194304 | tf_op jit(solution)/shard_map/all_to_all | solution.py:48
  112.7 1.3 copy.103
  114.1 1.2 copy.105
  115.4 0.8 copy.109.c_ref
  116.2 16.1 %shard_map.110.part_ref = f32[1024,4096]{1,0:T(8,128)} custom-call(f32[32]{0:T(128)} %skip_ref.1, bf16[1024,128]{1,0:T(8,128)(2,1)} %copy.109.c_ref, bf16[1024,128]{1,0:T(8,128)(2,1)} %copy-done.1, bf16[1024,4096]{1,0:T(8,128)(2,1)} %get-tuple-element.24.x_ref, f32[4,2,256,16]{3,2,1,0:T(8,128)} %bitcast.125, f32[4,2,16,256]{3,2,1,0:T(8,128)} %copy-done.2, ...), custom_call_target="tpu_custom_call" | custom-call | flops 2214592512 | bytes 25165824 | tf_op jit(solution)/shard_map/pallas_call | solution.py:203
  132.3 4.3 %all-to-all-done.1 = f32[4,32,32,128]{3,2,1,0:T(8,128)S(1)} async-done(((f32[4,32,32,128]{3,2,1,0:T(8,128)}), f32[4,32,32,128]{3,2,1,0:T(8,128)S(1)}, u32[]{:S(2)}, u32[]{:S(2)}) %all-to-all-start.1) | async-done | bytes 2097184 | tf_op jit(solution)/shard_map/all_to_all | solution.py:48
  137.6 22.5 %shard_map.111 = (f32[1024,4096]{1,0:T(8,128)}, f32[2,1024,1]{2,1,0:T(8,128)S(1)}) custom-call(f32[128]{0:T(128)S(1)} %exp.26.decay_ref, f32[1024,4096]{1,0:T(8,128)} %shard_map.110.part_ref, bf16[1024,128]{1,0:T(8,128)(2,1)S(1)} %copy-done, f32[4,32,128,128]{3,2,1,0:T(8,128)} %get-tuple-element.23.block_ref, f32[32,128,128]{2,1,0:T(8,128)S(1)} %bitcast.116, ...), custom_call_target="tpu_custom_call" | custom-call | flops 3221225472 | bytes 41943040 | tf_op jit(solution)/shard_map/pallas_call | solution.py:240
  160.3 5.7 %psum.7 = f32[1024]{0:T(1024)S(1)} all-reduce(f32[1024]{0:T(1024)S(1)} %reduce_sum.9), channel_id=1, replica_groups=mesh['seq'=8,'ch'=4] {'ch'}, use_global_device_ids=true, to_apply=%region_3.4 | all-reduce | flops 1024 | bytes 8192 | tf_op jit(solution)/shard_map/psum | solution.py:369
  166.0 10.0 %multiply_convert_fusion = bf16[1024,4096]{1,0:T(8,128)(2,1)} fusion(f32[1024,4096]{1,0:T(8,128)} %get-tuple-element.25, f32[1024]{0:T(1024)S(1)} %fusion.16, f32[4096]{0:T(1024)S(1)} %copy-done.5, f32[1024]{0:T(1024)S(1)} %add_rsqrt_fusion), kind=kLoop, calls=%fused_computation | loop fusion | flops 16777216 | bytes 25190400 | tf_op jit(solution)/shard_map/convert_element_type | solution.py:372
  (58 shorter events, 8.3 us)
Async XLA Ops:
  0.0 12.6 %copy-start.6 = (bf16[4,64]{1,0:T(4,128)(2,1)S(1)}, bf16[4,64]{1,0:T(4,128)(2,1)}, u32[]{:S(2)}) copy-start(bf16[4,64]{1,0:T(4,128)(2,1)} %param.21) | copy-start | bytes 1540
  2.5 12.6 %copy-start.4 = (bf16[1024,64]{0,1:T(8,128)(2,1)S(1)}, bf16[1024,64]{0,1:T(8,128)(2,1)}, u32[]{:S(2)}) copy-start(bf16[1024,64]{0,1:T(8,128)(2,1)} %param.15) | copy-start | bytes 393220
  2.5 12.4 %collective-permute-start = (bf16[3,4160]{1,0:T(4,128)(2,1)S(1)}, bf16[3,4160]{1,0:T(4,128)(2,1)S(1)}, u32[]{:S(2)}, u32[]{:S(2)}) collective-permute-start(bf16[3,4160]{1,0:T(4,128)(2,1)S(1)} %pad_maximum_fusion.3), channel_id=1, source_target_pairs={{0,4},{4,8},{8,12},{12,16},{16,20},{20,24},{24,28},{1,5},{5,9},{9,... | collective-permute-start | bytes 74888 | tf_op jit(solution)/shard_map/ppermute | solution.py:18
  23.4 22.3 %copy-start.1 = (bf16[1024,128]{1,0:T(8,128)(2,1)}, bf16[1024,128]{1,0:T(8,128)(2,1)S(1)}, u32[]{:S(2)}) copy-start(bf16[1024,128]{1,0:T(8,128)(2,1)S(1)} %copy.110.b_ref) | copy-start | bytes 786436
  81.5 14.1 %collective-permute-start.1 = (f32[32,32,128]{2,1,0:T(8,128)S(1)}, f32[32,32,128]{2,1,0:T(8,128)S(1)}, u32[]{:S(2)}, u32[]{:S(2)}) collective-permute-start(f32[32,32,128]{2,1,0:T(8,128)S(1)} %get-tuple-element.31), channel_id=1, source_target_pairs={{0,16},{4,20},{8,24},{12,28},{1,17},{5,21},{9,25},{13,29},{2,18},{... | collective-permute-start | bytes 1572872 | tf_op jit(solution)/shard_map/ppermute | solution.py:43
  97.4 39.3 %all-to-all-start.1 = ((f32[4,32,32,128]{3,2,1,0:T(8,128)}), f32[4,32,32,128]{3,2,1,0:T(8,128)S(1)}, u32[]{:S(2)}, u32[]{:S(2)}) async-start(f32[4,32,32,128]{3,2,1,0:T(8,128)} %pad_maximum_fusion.1), calls=%async_computation.1 | async-start | bytes 4194304 | tf_op jit(solution)/shard_map/all_to_all | solution.py:48
  111.0 4.4 %copy-start.3 = (bf16[1024,128]{0,1:T(8,128)(2,1)S(1)}, bf16[1024,128]{0,1:T(8,128)(2,1)}, u32[]{:S(2)}) copy-start(bf16[1024,128]{0,1:T(8,128)(2,1)} %get-tuple-element.46) | copy-start | bytes 786436
  112.0 4.2 %copy-start.2 = (f32[4,2,16,256]{3,2,1,0:T(8,128)}, f32[4,2,16,256]{3,2,1,0:T(8,128)S(1)}, u32[]{:S(2)}) copy-start(f32[4,2,16,256]{3,2,1,0:T(8,128)S(1)} %reduce_window_sum.22.cumr_ref) | copy-start | bytes 393220
  136.7 1.0 copy-start
  137.6 28.4 %copy-start.5 = (f32[4096]{0:T(1024)S(1)}, f32[4096]{0:T(1024)}, u32[]{:S(2)}) copy-start(f32[4096]{0:T(1024)} %param.22) | copy-start | bytes 49156

commit v11 on v10

--- a/solution.py
+++ b/solution.py
@@ -63,7 +63,7 @@
     return jax.nn.silu(accum).astype(jnp.bfloat16)
 
 
-HEAD_GROUP = 16
+HEAD_GROUP = 32
 
 
 def silu(value):
@@ -188,6 +188,7 @@
             jax.ShapeDtypeStruct((spans, heads, size, width), jnp.float32),
             jax.ShapeDtypeStruct((rows, heads * width), jnp.bfloat16),
         ],
+        compiler_params=pltpu.CompilerParams(vmem_limit_bytes=60 * 1024 * 1024),
         cost_estimate=pl.CostEstimate(
             flops=2 * rows * heads * width * size,
             bytes_accessed=rows * heads * width * 4 + spans * heads * size * width * 4,
@@ -214,6 +215,7 @@
         ],
         out_specs=pl.BlockSpec((SEGMENT_LENGTH, group * width), lambda c, g: (c, g)),
         out_shape=jax.ShapeDtypeStruct((rows, heads * width), jnp.float32),
+        compiler_params=pltpu.CompilerParams(vmem_limit_bytes=60 * 1024 * 1024),
         cost_estimate=pl.CostEstimate(
             flops=2 * rows * SEGMENT_LENGTH * (heads * width + size),
             bytes_accessed=rows * heads * width * 6,
@@ -257,7 +259,7 @@
             jax.ShapeDtypeStruct((rows, heads * width), jnp.float32),
             jax.ShapeDtypeStruct((groups, rows, 1), jnp.float32),
         ],
-        compiler_params=pltpu.CompilerParams(vmem_limit_bytes=48 * 1024 * 1024),
+        compiler_params=pltpu.CompilerParams(vmem_limit_bytes=60 * 1024 * 1024),
         cost_estimate=pl.CostEstimate(
             flops=6 * rows * size * heads * width,
             bytes_accessed=rows * heads * width * 10,

time: 177 us -> 178 us (level)
  waiting for transfers between devices: 14.8 us -> 17.3 us
    all_to_all x1, waiting for transfers between devices: 4.32 us -> 6.8 us  [scan_states(): lax.all_to_all(jnp.stack(entries, axis=0), axis, 0, 0, tiled=True, axis_i...]
    exp x2 -> x0, local copies, waits for them, and re-layouts: 1.95 us -> none  [local(): jnp.exp(cum_heads[:, heads])]
    transpose x0 -> x2, local copies, waits for them, and re-layouts: none -> 1.89 us  [columns_by_group(): return by_group(values, spans, heads).transpose(0, 1, 3, 2)]
  transfers between devices with their start and end apart: 3 -> 3, of which waited for: 2 -> 2; matrix products, arithmetic and copies ran while one was open for 7% -> 6% of each run, Pallas kernels for 9% -> 8%
where the time goes in v11:
time: 178 us; the launch traced here: 177 us
  Pallas kernels  58.3 us (33%)
  blocking collectives  43.3 us (24%)
  starting transfers between devices  22.2 us (12%)
  other arithmetic  19.9 us (11%)
  waiting for transfers between devices  17.3 us (10%)
  local copies, waits for them, and re-layouts  15.3 us (9%)
    all_to_all x1, blocking collectives, scan_states(): lax.all_to_all(payload, axis, 0, 0, tiled=True, axis_index_groups=groups)  30.4 us
    pallas_call x1, Pallas kernels, gate_terms(): pl.pallas_call(gate_kernel, grid=(groups, spans), in_specs=[pl.BlockSpec(...  22.5 us
    pallas_call x1, Pallas kernels, block_states(): pl.pallas_call(state_kernel, grid=(spans, heads // group), in_specs=[pl.B...  21 us
    pallas_call x1, Pallas kernels, intra_terms(): pl.pallas_call(intra_kernel, grid=(spans, heads // group), in_specs=[pl.B...  14.8 us
    all_to_all x1, starting transfers between devices, scan_states(): lax.all_to_all(jnp.stack(entries, axis=0), axis, 0, 0, tiled=True, axis_i...  13.7 us
    ppermute x1, waiting for transfers between devices, scan_states(): earlier = lax.ppermute(running, axis, route)  10.5 us
    convert_element_type x1, other arithmetic, local(): return normed.astype(jnp.bfloat16)  9.96 us
    all_gather x1, blocking collectives, local(): bc_full = lax.all_gather(bc_local, 'ch', axis=1, tiled=True)  7.2 us
  transfers between devices with their start and end apart: 3, of which 2 were waited for; matrix products, arithmetic and copies ran while one was open for 6% of the time, Pallas kernels for 8%

profile of v11, /device:TPU:0, one launch (start us, length us, event | category | flops | bytes accessed | tf_op | source)
XLA Modules:
  0.0 177.1 jit_solution(4062519921416989294)
XLA Ops:
  1.6 0.9 constant_dynamic-slice_fusion.1
  2.5 4.9 %collective-permute-start = (bf16[3,4160]{1,0:T(4,128)(2,1)S(1)}, bf16[3,4160]{1,0:T(4,128)(2,1)S(1)}, u32[]{:S(2)}, u32[]{:S(2)}) collective-permute-start(bf16[3,4160]{1,0:T(4,128)(2,1)S(1)} %pad_maximum_fusion.3), channel_id=1, source_target_pairs={{0,4},{4,8},{8,12},{12,16},{16,20},{20,24},{24,28},{1,5},{5,9},{9,... | collective-permute-start | bytes 74888 | tf_op jit(solution)/shard_map/ppermute | solution.py:18
  8.1 1.1 fusion.13
  9.4 2.3 %reduce-window.6 = f32[4,32,2,128]{3,1,2,0:T(8,128)S(1)} reduce-window(f32[4,32,2,128]{3,1,2,0:T(8,128)S(1)} %copy.43, f32[]{:T(128)} %constant.47.clone.1), window={size=1x1x1x128 pad=0_0x0_0x0_0x127_0}, to_apply=%region_0.1 | reduce-window | flops 4161536 | bytes 262148 | tf_op jit(solution)/shard_map/reduce-window
  12.5 1.0 slice.167
  13.5 1.0 copy.53.toend_ref
  14.9 7.2 %all_gather.3 = bf16[1024,256]{0,1:T(8,128)(2,1)S(1)} all-gather(bf16[1024,64]{0,1:T(8,128)(2,1)S(1)} %multiply_convert_fusion.1), channel_id=1, replica_groups=mesh['seq'=8,'ch'=4] {'ch'}, dimensions={1}, use_global_device_ids=true | all-gather | bytes 655360 | tf_op jit(solution)/shard_map/all_gather | solution.py:309
  22.3 0.9 copy.51
  24.0 21.0 %shard_map.109 = (f32[4,32,128,128]{3,2,1,0:T(8,128)}, bf16[1024,4096]{1,0:T(8,128)(2,1)}) custom-call(bf16[1024,4096]{1,0:T(8,128)(2,1)} %x_ref.1, bf16[4,8,4096]{2,1,0:T(8,128)(2,1)} %fusion.10.halo_ref, bf16[4,4096]{1,0:T(4,128)(2,1)} %taps_ref.1, bf16[4,128,256]{2,1,0:T(8,128)(2,1)} %bitcast.144, f32[4,1,256,32]{3,2,1,0:T(8,128)} %copy.53.toend_ref), custom_call_target="tpu_custom_call" | custom-call | flops 1073741824 | bytes 25165824 | tf_op jit(solution)/shard_map/pallas_call | solution.py:173
  45.1 4.1 %fusion.23 = (f32[1,32,128,128]{3,2,1,0:T(8,128)S(1)}, f32[1,32,128,128]{3,2,1,0:T(8,128)S(1)}, f32[1,32,128,128]{3,2,1,0:T(8,128)S(1)}, f32[1,32,128,128]{3,2,1,0:T(8,128)S(1)}) fusion(f32[4,32,128,128]{3,2,1,0:T(8,128)} %get-tuple-element.23.block_ref), kind=kLoop, calls=%fused_computation.71 | loop fusion | bytes 16777216 | tf_op jit(solution)/shard_map/slice | solution.py:340
  50.2 30.4 %all_to_all.10 = f32[4,33,32,128]{3,2,1,0:T(8,128)S(1)} all-to-all(f32[4,33,32,128]{3,2,1,0:T(8,128)S(1)} %pad_maximum_fusion), channel_id=1, replica_groups={{0,4,8,12},{16,20,24,28},{1,5,9,13},{17,21,25,29},{2,6,10,14},{18,22,26..., dimensions={0} | all-to-all | bytes 4325376 | tf_op jit(solution)/shard_map/all_to_all | solution.py:33
  80.8 3.6 %collective-permute-start.1 = (f32[32,32,128]{2,1,0:T(8,128)S(1)}, f32[32,32,128]{2,1,0:T(8,128)S(1)}, u32[]{:S(2)}, u32[]{:S(2)}) collective-permute-start(f32[32,32,128]{2,1,0:T(8,128)S(1)} %get-tuple-element.31), channel_id=1, source_target_pairs={{0,16},{4,20},{8,24},{12,28},{1,17},{5,21},{9,25},{13,29},{2,18},{... | collective-permute-start | bytes 1572872 | tf_op jit(solution)/shard_map/ppermute | solution.py:43
  84.5 10.5 %collective-permute-done.1 = f32[32,32,128]{2,1,0:T(8,128)S(1)} collective-permute-done((f32[32,32,128]{2,1,0:T(8,128)S(1)}, f32[32,32,128]{2,1,0:T(8,128)S(1)}, u32[]{:S(2)}, u32[]{:S(2)}) %collective-permute-start.1) | collective-permute-done | bytes 524320 | tf_op jit(solution)/shard_map/ppermute | solution.py:43
  95.2 1.5 pad_maximum_fusion.1
  96.7 13.7 %all-to-all-start.1 = ((f32[4,32,32,128]{3,2,1,0:T(8,128)}), f32[4,32,32,128]{3,2,1,0:T(8,128)S(1)}, u32[]{:S(2)}, u32[]{:S(2)}) async-start(f32[4,32,32,128]{3,2,1,0:T(8,128)} %pad_maximum_fusion.1), calls=%async_computation.1 | async-start | bytes 4194304 | tf_op jit(solution)/shard_map/all_to_all | solution.py:48
  112.0 0.9 copy.59.cumr_ref
  112.9 0.9 exponential_bitcast_fusion.ecum_ref
  114.6 14.8 %shard_map.110.part_ref = f32[1024,4096]{1,0:T(8,128)} custom-call(f32[32]{0:T(128)} %skip_ref.1, bf16[1024,128]{1,0:T(8,128)(2,1)} %copy.62.c_ref, bf16[1024,128]{1,0:T(8,128)(2,1)} %copy-done.1, bf16[1024,4096]{1,0:T(8,128)(2,1)} %get-tuple-element.24.x_ref, f32[4,1,256,32]{3,2,1,0:T(8,128)} %bitcast.134, f32[4,1,32,256]{3,2,1,0:T(8,128)} %copy.59.cumr_ref, ...), custom_call_target="tpu_custom_call" | custom-call | flops 2214592512 | bytes 25165824 | tf_op jit(solution)/shard_map/pallas_call | solution.py:204
  129.4 6.8 %all-to-all-done.1 = f32[4,32,32,128]{3,2,1,0:T(8,128)S(1)} async-done(((f32[4,32,32,128]{3,2,1,0:T(8,128)}), f32[4,32,32,128]{3,2,1,0:T(8,128)S(1)}, u32[]{:S(2)}, u32[]{:S(2)}) %all-to-all-start.1) | async-done | bytes 2097184 | tf_op jit(solution)/shard_map/all_to_all | solution.py:48
  136.2 1.6 copy.60
  137.8 22.5 %shard_map.111 = (f32[1024,4096]{1,0:T(8,128)}, f32[1,1024,1]{2,1,0:T(8,128)}) custom-call(f32[128]{0:T(128)} %exp.32.decay_ref, f32[1024,4096]{1,0:T(8,128)} %shard_map.110.part_ref, bf16[1024,128]{1,0:T(8,128)(2,1)} %copy.62.c_ref, f32[4,32,128,128]{3,2,1,0:T(8,128)} %get-tuple-element.23.block_ref, f32[32,128,128]{2,1,0:T(8,128)} %bitcast.131, ...), custom_call_target="tpu_custom_call" | custom-call | flops 3221225472 | bytes 41943040 | tf_op jit(solution)/shard_map/pallas_call | solution.py:242
  160.2 1.2 reduce.4
  161.5 5.7 %psum.7 = f32[1024]{0:T(1024)S(1)} all-reduce(f32[1024]{0:T(1024)S(1)} %reduce.4), channel_id=1, replica_groups=mesh['seq'=8,'ch'=4] {'ch'}, use_global_device_ids=true, to_apply=%region_2.3 | all-reduce | flops 1024 | bytes 8192 | tf_op jit(solution)/shard_map/psum | solution.py:371
  167.2 10.0 %multiply_convert_fusion = bf16[1024,4096]{1,0:T(8,128)(2,1)} fusion(f32[1024,4096]{1,0:T(8,128)} %get-tuple-element.25, f32[1024]{0:T(1024)S(1)} %fusion.18, f32[4096]{0:T(1024)S(1)} %copy-done.3, f32[1024]{0:T(1024)S(1)} %add_rsqrt_fusion), kind=kLoop, calls=%fused_computation | loop fusion | flops 16777216 | bytes 25190400 | tf_op jit(solution)/shard_map/convert_element_type | solution.py:374
  (52 shorter events, 8.0 us)
Async XLA Ops:
  0.0 14.6 %copy-start.2 = (bf16[1024,64]{0,1:T(8,128)(2,1)S(1)}, bf16[1024,64]{0,1:T(8,128)(2,1)}, u32[]{:S(2)}) copy-start(bf16[1024,64]{0,1:T(8,128)(2,1)} %param.15) | copy-start | bytes 393220
  0.0 12.5 %copy-start.4 = (bf16[4,64]{1,0:T(4,128)(2,1)S(1)}, bf16[4,64]{1,0:T(4,128)(2,1)}, u32[]{:S(2)}) copy-start(bf16[4,64]{1,0:T(4,128)(2,1)} %param.21) | copy-start | bytes 1540
  2.5 12.0 %collective-permute-start = (bf16[3,4160]{1,0:T(4,128)(2,1)S(1)}, bf16[3,4160]{1,0:T(4,128)(2,1)S(1)}, u32[]{:S(2)}, u32[]{:S(2)}) collective-permute-start(bf16[3,4160]{1,0:T(4,128)(2,1)S(1)} %pad_maximum_fusion.3), channel_id=1, source_target_pairs={{0,4},{4,8},{8,12},{12,16},{16,20},{20,24},{24,28},{1,5},{5,9},{9,... | collective-permute-start | bytes 74888 | tf_op jit(solution)/shard_map/ppermute | solution.py:18
  22.3 22.8 %copy-start.1 = (bf16[1024,128]{1,0:T(8,128)(2,1)}, bf16[1024,128]{1,0:T(8,128)(2,1)S(1)}, u32[]{:S(2)}) copy-start(bf16[1024,128]{1,0:T(8,128)(2,1)S(1)} %copy.63.b_ref) | copy-start | bytes 786436
  80.8 14.1 %collective-permute-start.1 = (f32[32,32,128]{2,1,0:T(8,128)S(1)}, f32[32,32,128]{2,1,0:T(8,128)S(1)}, u32[]{:S(2)}, u32[]{:S(2)}) collective-permute-start(f32[32,32,128]{2,1,0:T(8,128)S(1)} %get-tuple-element.31), channel_id=1, source_target_pairs={{0,16},{4,20},{8,24},{12,28},{1,17},{5,21},{9,25},{13,29},{2,18},{... | collective-permute-start | bytes 1572872 | tf_op jit(solution)/shard_map/ppermute | solution.py:43
  96.7 39.5 %all-to-all-start.1 = ((f32[4,32,32,128]{3,2,1,0:T(8,128)}), f32[4,32,32,128]{3,2,1,0:T(8,128)S(1)}, u32[]{:S(2)}, u32[]{:S(2)}) async-start(f32[4,32,32,128]{3,2,1,0:T(8,128)} %pad_maximum_fusion.1), calls=%async_computation.1 | async-start | bytes 4194304 | tf_op jit(solution)/shard_map/all_to_all | solution.py:48
  112.0 2.6 %copy-start = (f32[4,32,2,128]{1,3,2,0:T(8,128)}, f32[4,32,2,128]{1,3,2,0:T(8,128)S(1)}, u32[]{:S(2)}) copy-start(f32[4,32,2,128]{1,3,2,0:T(8,128)S(1)} %copy.58) | copy-start | bytes 393220
  137.8 29.4 %copy-start.3 = (f32[4096]{0:T(1024)S(1)}, f32[4096]{0:T(1024)}, u32[]{:S(2)}) copy-start(f32[4096]{0:T(1024)} %param.22) | copy-start | bytes 49156

commit v12 on v10

--- a/solution.py
+++ b/solution.py
@@ -154,6 +154,33 @@
         out_ref[:, columns] = gated
         total = total + gated * gated
     sq_ref[0] = jnp.sum(total, axis=1, keepdims=True)
+
+
+def scale_kernel(gated_ref, scale_ref, gain_ref, live_ref, out_ref):
+    out_ref[...] = (
+        gated_ref[...] * scale_ref[...] * gain_ref[...] * live_ref[...]
+    ).astype(jnp.bfloat16)
+
+
+def scaled_output(gated, scale, gain, live):
+    rows, channels = gated.shape
+    tile = 128
+    return pl.pallas_call(
+        scale_kernel,
+        grid=(rows // tile,),
+        in_specs=[
+            pl.BlockSpec((tile, channels), lambda r: (r, 0)),
+            pl.BlockSpec((tile, 1), lambda r: (r, 0)),
+            pl.BlockSpec((1, channels), lambda r: (0, 0)),
+            pl.BlockSpec((tile, 1), lambda r: (r, 0)),
+        ],
+        out_specs=pl.BlockSpec((tile, channels), lambda r: (r, 0)),
+        out_shape=jax.ShapeDtypeStruct((rows, channels), jnp.bfloat16),
+        compiler_params=pltpu.CompilerParams(vmem_limit_bytes=48 * 1024 * 1024),
+        cost_estimate=pl.CostEstimate(
+            flops=3 * rows * channels, bytes_accessed=6 * rows * channels, transcendentals=0
+        ),
+    )(gated, scale[:, None], gain[None, :], live[:, None])
 
 
 def by_group(values, spans, heads):
@@ -368,8 +395,7 @@
     gated = jnp.concatenate(gated_parts, axis=1)
     square_sum = lax.psum(square_part[:, 0], "ch")
     mean_sq = square_sum / INNER
-    normed = gated * lax.rsqrt(mean_sq + 1e-05)[:, None] * norm_gain[None, :] * row_valid[:, None]
-    return normed.astype(jnp.bfloat16)
+    return scaled_output(gated, lax.rsqrt(mean_sq + 1e-05), norm_gain, row_valid)
 
 
 def solution(mesh):

time: 177 us -> 180 us (1.017)
  Pallas kernels: 59.2 us -> 71 us
  other arithmetic: 18.9 us -> 8.91 us
  waiting for transfers between devices: 14.8 us -> 17.2 us
    pallas_call x0 -> x1, Pallas kernels: none -> 12 us  [scaled_output(): pl.pallas_call(scale_kernel, grid=(rows // tile,), in_specs=[pl.BlockSpec...]
    convert_element_type x1 -> x0, other arithmetic: 9.98 us -> none  [local(): return normed.astype(jnp.bfloat16)]
    all_to_all x1, waiting for transfers between devices: 4.32 us -> 6.77 us  [scan_states(): lax.all_to_all(jnp.stack(entries, axis=0), axis, 0, 0, tiled=True, axis_i...]
  transfers between devices with their start and end apart: 3 -> 3, of which waited for: 2 -> 2; matrix products, arithmetic and copies ran while one was open for 7% -> 6% of each run, Pallas kernels for 9% -> 9%
where the time goes in v12:
time: 180 us; the launch traced here: 179 us
  Pallas kernels  71 us (39%)
  blocking collectives  43.3 us (24%)
  starting transfers between devices  22.3 us (12%)
  waiting for transfers between devices  17.2 us (10%)
  local copies, waits for them, and re-layouts  15.5 us (9%)
  other arithmetic  8.91 us (5%)
    all_to_all x1, blocking collectives, scan_states(): lax.all_to_all(payload, axis, 0, 0, tiled=True, axis_index_groups=groups)  30.4 us
    pallas_call x1, Pallas kernels, gate_terms(): pl.pallas_call(gate_kernel, grid=(groups, spans), in_specs=[pl.BlockSpec(...  22.4 us
    pallas_call x1, Pallas kernels, block_states(): pl.pallas_call(state_kernel, grid=(spans, heads // group), in_specs=[pl.B...  20.6 us
    pallas_call x1, Pallas kernels, intra_terms(): pl.pallas_call(intra_kernel, grid=(spans, heads // group), in_specs=[pl.B...  16.1 us
    all_to_all x1, starting transfers between devices, scan_states(): lax.all_to_all(jnp.stack(entries, axis=0), axis, 0, 0, tiled=True, axis_i...  13.6 us
    pallas_call x1, Pallas kernels, scaled_output(): pl.pallas_call(scale_kernel, grid=(rows // tile,), in_specs=[pl.BlockSpec...  12 us
    ppermute x1, waiting for transfers between devices, scan_states(): earlier = lax.ppermute(running, axis, route)  10.5 us
    all_gather x1, blocking collectives, local(): bc_full = lax.all_gather(bc_local, 'ch', axis=1, tiled=True)  7.2 us
  transfers between devices with their start and end apart: 3, of which 2 were waited for; matrix products, arithmetic and copies ran while one was open for 6% of the time, Pallas kernels for 9%

profile of v12, /device:TPU:0, one launch (start us, length us, event | category | flops | bytes accessed | tf_op | source)
XLA Modules:
  0.0 179.3 jit_solution(12150671279709933969)
XLA Ops:
  0.7 0.9 constant_dynamic-slice_fusion.1
  2.5 5.0 %collective-permute-start = (bf16[3,4160]{1,0:T(4,128)(2,1)S(1)}, bf16[3,4160]{1,0:T(4,128)(2,1)S(1)}, u32[]{:S(2)}, u32[]{:S(2)}) collective-permute-start(bf16[3,4160]{1,0:T(4,128)(2,1)S(1)} %pad_maximum_fusion.3), channel_id=1, source_target_pairs={{0,4},{4,8},{8,12},{12,16},{16,20},{20,24},{24,28},{1,5},{5,9},{9,... | collective-permute-start | bytes 74888 | tf_op jit(solution)/shard_map/ppermute | solution.py:18
  7.5 1.1 fusion.14
  9.5 2.3 %reduce-window.6 = f32[4,32,2,128]{3,1,2,0:T(8,128)S(1)} reduce-window(f32[4,32,2,128]{3,1,2,0:T(8,128)S(1)} %copy.90, f32[]{:T(128)} %constant.47.clone.1), window={size=1x1x1x128 pad=0_0x0_0x0_0x127_0}, to_apply=%region_0.1 | reduce-window | flops 4161536 | bytes 262148 | tf_op jit(solution)/shard_map/reduce-window
  12.6 1.3 copy.100
  13.9 1.0 slice.167
  15.3 7.2 %all_gather.3 = bf16[1024,256]{0,1:T(8,128)(2,1)S(1)} all-gather(bf16[1024,64]{0,1:T(8,128)(2,1)S(1)} %multiply_convert_fusion), channel_id=1, replica_groups=mesh['seq'=8,'ch'=4] {'ch'}, dimensions={1}, use_global_device_ids=true | all-gather | bytes 655360 | tf_op jit(solution)/shard_map/all_gather | solution.py:334
  22.8 0.9 copy.98
  23.6 0.8 fusion.11.halo_ref
  24.5 20.6 %shard_map.109 = (f32[4,32,128,128]{3,2,1,0:T(8,128)}, bf16[1024,4096]{1,0:T(8,128)(2,1)}) custom-call(bf16[1024,4096]{1,0:T(8,128)(2,1)} %x_ref.1, bf16[4,8,4096]{2,1,0:T(8,128)(2,1)} %fusion.11.halo_ref, bf16[4,4096]{1,0:T(4,128)(2,1)} %taps_ref.1, bf16[4,128,256]{2,1,0:T(8,128)(2,1)} %bitcast.132, f32[4,2,256,16]{3,2,1,0:T(8,128)} %bitcast.126), custom_call_target="tpu_custom_call" | custom-call | flops 1073741824 | bytes 25165824 | tf_op jit(solution)/shard_map/pallas_call | solution.py:200
  45.0 4.1 %fusion.22 = (f32[1,32,128,128]{3,2,1,0:T(8,128)S(1)}, f32[1,32,128,128]{3,2,1,0:T(8,128)S(1)}, f32[1,32,128,128]{3,2,1,0:T(8,128)S(1)}, f32[1,32,128,128]{3,2,1,0:T(8,128)S(1)}) fusion(f32[4,32,128,128]{3,2,1,0:T(8,128)} %get-tuple-element.23.block_ref), kind=kLoop, calls=%fused_computation.69 | loop fusion | bytes 16777216 | tf_op jit(solution)/shard_map/slice | solution.py:365
  50.2 30.4 %all_to_all.10 = f32[4,33,32,128]{3,2,1,0:T(8,128)S(1)} all-to-all(f32[4,33,32,128]{3,2,1,0:T(8,128)S(1)} %pad_maximum_fusion), channel_id=1, replica_groups={{0,4,8,12},{16,20,24,28},{1,5,9,13},{17,21,25,29},{2,6,10,14},{18,22,26..., dimensions={0} | all-to-all | bytes 4325376 | tf_op jit(solution)/shard_map/all_to_all | solution.py:33
  80.8 3.6 %collective-permute-start.1 = (f32[32,32,128]{2,1,0:T(8,128)S(1)}, f32[32,32,128]{2,1,0:T(8,128)S(1)}, u32[]{:S(2)}, u32[]{:S(2)}) collective-permute-start(f32[32,32,128]{2,1,0:T(8,128)S(1)} %get-tuple-element.31), channel_id=1, source_target_pairs={{0,16},{4,20},{8,24},{12,28},{1,17},{5,21},{9,25},{13,29},{2,18},{... | collective-permute-start | bytes 1572872 | tf_op jit(solution)/shard_map/ppermute | solution.py:43
  84.4 10.5 %collective-permute-done.1 = f32[32,32,128]{2,1,0:T(8,128)S(1)} collective-permute-done((f32[32,32,128]{2,1,0:T(8,128)S(1)}, f32[32,32,128]{2,1,0:T(8,128)S(1)}, u32[]{:S(2)}, u32[]{:S(2)}) %collective-permute-start.1) | collective-permute-done | bytes 524320 | tf_op jit(solution)/shard_map/ppermute | solution.py:43
  95.2 1.5 pad_maximum_fusion.1
  96.6 13.6 %all-to-all-start.1 = ((f32[4,32,32,128]{3,2,1,0:T(8,128)}), f32[4,32,32,128]{3,2,1,0:T(8,128)}, u32[]{:S(2)}, u32[]{:S(2)}) async-start(f32[4,32,32,128]{3,2,1,0:T(8,128)} %pad_maximum_fusion.1), calls=%async_computation.1 | async-start | bytes 4194304 | tf_op jit(solution)/shard_map/all_to_all | solution.py:48
  111.3 1.4 copy.106
  113.2 0.8 copy.113.c_ref
  114.0 16.1 %shard_map.110.part_ref = f32[1024,4096]{1,0:T(8,128)} custom-call(f32[32]{0:T(128)} %skip_ref.1, bf16[1024,128]{1,0:T(8,128)(2,1)} %copy.113.c_ref, bf16[1024,128]{1,0:T(8,128)(2,1)} %copy-done.2, bf16[1024,4096]{1,0:T(8,128)(2,1)} %get-tuple-element.24.x_ref, f32[4,2,256,16]{3,2,1,0:T(8,128)} %bitcast.127, f32[4,2,16,256]{3,2,1,0:T(8,128)} %copy-done.3, ...), custom_call_target="tpu_custom_call" | custom-call | flops 2214592512 | bytes 25165824 | tf_op jit(solution)/shard_map/pallas_call | solution.py:230
  130.1 6.8 %all-to-all-done.1 = f32[4,32,32,128]{3,2,1,0:T(8,128)} async-done(((f32[4,32,32,128]{3,2,1,0:T(8,128)}), f32[4,32,32,128]{3,2,1,0:T(8,128)}, u32[]{:S(2)}, u32[]{:S(2)}) %all-to-all-start.1) | async-done | bytes 2097184 | tf_op jit(solution)/shard_map/all_to_all | solution.py:48
  136.9 1.9 %copy.107 = f32[32,4,32,128]{3,2,1,0:T(8,128)S(1)} copy(f32[32,4,32,128]{3,2,0,1:T(8,128)} %bitcast.37) | data formatting | bytes 4194304 | tf_op jit(solution)/shard_map/transpose | solution.py:51
  138.8 22.4 %shard_map.111 = (f32[1024,4096]{1,0:T(8,128)}, f32[2,1024,1]{2,1,0:T(8,128)S(1)}) custom-call(f32[128]{0:T(128)S(1)} %exp.26.decay_ref, f32[1024,4096]{1,0:T(8,128)} %shard_map.110.part_ref, bf16[1024,128]{1,0:T(8,128)(2,1)S(1)} %copy-done, f32[4,32,128,128]{3,2,1,0:T(8,128)} %get-tuple-element.23.block_ref, f32[32,128,128]{2,1,0:T(8,128)S(1)} %bitcast.118, ...), custom_call_target="tpu_custom_call" | custom-call | flops 3221225472 | bytes 41943040 | tf_op jit(solution)/shard_map/pallas_call | solution.py:267
  161.4 5.7 %psum.7 = f32[1024]{0:T(1024)S(1)} all-reduce(f32[1024]{0:T(1024)S(1)} %reduce_sum.9), channel_id=1, replica_groups=mesh['seq'=8,'ch'=4] {'ch'}, use_global_device_ids=true, to_apply=%region_3.4 | all-reduce | flops 1024 | bytes 8192 | tf_op jit(solution)/shard_map/psum | solution.py:396
  167.3 12.0 %shard_map.112 = bf16[1024,4096]{1,0:T(8,128)(2,1)} custom-call(f32[1024,4096]{1,0:T(8,128)} %get-tuple-element.25.gated_ref, f32[1024,1]{1,0:T(8,128)S(1)} %copy.109.scale_ref, f32[1,4096]{1,0:T(1,128)S(1)} %bitcast.120, f32[1024,1]{1,0:T(8,128)S(1)} %fusion.10.live_ref), custom_call_target="tpu_custom_call" | custom-call | flops 12582912 | bytes 25165824 | tf_op jit(solution)/shard_map/pallas_call | solution.py:168
  (58 shorter events, 6.6 us)
Async XLA Ops:
  0.0 12.6 %copy-start.5 = (bf16[4,64]{1,0:T(4,128)(2,1)S(1)}, bf16[4,64]{1,0:T(4,128)(2,1)}, u32[]{:S(2)}) copy-start(bf16[4,64]{1,0:T(4,128)(2,1)} %param.21) | copy-start | bytes 1540
  2.5 12.6 %copy-start.4 = (bf16[1024,64]{0,1:T(8,128)(2,1)S(1)}, bf16[1024,64]{0,1:T(8,128)(2,1)}, u32[]{:S(2)}) copy-start(bf16[1024,64]{0,1:T(8,128)(2,1)} %param.15) | copy-start | bytes 393220
  2.5 12.4 %collective-permute-start = (bf16[3,4160]{1,0:T(4,128)(2,1)S(1)}, bf16[3,4160]{1,0:T(4,128)(2,1)S(1)}, u32[]{:S(2)}, u32[]{:S(2)}) collective-permute-start(bf16[3,4160]{1,0:T(4,128)(2,1)S(1)} %pad_maximum_fusion.3), channel_id=1, source_target_pairs={{0,4},{4,8},{8,12},{12,16},{16,20},{20,24},{24,28},{1,5},{5,9},{9,... | collective-permute-start | bytes 74888 | tf_op jit(solution)/shard_map/ppermute | solution.py:18
  22.7 22.3 %copy-start.2 = (bf16[1024,128]{1,0:T(8,128)(2,1)}, bf16[1024,128]{1,0:T(8,128)(2,1)S(1)}, u32[]{:S(2)}) copy-start(bf16[1024,128]{1,0:T(8,128)(2,1)S(1)} %copy.114.b_ref) | copy-start | bytes 786436
  80.8 14.1 %collective-permute-start.1 = (f32[32,32,128]{2,1,0:T(8,128)S(1)}, f32[32,32,128]{2,1,0:T(8,128)S(1)}, u32[]{:S(2)}, u32[]{:S(2)}) collective-permute-start(f32[32,32,128]{2,1,0:T(8,128)S(1)} %get-tuple-element.31), channel_id=1, source_target_pairs={{0,16},{4,20},{8,24},{12,28},{1,17},{5,21},{9,25},{13,29},{2,18},{... | collective-permute-start | bytes 1572872 | tf_op jit(solution)/shard_map/ppermute | solution.py:43
  96.6 40.2 %all-to-all-start.1 = ((f32[4,32,32,128]{3,2,1,0:T(8,128)}), f32[4,32,32,128]{3,2,1,0:T(8,128)}, u32[]{:S(2)}, u32[]{:S(2)}) async-start(f32[4,32,32,128]{3,2,1,0:T(8,128)} %pad_maximum_fusion.1), calls=%async_computation.1 | async-start | bytes 4194304 | tf_op jit(solution)/shard_map/all_to_all | solution.py:48
  111.3 2.7 %copy-start.3 = (f32[4,2,16,256]{3,2,1,0:T(8,128)}, f32[4,2,16,256]{3,2,1,0:T(8,128)S(1)}, u32[]{:S(2)}) copy-start(f32[4,2,16,256]{3,2,1,0:T(8,128)S(1)} %reduce_window_sum.22.cumr_ref) | copy-start | bytes 393220
  136.9 1.9 %copy-start = (bf16[1024,128]{1,0:T(8,128)(2,1)S(1)}, bf16[1024,128]{1,0:T(8,128)(2,1)}, u32[]{:S(2)}) copy-start(bf16[1024,128]{1,0:T(8,128)(2,1)} %copy.113.c_ref) | copy-start | bytes 786436
  138.8 28.5 %copy-start.1 = (f32[4096]{0:T(1024)S(1)}, f32[4096]{0:T(1024)}, u32[]{:S(2)}) copy-start(f32[4096]{0:T(1024)} %param.22) | copy-start | bytes 49156

commit v13 on v10

--- a/solution.py
+++ b/solution.py
@@ -139,13 +139,9 @@
             factor = jnp.where(take, factor * decay, factor)
         state = local_state + factor * group_ref[j]
         high = state.astype(jnp.bfloat16)
-        rest = state - high.astype(jnp.float32)
-        mid = rest.astype(jnp.bfloat16)
-        low = (rest - mid.astype(jnp.float32)).astype(jnp.bfloat16)
-        inter = (
-            jnp.dot(c, high, preferred_element_type=jnp.float32)
-            + jnp.dot(c, mid, preferred_element_type=jnp.float32)
-            + jnp.dot(c, low, preferred_element_type=jnp.float32)
+        low = (state - high.astype(jnp.float32)).astype(jnp.bfloat16)
+        inter = jnp.dot(c, high, preferred_element_type=jnp.float32) + jnp.dot(
+            c, low, preferred_element_type=jnp.float32
         )
         columns = slice(j * width, (j + 1) * width)
         y = part_ref[:, columns] + inter * ecum_ref[0, 0, :, j : j + 1]

time: 177 us -> 177 us (level)
  no operation moved by 1% of the time
where the time goes in v13:
time: 177 us; the launch traced here: 176 us
  Pallas kernels  59 us (33%)
  blocking collectives  43.3 us (24%)
  starting transfers between devices  22.3 us (13%)
  other arithmetic  18.9 us (11%)
  local copies, waits for them, and re-layouts  16.6 us (9%)
  waiting for transfers between devices  14.8 us (8%)
    all_to_all x1, blocking collectives, scan_states(): lax.all_to_all(payload, axis, 0, 0, tiled=True, axis_index_groups=groups)  30.4 us
    pallas_call x1, Pallas kernels, gate_terms(): pl.pallas_call(gate_kernel, grid=(groups, spans), in_specs=[pl.BlockSpec(...  22.3 us
    pallas_call x1, Pallas kernels, block_states(): pl.pallas_call(state_kernel, grid=(spans, heads // group), in_specs=[pl.B...  20.6 us
    pallas_call x1, Pallas kernels, intra_terms(): pl.pallas_call(intra_kernel, grid=(spans, heads // group), in_specs=[pl.B...  16.1 us
    all_to_all x1, starting transfers between devices, scan_states(): lax.all_to_all(jnp.stack(entries, axis=0), axis, 0, 0, tiled=True, axis_i...  13.7 us
    ppermute x1, waiting for transfers between devices, scan_states(): earlier = lax.ppermute(running, axis, route)  10.5 us
    convert_element_type x1, other arithmetic, local(): return normed.astype(jnp.bfloat16)  9.98 us
    all_gather x1, blocking collectives, local(): bc_full = lax.all_gather(bc_local, 'ch', axis=1, tiled=True)  7.2 us
  transfers between devices with their start and end apart: 3, of which 2 were waited for; matrix products, arithmetic and copies ran while one was open for 7% of the time, Pallas kernels for 9%

profile of v13, /device:TPU:0, one launch (start us, length us, event | category | flops | bytes accessed | tf_op | source)
XLA Modules:
  0.0 175.8 jit_solution(14660330352196630087)
XLA Ops:
  1.6 0.9 constant_dynamic-slice_fusion.1
  2.5 5.0 %collective-permute-start = (bf16[3,4160]{1,0:T(4,128)(2,1)S(1)}, bf16[3,4160]{1,0:T(4,128)(2,1)S(1)}, u32[]{:S(2)}, u32[]{:S(2)}) collective-permute-start(bf16[3,4160]{1,0:T(4,128)(2,1)S(1)} %pad_maximum_fusion.3), channel_id=1, source_target_pairs={{0,4},{4,8},{8,12},{12,16},{16,20},{20,24},{24,28},{1,5},{5,9},{9,... | collective-permute-start | bytes 74888 | tf_op jit(solution)/shard_map/ppermute | solution.py:18
  8.2 1.1 fusion.13
  9.5 2.3 %reduce-window.6 = f32[4,32,2,128]{3,1,2,0:T(8,128)S(1)} reduce-window(f32[4,32,2,128]{3,1,2,0:T(8,128)S(1)} %copy.87, f32[]{:T(128)} %constant.47.clone.1), window={size=1x1x1x128 pad=0_0x0_0x0_0x127_0}, to_apply=%region_0.1 | reduce-window | flops 4161536 | bytes 262148 | tf_op jit(solution)/shard_map/reduce-window
  12.6 1.0 slice.167
  13.6 1.3 copy.97
  15.3 7.2 %all_gather.3 = bf16[1024,256]{0,1:T(8,128)(2,1)S(1)} all-gather(bf16[1024,64]{0,1:T(8,128)(2,1)S(1)} %multiply_convert_fusion.1), channel_id=1, replica_groups=mesh['seq'=8,'ch'=4] {'ch'}, dimensions={1}, use_global_device_ids=true | all-gather | bytes 655360 | tf_op jit(solution)/shard_map/all_gather | solution.py:303
  23.4 0.9 copy.95
  24.3 0.8 fusion.10.halo_ref
  25.2 20.6 %shard_map.109 = (f32[4,32,128,128]{3,2,1,0:T(8,128)}, bf16[1024,4096]{1,0:T(8,128)(2,1)}) custom-call(bf16[1024,4096]{1,0:T(8,128)(2,1)} %x_ref.1, bf16[4,8,4096]{2,1,0:T(8,128)(2,1)} %fusion.10.halo_ref, bf16[4,4096]{1,0:T(4,128)(2,1)} %taps_ref.1, bf16[4,128,256]{2,1,0:T(8,128)(2,1)} %bitcast.130, f32[4,2,256,16]{3,2,1,0:T(8,128)} %bitcast.124), custom_call_target="tpu_custom_call" | custom-call | flops 1073741824 | bytes 25165824 | tf_op jit(solution)/shard_map/pallas_call | solution.py:169
  45.7 4.1 %fusion.21 = (f32[1,32,128,128]{3,2,1,0:T(8,128)S(1)}, f32[1,32,128,128]{3,2,1,0:T(8,128)S(1)}, f32[1,32,128,128]{3,2,1,0:T(8,128)S(1)}, f32[1,32,128,128]{3,2,1,0:T(8,128)S(1)}) fusion(f32[4,32,128,128]{3,2,1,0:T(8,128)} %get-tuple-element.23.block_ref), kind=kLoop, calls=%fused_computation.68 | loop fusion | bytes 16777216 | tf_op jit(solution)/shard_map/slice | solution.py:334
  50.8 30.4 %all_to_all.10 = f32[4,33,32,128]{3,2,1,0:T(8,128)S(1)} all-to-all(f32[4,33,32,128]{3,2,1,0:T(8,128)S(1)} %pad_maximum_fusion), channel_id=1, replica_groups={{0,4,8,12},{16,20,24,28},{1,5,9,13},{17,21,25,29},{2,6,10,14},{18,22,26..., dimensions={0} | all-to-all | bytes 4325376 | tf_op jit(solution)/shard_map/all_to_all | solution.py:33
  81.5 3.6 %collective-permute-start.1 = (f32[32,32,128]{2,1,0:T(8,128)S(1)}, f32[32,32,128]{2,1,0:T(8,128)S(1)}, u32[]{:S(2)}, u32[]{:S(2)}) collective-permute-start(f32[32,32,128]{2,1,0:T(8,128)S(1)} %get-tuple-element.31), channel_id=1, source_target_pairs={{0,16},{4,20},{8,24},{12,28},{1,17},{5,21},{9,25},{13,29},{2,18},{... | collective-permute-start | bytes 1572872 | tf_op jit(solution)/shard_map/ppermute | solution.py:43
  85.1 10.5 %collective-permute-done.1 = f32[32,32,128]{2,1,0:T(8,128)S(1)} collective-permute-done((f32[32,32,128]{2,1,0:T(8,128)S(1)}, f32[32,32,128]{2,1,0:T(8,128)S(1)}, u32[]{:S(2)}, u32[]{:S(2)}) %collective-permute-start.1) | collective-permute-done | bytes 524320 | tf_op jit(solution)/shard_map/ppermute | solution.py:43
  95.8 1.5 pad_maximum_fusion.1
  97.4 13.7 %all-to-all-start.1 = ((f32[4,32,32,128]{3,2,1,0:T(8,128)}), f32[4,32,32,128]{3,2,1,0:T(8,128)S(1)}, u32[]{:S(2)}, u32[]{:S(2)}) async-start(f32[4,32,32,128]{3,2,1,0:T(8,128)} %pad_maximum_fusion.1), calls=%async_computation.1 | async-start | bytes 4194304 | tf_op jit(solution)/shard_map/all_to_all | solution.py:48
  112.7 1.3 copy.103
  114.1 1.2 copy.105
  115.4 0.8 copy.109.c_ref
  116.2 16.1 %shard_map.110.part_ref = f32[1024,4096]{1,0:T(8,128)} custom-call(f32[32]{0:T(128)} %skip_ref.1, bf16[1024,128]{1,0:T(8,128)(2,1)} %copy.109.c_ref, bf16[1024,128]{1,0:T(8,128)(2,1)} %copy-done.1, bf16[1024,4096]{1,0:T(8,128)(2,1)} %get-tuple-element.24.x_ref, f32[4,2,256,16]{3,2,1,0:T(8,128)} %bitcast.125, f32[4,2,16,256]{3,2,1,0:T(8,128)} %copy-done.2, ...), custom_call_target="tpu_custom_call" | custom-call | flops 2214592512 | bytes 25165824 | tf_op jit(solution)/shard_map/pallas_call | solution.py:199
  132.3 4.3 %all-to-all-done.1 = f32[4,32,32,128]{3,2,1,0:T(8,128)S(1)} async-done(((f32[4,32,32,128]{3,2,1,0:T(8,128)}), f32[4,32,32,128]{3,2,1,0:T(8,128)S(1)}, u32[]{:S(2)}, u32[]{:S(2)}) %all-to-all-start.1) | async-done | bytes 2097184 | tf_op jit(solution)/shard_map/all_to_all | solution.py:48
  137.6 22.3 %shard_map.111 = (f32[1024,4096]{1,0:T(8,128)}, f32[2,1024,1]{2,1,0:T(8,128)S(1)}) custom-call(f32[128]{0:T(128)S(1)} %exp.26.decay_ref, f32[1024,4096]{1,0:T(8,128)} %shard_map.110.part_ref, bf16[1024,128]{1,0:T(8,128)(2,1)S(1)} %copy-done, f32[4,32,128,128]{3,2,1,0:T(8,128)} %get-tuple-element.23.block_ref, f32[32,128,128]{2,1,0:T(8,128)S(1)} %bitcast.116, ...), custom_call_target="tpu_custom_call" | custom-call | flops 3221225472 | bytes 41943040 | tf_op jit(solution)/shard_map/pallas_call | solution.py:236
  160.1 5.7 %psum.7 = f32[1024]{0:T(1024)S(1)} all-reduce(f32[1024]{0:T(1024)S(1)} %reduce_sum.9), channel_id=1, replica_groups=mesh['seq'=8,'ch'=4] {'ch'}, use_global_device_ids=true, to_apply=%region_3.4 | all-reduce | flops 1024 | bytes 8192 | tf_op jit(solution)/shard_map/psum | solution.py:365
  165.8 10.0 %multiply_convert_fusion = bf16[1024,4096]{1,0:T(8,128)(2,1)} fusion(f32[1024,4096]{1,0:T(8,128)} %get-tuple-element.25, f32[1024]{0:T(1024)S(1)} %fusion.16, f32[4096]{0:T(1024)S(1)} %copy-done.5, f32[1024]{0:T(1024)S(1)} %add_rsqrt_fusion), kind=kLoop, calls=%fused_computation | loop fusion | flops 16777216 | bytes 25190400 | tf_op jit(solution)/shard_map/convert_element_type | solution.py:368
  (58 shorter events, 8.3 us)
Async XLA Ops:
  0.0 12.6 %copy-start.6 = (bf16[4,64]{1,0:T(4,128)(2,1)S(1)}, bf16[4,64]{1,0:T(4,128)(2,1)}, u32[]{:S(2)}) copy-start(bf16[4,64]{1,0:T(4,128)(2,1)} %param.21) | copy-start | bytes 1540
  2.5 12.6 %copy-start.4 = (bf16[1024,64]{0,1:T(8,128)(2,1)S(1)}, bf16[1024,64]{0,1:T(8,128)(2,1)}, u32[]{:S(2)}) copy-start(bf16[1024,64]{0,1:T(8,128)(2,1)} %param.15) | copy-start | bytes 393220
  2.5 12.4 %collective-permute-start = (bf16[3,4160]{1,0:T(4,128)(2,1)S(1)}, bf16[3,4160]{1,0:T(4,128)(2,1)S(1)}, u32[]{:S(2)}, u32[]{:S(2)}) collective-permute-start(bf16[3,4160]{1,0:T(4,128)(2,1)S(1)} %pad_maximum_fusion.3), channel_id=1, source_target_pairs={{0,4},{4,8},{8,12},{12,16},{16,20},{20,24},{24,28},{1,5},{5,9},{9,... | collective-permute-start | bytes 74888 | tf_op jit(solution)/shard_map/ppermute | solution.py:18
  23.4 22.3 %copy-start.1 = (bf16[1024,128]{1,0:T(8,128)(2,1)}, bf16[1024,128]{1,0:T(8,128)(2,1)S(1)}, u32[]{:S(2)}) copy-start(bf16[1024,128]{1,0:T(8,128)(2,1)S(1)} %copy.110.b_ref) | copy-start | bytes 786436
  81.5 14.1 %collective-permute-start.1 = (f32[32,32,128]{2,1,0:T(8,128)S(1)}, f32[32,32,128]{2,1,0:T(8,128)S(1)}, u32[]{:S(2)}, u32[]{:S(2)}) collective-permute-start(f32[32,32,128]{2,1,0:T(8,128)S(1)} %get-tuple-element.31), channel_id=1, source_target_pairs={{0,16},{4,20},{8,24},{12,28},{1,17},{5,21},{9,25},{13,29},{2,18},{... | collective-permute-start | bytes 1572872 | tf_op jit(solution)/shard_map/ppermute | solution.py:43
  97.4 39.3 %all-to-all-start.1 = ((f32[4,32,32,128]{3,2,1,0:T(8,128)}), f32[4,32,32,128]{3,2,1,0:T(8,128)S(1)}, u32[]{:S(2)}, u32[]{:S(2)}) async-start(f32[4,32,32,128]{3,2,1,0:T(8,128)} %pad_maximum_fusion.1), calls=%async_computation.1 | async-start | bytes 4194304 | tf_op jit(solution)/shard_map/all_to_all | solution.py:48
  111.0 4.4 %copy-start.3 = (bf16[1024,128]{0,1:T(8,128)(2,1)S(1)}, bf16[1024,128]{0,1:T(8,128)(2,1)}, u32[]{:S(2)}) copy-start(bf16[1024,128]{0,1:T(8,128)(2,1)} %get-tuple-element.46) | copy-start | bytes 786436
  112.0 4.2 %copy-start.2 = (f32[4,2,16,256]{3,2,1,0:T(8,128)}, f32[4,2,16,256]{3,2,1,0:T(8,128)S(1)}, u32[]{:S(2)}) copy-start(f32[4,2,16,256]{3,2,1,0:T(8,128)S(1)} %reduce_window_sum.22.cumr_ref) | copy-start | bytes 393220
  136.7 1.0 copy-start
  137.6 28.2 %copy-start.5 = (f32[4096]{0:T(1024)S(1)}, f32[4096]{0:T(1024)}, u32[]{:S(2)}) copy-start(f32[4096]{0:T(1024)} %param.22) | copy-start | bytes 49156
